TPU v7x, 32 devices: a whole 2x2x4 slice. The times are simulated.
32 devices in a mesh: slab: 4 (over y, core), rot: 8 (over z, x).
Axes of the slice: x: 2, y: 2, z: 4, core: 2. Of those that a mesh axis runs over, the one named last changes fastest.
Arguments:
- receptor: float32 [2, 128, 128, 128], P(None, 'slab'), may hold values from -6 to 6
- ligand_box: float32 [2, 8, 2, 32, 32, 32], P(None, 'rot', None, 'slab'), may hold values from -0.0234375 to 0.0234375
- channel_weight: float32 [2], replicated, may hold values from 0.3 to 3
- rotation_table: float32 [9, 16], replicated, may hold values from -1 to 1, as said below
- ligand_atoms: float32 [3, 128], replicated, may hold values from -0.12 to 0.12
- cluster_center: float32 [64, 3, 128], P('rot'), may hold values from -1.5 to 1.5
- pose_rotation: int32 [8192], P(('slab', 'rot')), may hold values from 0 to 15
- pose_translation: int32 [8192], P(('slab', 'rot')), may hold values from 0 to 2097151
- pose_owner: int32 [8192, 1], P(('slab', 'rot')), may hold values from 0 to 7; in each aligned block of 256 rows (0 to 255, 256 to 511, ...) at most 64 rows name the same one
- pose_member: int32 [8192], P(('slab', 'rot')), may hold values from 0 to 7
Outputs:
- scores: float32 [2, 8, 128, 128, 128], P(None, 'rot', 'slab')
- pose_stats: float32 [10, 8192], P(None, ('slab', 'rot'))
Inputs may be any that keep to these rules, and one draw needn't show every extreme that they name: `pose_owner`: the rows of one device name one owner at most 64 times, and some device's rows name some owner exactly 64 times. `rotation_table`: each column is a proper rotation matrix up to float32 rounding, row-major.
All inputs are finite; a program needn't handle non-finite values.
Results may differ from a plain program's by a relative error of at most 0.0003.
Values sent between devices are 32-bit elements; how exact they have to be, the bound alone decides.
No kernel may reach another device: no remote copies, remote signals or barrier semaphores. Data moves between devices by JAX's collectives and lax.ppermute only.
A program may use at most 128 MiB of HBM per device.

v0:
```python
import functools

import jax
import jax.numpy as jnp
from jax import lax
from jax.experimental import pallas as pl
from jax.experimental.pallas import tpu as pltpu
from jax.sharding import PartitionSpec as P

PRECISE = lax.Precision.HIGHEST
SPLIT3 = lax.Precision.HIGH
TWO_PI = 6.283185307179586
F32 = jnp.float32
BF16 = jnp.bfloat16


def phase_tables(rows, cols, length):
    row_index = lax.broadcasted_iota(jnp.int32, (rows, cols), 0)
    col_index = lax.broadcasted_iota(jnp.int32, (rows, cols), 1)
    phase = (row_index * col_index % length).astype(F32) * (TWO_PI / length)
    return (jnp.cos(phase), jnp.sin(phase))


def block2(top_left, top_right, bottom_left, bottom_right):
    top = jnp.concatenate([top_left, top_right], axis=1)
    bottom = jnp.concatenate([bottom_left, bottom_right], axis=1)
    return jnp.concatenate([top, bottom], axis=0)


def hi_lo(table):
    high = table.astype(BF16)
    low = (table - high.astype(F32)).astype(BF16)
    return high, low


def split_dot(a, b_high, b_low, a_left):
    a_high = a.astype(BF16)
    a_low = (a - a_high.astype(F32)).astype(BF16)
    dot = functools.partial(jnp.dot, preferred_element_type=F32)
    if a_left:
        return dot(a_high, b_high) + (dot(a_low, b_high) + dot(a_high, b_low))
    return dot(b_high, a_high) + (dot(b_high, a_low) + dot(b_low, a_high))


def forward_plane_kernel(in_ref, rz_ref, ly_ref, out_ref):
    planes = in_ref.shape[1]
    size = in_ref.shape[3]
    rz_hi, rz_lo = hi_lo(rz_ref[...])
    ly_hi, ly_lo = hi_lo(ly_ref[...])

    def body(p, carry):
        joined = jnp.concatenate([in_ref[0, p], in_ref[1, p]], axis=1)
        along_z = split_dot(joined, rz_hi, rz_lo, True)
        stacked = jnp.concatenate([along_z[:, :size], along_z[:, size:]], axis=0)
        along_y = split_dot(stacked, ly_hi, ly_lo, False)
        out_ref[0, p] = along_y[:size]
        out_ref[1, p] = along_y[size:]
        return carry

    lax.fori_loop(0, planes, body, 0)


def inverse_plane_kernel(in_ref, ly_ref, rz_ref, out_ref):
    planes = in_ref.shape[2]
    size = in_ref.shape[4]
    ly_hi, ly_lo = hi_lo(ly_ref[...])
    rz_hi, rz_lo = hi_lo(rz_ref[...])

    def body(p, carry):
        stacked = jnp.concatenate([in_ref[0, 0, p], in_ref[0, 1, p]], axis=0)
        along_y = split_dot(stacked, ly_hi, ly_lo, False)
        joined = jnp.concatenate([along_y[:size], along_y[size:]], axis=1)
        out_ref[0, p] = split_dot(joined, rz_hi, rz_lo, True)
        return carry

    lax.fori_loop(0, planes, body, 0)


def forward_planes(block, tables, plane_step):
    planes, size = block.shape[1], block.shape[3]
    table_spec = pl.BlockSpec((2 * size, 2 * size), lambda i: (0, 0))
    data_spec = pl.BlockSpec((2, plane_step, size, size), lambda i: (0, i, 0, 0))
    return pl.pallas_call(
        forward_plane_kernel,
        grid=(planes // plane_step,),
        in_specs=[data_spec, table_spec, table_spec],
        out_specs=data_spec,
        out_shape=jax.ShapeDtypeStruct(block.shape, F32),
    )(block, *tables)


def inverse_planes(spectra, tables, plane_step):
    sets, planes, size = spectra.shape[0], spectra.shape[2], spectra.shape[4]
    ly_spec = pl.BlockSpec((2 * size, 2 * size), lambda s, i: (0, 0))
    rz_spec = pl.BlockSpec((2 * size, size), lambda s, i: (0, 0))
    return pl.pallas_call(
        inverse_plane_kernel,
        grid=(sets, planes // plane_step),
        in_specs=[
            pl.BlockSpec((1, 2, plane_step, size, size), lambda s, i: (s, 0, i, 0, 0)),
            ly_spec,
            rz_spec,
        ],
        out_specs=pl.BlockSpec((1, plane_step, size, size), lambda s, i: (s, i, 0, 0)),
        out_shape=jax.ShapeDtypeStruct((sets, planes, size, size), F32),
    )(spectra, *tables)


def gather_by_sum(piece, axis_name, dim):
    count = lax.axis_size(axis_name)
    index = lax.axis_index(axis_name)
    width = piece.shape[dim]
    shape = list(piece.shape)
    shape[dim] = width * count
    start = [0] * len(shape)
    start[dim] = index * width
    placed = lax.dynamic_update_slice(jnp.zeros(shape, piece.dtype), piece, start)
    return lax.psum(placed, axis_name)


def score_grids(receptor, ligand_box, channel_weight):
    size = receptor.shape[2]
    slab_count = lax.axis_size("slab")
    part = receptor.shape[1]
    box = ligand_box.shape[4]
    sets = ligand_box.shape[0]
    extra = -(-(box - 1) // part)
    window = part * (1 + extra)
    plane_step = 8

    full_box = gather_by_sum(ligand_box, "slab", 3)
    blocks = [receptor]
    for hop in range(1, extra + 1):
        pairs = [(i, (i - hop) % slab_count) for i in range(slab_count)]
        blocks.append(lax.ppermute(receptor, "slab", perm=pairs))

    cos_n, sin_n = phase_tables(size, size, size)
    rz = block2(cos_n, -sin_n, sin_n, cos_n)
    ly = block2(cos_n, sin_n, -sin_n, cos_n)
    forward_tables = (rz, ly)

    cos_w, sin_w = phase_tables(window, window, window)
    rec_real = None
    rec_imag = None
    for index, planes in enumerate(blocks):
        along_yz = forward_planes(planes, forward_tables, plane_step)
        cols = slice(index * part, (index + 1) * part)
        stacked = along_yz.reshape(2 * part, size, size)
        g_real = jnp.concatenate([cos_w[:, cols], sin_w[:, cols]], axis=1)
        g_imag = jnp.concatenate([-sin_w[:, cols], cos_w[:, cols]], axis=1)
        term_real = jnp.einsum("uc,cjk->ujk", g_real, stacked, precision=SPLIT3)
        term_imag = jnp.einsum("uc,cjk->ujk", g_imag, stacked, precision=SPLIT3)
        rec_real = term_real if rec_real is None else rec_real + term_real
        rec_imag = term_imag if rec_imag is None else rec_imag + term_imag

    lig_real = full_box[:, 0, 0] * channel_weight[0]
    lig_imag = full_box[:, 0, 1] * channel_weight[1]
    cos_b, sin_b = phase_tables(box, size, size)
    z_real = jnp.einsum("sxyz,zk->sxyk", lig_real, cos_b, precision=SPLIT3) + jnp.einsum(
        "sxyz,zk->sxyk", lig_imag, sin_b, precision=SPLIT3
    )
    z_imag = jnp.einsum("sxyz,zk->sxyk", lig_imag, cos_b, precision=SPLIT3) - jnp.einsum(
        "sxyz,zk->sxyk", lig_real, sin_b, precision=SPLIT3
    )
    cos_yb = cos_b.T
    sin_yb = sin_b.T
    wy = block2(cos_yb, sin_yb, -sin_yb, cos_yb)
    along_y = jnp.einsum(
        "jc,sxck->sxjk", wy, jnp.concatenate([z_real, z_imag], axis=2), precision=SPLIT3
    )
    along_y = along_y.reshape(sets, box, 2, size, size)
    cos_xb, sin_xb = phase_tables(window, box, window)
    lx_real = jnp.stack([cos_xb, sin_xb], axis=2)
    lx_imag = jnp.stack([-sin_xb, cos_xb], axis=2)
    lig_spec_real = jnp.einsum("uxc,sxcjk->sujk", lx_real, along_y, precision=SPLIT3)
    lig_spec_imag = jnp.einsum("uxc,sxcjk->sujk", lx_imag, along_y, precision=SPLIT3)

    prod_real = rec_real[None] * lig_spec_real + rec_imag[None] * lig_spec_imag
    prod_imag = rec_imag[None] * lig_spec_real - rec_real[None] * lig_spec_imag

    cos_t, sin_t = phase_tables(part, window, window)
    scale = 1.0 / float(window * size * size)
    h_from_real = jnp.concatenate([cos_t, sin_t], axis=0) * scale
    h_from_imag = jnp.concatenate([-sin_t, cos_t], axis=0) * scale
    back_x = jnp.einsum("tu,sujk->stjk", h_from_real, prod_real, precision=SPLIT3) + jnp.einsum(
        "tu,sujk->stjk", h_from_imag, prod_imag, precision=SPLIT3
    )
    back_x = back_x.reshape(sets, 2, part, size, size)

    lyi = block2(cos_n, -sin_n, sin_n, cos_n)
    rzi = jnp.concatenate([cos_n, -sin_n], axis=0)
    inverse_tables = (lyi, rzi)
    grids = inverse_planes(back_x, inverse_tables, plane_step)
    return grids.reshape(sets, 1, part, size, size)


def pose_statistics(
    rotation_table,
    ligand_atoms,
    cluster_center,
    pose_rotation,
    pose_translation,
    pose_owner,
    pose_member,
    size,
):
    all_centers = gather_by_sum(cluster_center, "rot", 0)
    local_count = cluster_center.shape[0]
    cluster = pose_owner[:, 0] * local_count + pose_member
    rotation = jnp.take(rotation_table, pose_rotation, axis=1, mode="clip").T.reshape(-1, 3, 3)
    coords = jnp.stack(
        [
            pose_translation // (size * size),
            pose_translation // size % size,
            pose_translation % size,
        ],
        axis=1,
    )
    shifts = ((coords + size // 2) % size - size // 2).astype(F32) / size
    center = jnp.take(all_centers, cluster, axis=0, mode="clip")
    moved = jnp.einsum("pjk,ka->pja", rotation, ligand_atoms, precision=PRECISE) + shifts[:, :, None]
    spread = moved - center
    mean_square = jnp.mean(jnp.sum(spread * spread, axis=1), axis=1)
    moved_centred = moved - jnp.mean(moved, axis=2, keepdims=True)
    center_centred = center - jnp.mean(center, axis=2, keepdims=True)
    covariance = jnp.einsum("pja,pka->pjk", moved_centred, center_centred, precision=PRECISE)
    stats = jnp.concatenate([covariance.reshape(-1, 9), mean_square[:, None]], axis=1)
    return stats.T


def local(
    receptor,
    ligand_box,
    channel_weight,
    rotation_table,
    ligand_atoms,
    cluster_center,
    pose_rotation,
    pose_translation,
    pose_owner,
    pose_member,
):
    size = receptor.shape[2]
    scores = score_grids(receptor, ligand_box, channel_weight)
    pose_stats = pose_statistics(
        rotation_table,
        ligand_atoms,
        cluster_center,
        pose_rotation,
        pose_translation,
        pose_owner,
        pose_member,
        size,
    )
    return (scores, pose_stats)


def solution(mesh):
    return jax.shard_map(
        local,
        mesh=mesh,
        in_specs=(
            P(None, "slab", None, None),
            P(None, "rot", None, "slab", None, None),
            P(),
            P(),
            P(),
            P("rot", None, None),
            P(("slab", "rot")),
            P(("slab", "rot")),
            P(("slab", "rot"), None),
            P(("slab", "rot")),
        ),
        out_specs=(P(None, "rot", "slab", None, None), P(None, ("slab", "rot"))),
        check_vma=False,
    )
```

profile of v0, /device:TPU:0, one launch (start us, length us, event | category | flops | bytes accessed | tf_op | source)
XLA Modules:
  0.0 305.8 jit_solution(16172841009689607872)
XLA Ops:
  8.8 2.5 collective-permute-start
  12.6 1.3 copy-done.8
  18.5 20.7 %shard_map.113 = f32[2,32,128,128]{3,2,1,0:T(8,128)} custom-call(f32[2,32,128,128]{3,2,1,0:T(8,128)} %in_ref.1, f32[256,256]{1,0:T(8,128)} %get-tuple-element.15.rz_ref.ly_ref, f32[256,256]{1,0:T(8,128)} %get-tuple-element.14.ly_ref), custom_call_target="tpu_custom_call" | custom-call | tf_op jit(solution)/shard_map/pallas_call | solution.py:83
  39.3 8.5 %fusion.14 = f32[64,128,128]{2,0,1:T(8,128)} fusion(f32[64,128,128]{2,1,0:T(8,128)} %bitcast.125, f32[64,32]{1,0:T(8,128)S(1)} %get-tuple-element.34, f32[64,32]{1,0:T(8,128)S(1)} %get-tuple-element.17), kind=kOutput, calls=%fused_computation.19 | convolution fusion | flops 402657280 | bytes 8404992 | tf_op jit(solution)/shard_map/uc,cjk->ujk/dot_general | solution.py:152
  47.8 6.2 %fusion.16 = f32[64,128,128]{2,0,1:T(8,128)} fusion(f32[64,128,128]{2,1,0:T(8,128)S(1)} %bitcast.126, f32[64,32]{1,0:T(8,128)S(1)} %get-tuple-element.19, f32[64,32]{1,0:T(8,128)S(1)} %get-tuple-element.34), kind=kOutput, calls=%fused_computation.21 | convolution fusion | flops 402657280 | bytes 8404992 | tf_op jit(solution)/shard_map/uc,cjk->ujk/dot_general | solution.py:151
  54.0 29.9 %all-reduce.5.cloned.1.call-done = f32[64,3,128]{2,1,0:T(4,128)} async-done(((f32[64,3,128]{2,1,0:T(4,128)}), f32[64,3,128]{2,1,0:T(4,128)}) %all-reduce.5.cloned.1.call-update) | async-done | bytes 98320 | tf_op jit(solution)/shard_map/psum | solution.py:118
  83.9 1.9 gather_fusion.1
  87.3 1.9 fusion.37
  90.0 47.1 %all-reduce.3.cloned.1.call-done = f32[2,1,2,32,32,32]{5,4,3,0,2,1:T(8,128)} async-done(((f32[2,1,2,32,32,32]{5,4,3,0,2,1:T(8,128)}), f32[2,1,2,32,32,32]{5,4,3,0,2,1:T(8,128)}) %all-reduce.3.cloned.1.call-update) | async-done | bytes 524304 | tf_op jit(solution)/shard_map/psum | solution.py:118
  137.1 2.8 fusion.34
  139.9 2.5 fusion.32
  142.5 1.3 convolution_subtract_fusion
  145.0 5.6 %convolution_bitcast_fusion = f32[2,32,256,128]{2,3,1,0:T(8,128)} fusion(f32[2,32,32,128]{3,2,1,0:T(8,128)S(1)} %convolution_subtract_fusion, f32[2,32,32,128]{3,2,1,0:T(8,128)S(1)} %convolution_add_fusion, f32[128,32]{0,1:T(8,128)S(1)} %get-tuple-element.29, f32[128,32]{0,1:T(8,128)S(1)} %fusion.133, f32[128,32]{0,1:T(8,128)S(1)} %get-tuple-element.28), kind=kOutput, calls=%fused_computation.23 | convolution fusion | flops 805879808 | bytes 10534912 | tf_op jit(solution)/shard_map/jc,sxck->sxjk/dot_general | solution.py:168
  150.7 10.8 %reshape.154 = f32[2,32,2,128,128]{3,2,4,1,0:T(2,128)} reshape(f32[2,32,256,128]{2,3,1,0:T(8,128)} %convolution_bitcast_fusion) | data formatting | bytes 16777216 | tf_op jit(solution)/shard_map/reshape | solution.py:171
  161.5 10.4 %copy.80 = f32[2,32,2,128,128]{4,1,2,3,0:T(8,128)} copy(f32[2,32,2,128,128]{3,2,4,1,0:T(2,128)} %reshape.154) | data formatting | bytes 16777216 | tf_op jit(solution)/shard_map/reshape | solution.py:171
  171.9 10.3 %fusion.72 = f32[2,128,128,64,1]{2,3,4,1,0:T(8,128)} fusion(f32[2,32,2,128,128]{4,1,2,3,0:T(8,128)} %copy.80, f32[64,32,1]{0,1,2:T(8,128)S(1)} %get-tuple-element.30, f32[64,32,1]{0,1,2:T(8,128)S(1)} %get-tuple-element.31), kind=kOutput, calls=%fused_computation.95 | convolution fusion | flops 805310464 | bytes 16793600 | tf_op jit(solution)/shard_map/uxc,sxcjk->sujk/dot_general | solution.py:176
  182.2 5.7 %fusion.65 = f32[2,128,128,64,1]{2,3,4,1,0:T(8,128)} fusion(f32[2,32,2,128,128]{4,1,2,3,0:T(8,128)S(1)} %copy-done.3, f32[64,32,1]{0,1,2:T(8,128)S(1)} %fusion.123, f32[64,32,1]{0,1,2:T(8,128)S(1)} %get-tuple-element.30), kind=kOutput, calls=%fused_computation.85 | convolution fusion | flops 805310464 | bytes 16793600 | tf_op jit(solution)/shard_map/uxc,sxcjk->sujk/dot_general | solution.py:175
  187.9 20.4 %shard_map.114 = f32[2,32,128,128]{3,2,1,0:T(8,128)} custom-call(f32[2,32,128,128]{3,2,1,0:T(8,128)} %collective-permute-done.in_ref, f32[256,256]{1,0:T(8,128)} %get-tuple-element.15.rz_ref.ly_ref, f32[256,256]{1,0:T(8,128)} %get-tuple-element.14.ly_ref), custom_call_target="tpu_custom_call" | custom-call | tf_op jit(solution)/shard_map/pallas_call | solution.py:83
  208.3 8.0 %fusion.23 = f32[64,128,128]{2,0,1:T(8,128)S(1)} fusion(f32[64,128,128]{2,0,1:T(8,128)} %fusion.14, f32[64,128,128]{2,1,0:T(8,128)} %bitcast.123, f32[64,32]{1,0:T(8,128)S(1)} %get-tuple-element.35, f32[64,32]{1,0:T(8,128)S(1)} %get-tuple-element.18), kind=kOutput, calls=%fused_computation.25 | convolution fusion | flops 403705856 | bytes 12599296 | tf_op jit(solution)/shard_map/uc,cjk->ujk/dot_general | solution.py:152
  216.3 6.4 %fusion.20 = f32[64,128,128]{2,0,1:T(8,128)} fusion(f32[64,128,128]{2,0,1:T(8,128)S(1)} %copy-done.6, f32[64,128,128]{2,1,0:T(8,128)S(1)} %bitcast.124, f32[64,32]{1,0:T(8,128)S(1)} %get-tuple-element.16, f32[64,32]{1,0:T(8,128)S(1)} %get-tuple-element.35), kind=kOutput, calls=%fused_computation.24 | convolution fusion | flops 403705856 | bytes 12599296 | tf_op jit(solution)/shard_map/uc,cjk->ujk/dot_general | solution.py:151
  222.8 14.7 %fusion.1 = f32[2,128,128,64]{2,3,1,0:T(8,128)} fusion(f32[2,128,128,64,1]{2,3,4,1,0:T(8,128)} %fusion.72, f32[2,128,128,64,1]{2,3,4,1,0:T(8,128)} %fusion.65, f32[64,128,128]{2,0,1:T(8,128)S(1)} %fusion.23, f32[64,128,128]{2,0,1:T(8,128)} %fusion.20, f32[32,64]{1,0:T(8,128)S(1)} %get-tuple-element.36, f32[32,64]{1,0:T(8,128)S(1)} %get-tuple-element.37), kind=kOutput, calls=%fused_computation.5 | convolution fusion | flops 811606016 | bytes 33570816 | tf_op jit(solution)/shard_map/tu,sujk->stjk/dot_general | solution.py:185
  237.5 18.1 %add_bitcast_fusion = f32[2,64,128,128]{3,1,2,0:T(8,128)} fusion(f32[2,128,128,64]{2,3,1,0:T(8,128)} %fusion.1, f32[2,128,128,64,1]{2,3,4,1,0:T(8,128)} %fusion.72, f32[2,128,128,64,1]{2,3,4,1,0:T(8,128)} %fusion.65, f32[64,128,128]{2,0,1:T(8,128)} %copy-done.2, f32[64,128,128]{2,0,1:T(8,128)} %fusion.20, f32[32,64]{1,0:T(8,128)S(1)} %get-tuple-element.37, ...), kind=kOutput, calls=%fused_computation.10 | convolution fusion | flops 813703168 | bytes 41959424 | tf_op jit(solution)/shard_map/tu,sujk->stjk/dot_general | solution.py:185
  255.6 11.5 %copy.84 = f32[2,64,128,128]{3,2,1,0:T(8,128)} copy(f32[2,64,128,128]{3,1,2,0:T(8,128)} %add_bitcast_fusion) | data formatting | bytes 16777216 | tf_op jit(solution)/shard_map/add | solution.py:185
  267.1 31.5 %shard_map.115 = f32[2,32,128,128]{3,2,1,0:T(8,128)} custom-call(f32[2,2,32,128,128]{4,3,2,1,0:T(8,128)} %bitcast.127, f32[256,256]{1,0:T(8,128)} %get-tuple-element.15.rz_ref.ly_ref, f32[256,128]{1,0:T(8,128)} %pad_maximum_fusion.4.rz_ref), custom_call_target="tpu_custom_call" | custom-call | tf_op jit(solution)/shard_map/pallas_call | solution.py:96
  (76 shorter events, 10.8 us)
Async XLA Ops:
  7.2 78.9 %copy-start = (f32[3,128]{1,0:T(4,128)S(1)}, f32[3,128]{1,0:T(4,128)}, u32[]{:S(2)}) copy-start(f32[3,128]{1,0:T(4,128)} %param.14) | copy-start | bytes 4612
  7.2 8.1 %copy-start.14 = (s32[256,1]{0,1:T(1,128)S(1)}, s32[256,1]{0,1:T(1,128)}, u32[]{:S(2)}) copy-start(s32[256,1]{0,1:T(1,128)} %param.18) | copy-start | bytes 3076
  7.2 8.1 %copy-start.11 = (f32[2]{0:T(128)S(1)}, f32[2]{0:T(128)}, u32[]{:S(2)}) copy-start(f32[2]{0:T(128)} %param.12) | copy-start | bytes 28
  7.2 8.7 %copy-start.12 = (s32[256]{0:T(256)S(1)}, s32[256]{0:T(256)}, u32[]{:S(2)}) copy-start(s32[256]{0:T(256)} %param.19) | copy-start | bytes 3076
  7.2 8.7 %copy-start.15 = (s32[256]{0:T(256)S(1)}, s32[256]{0:T(256)}, u32[]{:S(2)}) copy-start(s32[256]{0:T(256)} %param.17) | copy-start | bytes 3076
  7.2 8.7 %copy-start.13 = (s32[256]{0:T(256)S(1)}, s32[256]{0:T(256)}, u32[]{:S(2)}) copy-start(s32[256]{0:T(256)} %param.16) | copy-start | bytes 3076
  7.2 8.8 %copy-start.10 = (f32[9,16]{1,0:T(8,128)S(1)}, f32[9,16]{1,0:T(8,128)}, u32[]{:S(2)}) copy-start(f32[9,16]{1,0:T(8,128)} %param.13) | copy-start | bytes 1732
  7.2 76.7 %all-reduce.5.cloned.1.call-start = ((), (), s32[]{:S(2)}) async-start(), calls=%async_computation.1 | async-start | bytes 262144 | tf_op jit(solution)/shard_map/psum | solution.py:118
  8.0 0.7 copy-start.9
  8.7 128.4 %all-reduce.3.cloned.1.call-start = ((), (), s32[]{:S(2)}) async-start(), calls=%async_computation | async-start | bytes 4194304 | tf_op jit(solution)/shard_map/psum | solution.py:118
  8.8 179.1 %collective-permute-start = (f32[2,32,128,128]{3,2,1,0:T(8,128)}, f32[2,32,128,128]{3,2,1,0:T(8,128)}, u32[]{:S(2)}, u32[]{:S(2)}) collective-permute-start(f32[2,32,128,128]{3,2,1,0:T(8,128)} %in_ref.1), channel_id=1, source_target_pairs={{0,24},{8,0},{16,8},{24,16},{1,25},{9,1},{17,9},{25,17},{2,26},{10... | collective-permute-start | bytes 12582920 | tf_op jit(solution)/shard_map/ppermute | solution.py:135
  12.6 1.3 copy-start.8
  39.3 8.5 %copy-start.5 = (f32[2,32,128,128]{3,2,1,0:T(8,128)S(1)}, f32[2,32,128,128]{3,2,1,0:T(8,128)}, u32[]{:S(2)}) copy-start(f32[2,32,128,128]{3,2,1,0:T(8,128)} %shard_map.113) | copy-start | bytes 12582916
  137.1 5.3 %copy-start.7 = (f32[2,1,2,32,32,32]{5,4,3,0,2,1:T(8,128)S(1)}, f32[2,1,2,32,32,32]{5,4,3,0,2,1:T(8,128)}, u32[]{:S(2)}) copy-start(f32[2,1,2,32,32,32]{5,4,3,0,2,1:T(8,128)} %all-reduce.3.cloned.1.call-done) | copy-start | bytes 1572868
  171.9 10.3 %copy-start.3 = (f32[2,32,2,128,128]{4,1,2,3,0:T(8,128)S(1)}, f32[2,32,2,128,128]{4,1,2,3,0:T(8,128)}, u32[]{:S(2)}) copy-start(f32[2,32,2,128,128]{4,1,2,3,0:T(8,128)} %copy.80) | copy-start | bytes 25165828
  208.3 8.0 %copy-start.4 = (f32[2,32,128,128]{3,2,1,0:T(8,128)S(1)}, f32[2,32,128,128]{3,2,1,0:T(8,128)}, u32[]{:S(2)}) copy-start(f32[2,32,128,128]{3,2,1,0:T(8,128)} %shard_map.114) | copy-start | bytes 12582916
  208.3 8.0 %copy-start.6 = (f32[64,128,128]{2,0,1:T(8,128)S(1)}, f32[64,128,128]{2,0,1:T(8,128)}, u32[]{:S(2)}) copy-start(f32[64,128,128]{2,0,1:T(8,128)} %fusion.16) | copy-start | bytes 12582916
  216.3 6.5 %copy-start.2 = (f32[64,128,128]{2,0,1:T(8,128)}, f32[64,128,128]{2,0,1:T(8,128)S(1)}, u32[]{:S(2)}) copy-start(f32[64,128,128]{2,0,1:T(8,128)S(1)} %fusion.23) | copy-start | bytes 12582916
  267.0 31.5 %copy-start.1 = (f32[3,128]{1,0:T(4,128)S(1)}, f32[3,128]{1,0:T(4,128)}, u32[]{:S(2)}) copy-start(f32[3,128]{1,0:T(4,128)} %param.14) | copy-start | bytes 4612
Sparse Core Ops, SparseCore 0:
  11.4 72.4 all-reduce.4
  86.4 50.6 all-reduce.2
where the time goes:
time: 309 us; the launch traced here: 306 us
  matrix products  93.9 us (30%)
  waiting for transfers between devices  77.1 us (25%)
  Pallas kernels  72.7 us (24%)
  local copies, waits for them, and re-layouts  40.8 us (13%)
  between operations  14.9 us (5%)
  other arithmetic  4 us (1%)
    psum x2, waiting for transfers between devices, gather_by_sum(): return lax.psum(placed, axis_name)  77.1 us
    pallas_call x2, Pallas kernels, forward_planes(): pl.pallas_call(forward_plane_kernel, grid=(planes // plane_step,), in_spe...  41.2 us
    pallas_call x1, Pallas kernels, inverse_planes(): pl.pallas_call(inverse_plane_kernel, grid=(sets, planes // plane_step), i...  31.5 us
    reshape x2, local copies, waits for them, and re-layouts, score_grids(): along_y = along_y.reshape(sets, box, 2, size, size)  21.2 us
    dot_general x1, matrix products, score_grids(): jnp.einsum('tu,sujk->stjk', h_from_imag, prod_imag, precision=SPLIT3)  18.1 us
    dot_general x2, matrix products, score_grids(): term_imag = jnp.einsum('uc,cjk->ujk', g_imag, stacked, precision=SPLIT3)  16.5 us
    dot_general x1, matrix products, score_grids(): jnp.einsum('tu,sujk->stjk', h_from_real, prod_real, precision=SPLIT3)  14.7 us
    dot_general x2, matrix products, score_grids(): term_real = jnp.einsum('uc,cjk->ujk', g_real, stacked, precision=SPLIT3)  12.6 us
  transfers between devices with their start and end apart: 3, of which 2 were waited for; matrix products, arithmetic and copies ran while one was open for 25% of the time, Pallas kernels for 7%

commit v1 on v0

--- a/solution.py
+++ b/solution.py
@@ -44,7 +44,7 @@
 
 def forward_plane_kernel(in_ref, rz_ref, ly_ref, out_ref):
     planes = in_ref.shape[1]
-    size = in_ref.shape[3]
+    size = out_ref.shape[3]
     rz_hi, rz_lo = hi_lo(rz_ref[...])
     ly_hi, ly_lo = hi_lo(ly_ref[...])
 
@@ -76,17 +76,70 @@
     lax.fori_loop(0, planes, body, 0)
 
 
-def forward_planes(block, tables, plane_step):
-    planes, size = block.shape[1], block.shape[3]
-    table_spec = pl.BlockSpec((2 * size, 2 * size), lambda i: (0, 0))
-    data_spec = pl.BlockSpec((2, plane_step, size, size), lambda i: (0, i, 0, 0))
+def forward_planes(block, tables, plane_step, size):
+    planes, rows, cols = block.shape[1], block.shape[2], block.shape[3]
+    table_specs = [pl.BlockSpec(t.shape, lambda i: (0, 0)) for t in tables]
     return pl.pallas_call(
         forward_plane_kernel,
         grid=(planes // plane_step,),
-        in_specs=[data_spec, table_spec, table_spec],
-        out_specs=data_spec,
-        out_shape=jax.ShapeDtypeStruct(block.shape, F32),
+        in_specs=[pl.BlockSpec((2, plane_step, rows, cols), lambda i: (0, i, 0, 0))] + table_specs,
+        out_specs=pl.BlockSpec((2, plane_step, size, size), lambda i: (0, i, 0, 0)),
+        out_shape=jax.ShapeDtypeStruct((2, planes, size, size), F32),
     )(block, *tables)
+
+
+def cross_kernel(*refs, blocks, sets, box, window, part):
+    rec_refs = refs[:blocks]
+    lig_ref = refs[blocks]
+    g_tables = [hi_lo(t[...]) for t in refs[blocks + 1 : 2 * blocks + 1]]
+    gl_hi, gl_lo = hi_lo(refs[2 * blocks + 1][...])
+    h_hi, h_lo = hi_lo(refs[2 * blocks + 2][...])
+    out_ref = refs[-1]
+    rows = out_ref.shape[3]
+    lanes = out_ref.shape[4]
+
+    def body(r, carry):
+        rec = None
+        for b in range(blocks):
+            piece = rec_refs[b][:, :, r, :].reshape(2 * part, lanes)
+            term = split_dot(piece, g_tables[b][0], g_tables[b][1], False)
+            rec = term if rec is None else rec + term
+        rec_real = rec[:window]
+        rec_imag = rec[window:]
+        for s in range(sets):
+            piece = lig_ref[:, s * box : (s + 1) * box, r, :].reshape(2 * box, lanes)
+            lig = split_dot(piece, gl_hi, gl_lo, False)
+            lig_real = lig[:window]
+            lig_imag = lig[window:]
+            prod = jnp.concatenate(
+                [rec_real * lig_real + rec_imag * lig_imag, rec_imag * lig_real - rec_real * lig_imag],
+                axis=0,
+            )
+            back = split_dot(prod, h_hi, h_lo, False)
+            out_ref[s, :, :, r, :] = back.reshape(2, part, lanes)
+        return carry
+
+    lax.fori_loop(0, rows, body, 0)
+
+
+def cross_spectra(rec_blocks, lig_yz, g_tables, gl, hx, sets, box, window, row_step):
+    part = rec_blocks[0].shape[1]
+    size = rec_blocks[0].shape[2]
+    lanes = rec_blocks[0].shape[3]
+    blocks = len(rec_blocks)
+    tables = list(g_tables) + [gl, hx]
+    kernel = functools.partial(
+        cross_kernel, blocks=blocks, sets=sets, box=box, window=window, part=part
+    )
+    return pl.pallas_call(
+        kernel,
+        grid=(size // row_step,),
+        in_specs=[pl.BlockSpec((2, part, row_step, lanes), lambda i: (0, 0, i, 0))] * blocks
+        + [pl.BlockSpec((2, sets * box, row_step, lanes), lambda i: (0, 0, i, 0))]
+        + [pl.BlockSpec(t.shape, lambda i: (0, 0)) for t in tables],
+        out_specs=pl.BlockSpec((sets, 2, part, row_step, lanes), lambda i: (0, 0, 0, i, 0)),
+        out_shape=jax.ShapeDtypeStruct((sets, 2, part, size, lanes), F32),
+    )(*rec_blocks, lig_yz, *tables)
 
 
 def inverse_planes(spectra, tables, plane_step):
@@ -118,6 +171,26 @@
     return lax.psum(placed, axis_name)
 
 
+def gather_pieces(piece, axis_name, dim):
+    count = lax.axis_size(axis_name)
+    if count & (count - 1):
+        return gather_by_sum(piece, axis_name, dim)
+    index = lax.axis_index(axis_name)
+    held = piece
+    step = 1
+    while step < count:
+        pairs = [(i, i ^ step) for i in range(count)]
+        other = lax.ppermute(held, axis_name, perm=pairs)
+        low_half = (index // step) % 2 == 0
+        held = jnp.where(
+            low_half,
+            jnp.concatenate([held, other], axis=dim),
+            jnp.concatenate([other, held], axis=dim),
+        )
+        step *= 2
+    return held
+
+
 def score_grids(receptor, ligand_box, channel_weight):
     size = receptor.shape[2]
     slab_count = lax.axis_size("slab")
@@ -127,8 +200,9 @@
     extra = -(-(box - 1) // part)
     window = part * (1 + extra)
     plane_step = 8
-
-    full_box = gather_by_sum(ligand_box, "slab", 3)
+    row_step = 8
+
+    full_box = gather_pieces(ligand_box, "slab", 3)
     blocks = [receptor]
     for hop in range(1, extra + 1):
         pairs = [(i, (i - hop) % slab_count) for i in range(slab_count)]
@@ -137,55 +211,27 @@
     cos_n, sin_n = phase_tables(size, size, size)
     rz = block2(cos_n, -sin_n, sin_n, cos_n)
     ly = block2(cos_n, sin_n, -sin_n, cos_n)
-    forward_tables = (rz, ly)
+    rec_blocks = [forward_planes(planes, (rz, ly), plane_step, size) for planes in blocks]
+
+    lig = jnp.stack(
+        [full_box[:, 0, 0] * channel_weight[0], full_box[:, 0, 1] * channel_weight[1]], axis=0
+    ).reshape(2, sets * box, box, box)
+    cos_b, sin_b = phase_tables(box, size, size)
+    rz_box = block2(cos_b, -sin_b, sin_b, cos_b)
+    ly_box = block2(cos_b.T, sin_b.T, -sin_b.T, cos_b.T)
+    lig_yz = forward_planes(lig, (rz_box, ly_box), plane_step, size)
 
     cos_w, sin_w = phase_tables(window, window, window)
-    rec_real = None
-    rec_imag = None
-    for index, planes in enumerate(blocks):
-        along_yz = forward_planes(planes, forward_tables, plane_step)
+    g_tables = []
+    for index in range(len(blocks)):
         cols = slice(index * part, (index + 1) * part)
-        stacked = along_yz.reshape(2 * part, size, size)
-        g_real = jnp.concatenate([cos_w[:, cols], sin_w[:, cols]], axis=1)
-        g_imag = jnp.concatenate([-sin_w[:, cols], cos_w[:, cols]], axis=1)
-        term_real = jnp.einsum("uc,cjk->ujk", g_real, stacked, precision=SPLIT3)
-        term_imag = jnp.einsum("uc,cjk->ujk", g_imag, stacked, precision=SPLIT3)
-        rec_real = term_real if rec_real is None else rec_real + term_real
-        rec_imag = term_imag if rec_imag is None else rec_imag + term_imag
-
-    lig_real = full_box[:, 0, 0] * channel_weight[0]
-    lig_imag = full_box[:, 0, 1] * channel_weight[1]
-    cos_b, sin_b = phase_tables(box, size, size)
-    z_real = jnp.einsum("sxyz,zk->sxyk", lig_real, cos_b, precision=SPLIT3) + jnp.einsum(
-        "sxyz,zk->sxyk", lig_imag, sin_b, precision=SPLIT3
-    )
-    z_imag = jnp.einsum("sxyz,zk->sxyk", lig_imag, cos_b, precision=SPLIT3) - jnp.einsum(
-        "sxyz,zk->sxyk", lig_real, sin_b, precision=SPLIT3
-    )
-    cos_yb = cos_b.T
-    sin_yb = sin_b.T
-    wy = block2(cos_yb, sin_yb, -sin_yb, cos_yb)
-    along_y = jnp.einsum(
-        "jc,sxck->sxjk", wy, jnp.concatenate([z_real, z_imag], axis=2), precision=SPLIT3
-    )
-    along_y = along_y.reshape(sets, box, 2, size, size)
+        g_tables.append(block2(cos_w[:, cols], sin_w[:, cols], -sin_w[:, cols], cos_w[:, cols]))
     cos_xb, sin_xb = phase_tables(window, box, window)
-    lx_real = jnp.stack([cos_xb, sin_xb], axis=2)
-    lx_imag = jnp.stack([-sin_xb, cos_xb], axis=2)
-    lig_spec_real = jnp.einsum("uxc,sxcjk->sujk", lx_real, along_y, precision=SPLIT3)
-    lig_spec_imag = jnp.einsum("uxc,sxcjk->sujk", lx_imag, along_y, precision=SPLIT3)
-
-    prod_real = rec_real[None] * lig_spec_real + rec_imag[None] * lig_spec_imag
-    prod_imag = rec_imag[None] * lig_spec_real - rec_real[None] * lig_spec_imag
-
+    gl = block2(cos_xb, sin_xb, -sin_xb, cos_xb)
     cos_t, sin_t = phase_tables(part, window, window)
     scale = 1.0 / float(window * size * size)
-    h_from_real = jnp.concatenate([cos_t, sin_t], axis=0) * scale
-    h_from_imag = jnp.concatenate([-sin_t, cos_t], axis=0) * scale
-    back_x = jnp.einsum("tu,sujk->stjk", h_from_real, prod_real, precision=SPLIT3) + jnp.einsum(
-        "tu,sujk->stjk", h_from_imag, prod_imag, precision=SPLIT3
-    )
-    back_x = back_x.reshape(sets, 2, part, size, size)
+    hx = block2(cos_t, -sin_t, sin_t, cos_t) * scale
+    back_x = cross_spectra(rec_blocks, lig_yz, g_tables, gl, hx, sets, box, window, row_step)
 
     lyi = block2(cos_n, -sin_n, sin_n, cos_n)
     rzi = jnp.concatenate([cos_n, -sin_n], axis=0)
@@ -204,7 +250,7 @@
     pose_member,
     size,
 ):
-    all_centers = gather_by_sum(cluster_center, "rot", 0)
+    all_centers = gather_pieces(cluster_center, "rot", 0)
     local_count = cluster_center.shape[0]
     cluster = pose_owner[:, 0] * local_count + pose_member
     rotation = jnp.take(rotation_table, pose_rotation, axis=1, mode="clip").T.reshape(-1, 3, 3)

time: 309 us -> 266 us (0.86)
  Pallas kernels: 72.7 us -> 209 us
  matrix products: 93.9 us -> 2.39 us
  waiting for transfers between devices: 77.1 us -> 24.5 us
  local copies, waits for them, and re-layouts: 40.8 us -> 4.63 us
  between operations: 14.9 us -> 0.85 us
  other arithmetic: 4 us -> 14.5 us
  starting transfers between devices: 2.54 us -> 9.44 us
    pallas_call x0 -> x1, Pallas kernels: none -> 109 us  [cross_spectra(): pl.pallas_call(kernel, grid=(size // row_step,), in_specs=[pl.BlockSpec((...]
    dot_general x13 -> x0, matrix products: 91.4 us -> none  [the longest x1 18.1 us: score_grids(): jnp.einsum('tu,sujk->stjk', h_from_imag, prod_imag, precision=SPLIT3)]
    psum x2 -> x0, waiting for transfers between devices: 77.1 us -> none  [gather_by_sum(): return lax.psum(placed, axis_name)]
    pallas_call x2 -> x3, Pallas kernels: 41.2 us -> 69.1 us  [forward_planes(): pl.pallas_call(forward_plane_kernel, grid=(planes // plane_step,), in_spe...]
    ppermute x0 -> x5, waiting for transfers between devices: none -> 24.5 us  [gather_pieces(): other = lax.ppermute(held, axis_name, perm=pairs)]
    reshape x2 -> x0, local copies, waits for them, and re-layouts: 21.2 us -> none  [score_grids(): along_y = along_y.reshape(sets, box, 2, size, size)]
    add x1 -> x0, local copies, waits for them, and re-layouts: 11.5 us -> none  [score_grids(): jnp.einsum('tu,sujk->stjk', h_from_real, prod_real, precision=SPLIT3)]
    ppermute x0 -> x5, starting transfers between devices: none -> 6.81 us  [gather_pieces(): other = lax.ppermute(held, axis_name, perm=pairs)]
  transfers between devices with their start and end apart: 3 -> 6, of which waited for: 2 -> 2; matrix products, arithmetic and copies ran while one was open for 25% -> 8% of each run, Pallas kernels for 7% -> 18%
where the time goes in v1:
time: 266 us
  Pallas kernels  209 us (79%)
  waiting for transfers between devices  24.5 us (9%)
  other arithmetic  14.5 us (5%)
  starting transfers between devices  9.44 us (4%)
  local copies, waits for them, and re-layouts  4.63 us (2%)
    pallas_call x1, Pallas kernels, cross_spectra(): pl.pallas_call(kernel, grid=(size // row_step,), in_specs=[pl.BlockSpec((...  109 us
    pallas_call x3, Pallas kernels, forward_planes(): pl.pallas_call(forward_plane_kernel, grid=(planes // plane_step,), in_spe...  69.1 us
    pallas_call x1, Pallas kernels, inverse_planes(): pl.pallas_call(inverse_plane_kernel, grid=(sets, planes // plane_step), i...  31.5 us
    ppermute x5, waiting for transfers between devices, gather_pieces(): other = lax.ppermute(held, axis_name, perm=pairs)  24.5 us
    ppermute x5, starting transfers between devices, gather_pieces(): other = lax.ppermute(held, axis_name, perm=pairs)  6.81 us
  transfers between devices with their start and end apart: 6, of which 2 were waited for; matrix products, arithmetic and copies ran while one was open for 8% of the time, Pallas kernels for 18%

profile of v1, /device:TPU:0, one launch (start us, length us, event | category | flops | bytes accessed | tf_op | source)
XLA Modules:
  0.0 265.7 jit_solution(2106185676368758069)
XLA Ops:
  1.2 2.6 collective-permute-start
  3.8 0.7 copy.56
  4.5 1.5 collective-permute-start.3
  8.1 0.7 and_select_fusion.3
  8.8 0.8 copy.53
  10.2 0.7 gather_fusion
  11.7 0.8 maximum_maximum_fusion.ly_ref
  13.1 0.7 maximum_maximum_fusion.4.refs_5_
  14.0 0.8 maximum_maximum_fusion.2
  14.7 0.8 fusion.4
  16.8 1.6 collective-permute-start.4
  19.1 1.7 collective-permute-done.4
  20.8 2.7 collective-permute-start.5
  23.5 20.2 %shard_map.113.refs_0_ = f32[2,32,128,128]{3,2,1,0:T(8,128)} custom-call(f32[2,32,128,128]{3,2,1,0:T(8,128)} %in_ref.1, f32[256,256]{1,0:T(8,128)} %get-tuple-element.17.rz_ref.ly_ref, f32[256,256]{1,0:T(8,128)} %get-tuple-element.16.ly_ref), custom_call_target="tpu_custom_call" | custom-call | tf_op jit(solution)/shard_map/pallas_call | solution.py:82
  43.7 1.0 gather_fusion.1
  45.7 1.9 fusion.1
  47.6 1.1 maximum_select_fusion.2
  50.1 22.8 %collective-permute-done.2 = f32[2,1,2,16,32,32]{5,4,3,2,1,0:T(8,128)S(1)} collective-permute-done((f32[2,1,2,16,32,32]{5,4,3,2,1,0:T(8,128)}, f32[2,1,2,16,32,32]{5,4,3,2,1,0:T(8,128)S(1)}, u32[]{:S(2)}, u32[]{:S(2)}) %collective-permute-start.2) | collective-permute-done | bytes 262176 | tf_op jit(solution)/shard_map/ppermute | solution.py:183
  73.4 1.6 slice_multiply_fusion.1
  74.9 1.6 pad_maximum_fusion.in_ref
  76.5 28.6 %shard_map.115.refs_2_ = f32[2,64,128,128]{3,2,1,0:T(8,128)} custom-call(f32[2,64,32,32]{3,2,1,0:T(8,128)} %pad_maximum_fusion.in_ref, f32[64,256]{1,0:T(8,128)} %maximum_maximum_fusion.1.rz_ref, f32[256,64]{1,0:T(8,128)} %maximum_maximum_fusion.ly_ref), custom_call_target="tpu_custom_call" | custom-call | tf_op jit(solution)/shard_map/pallas_call | solution.py:82
  105.1 20.2 %shard_map.114.refs_1_ = f32[2,32,128,128]{3,2,1,0:T(8,128)} custom-call(f32[2,32,128,128]{3,2,1,0:T(8,128)} %collective-permute-done.in_ref, f32[256,256]{1,0:T(8,128)} %get-tuple-element.17.rz_ref.ly_ref, f32[256,256]{1,0:T(8,128)} %get-tuple-element.16.ly_ref), custom_call_target="tpu_custom_call" | custom-call | tf_op jit(solution)/shard_map/pallas_call | solution.py:82
  125.4 108.8 %shard_map.116.in_ref = f32[2,2,32,128,128]{4,3,2,1,0:T(8,128)} custom-call(f32[2,32,128,128]{3,2,1,0:T(8,128)} %shard_map.113.refs_0_, f32[2,32,128,128]{3,2,1,0:T(8,128)} %shard_map.114.refs_1_, f32[2,64,128,128]{3,2,1,0:T(8,128)} %shard_map.115.refs_2_, f32[128,64]{1,0:T(8,128)} %get-tuple-element.35.refs_3_, f32[128,64]{1,0:T(8,128)} %get-tuple-element.36.refs_4_, ...), custom_call_target="tpu_custom_call" | custom-call | tf_op jit(solution)/shard_map/pallas_call | solution.py:134
  234.2 31.5 %shard_map.117 = f32[2,32,128,128]{3,2,1,0:T(8,128)} custom-call(f32[2,2,32,128,128]{4,3,2,1,0:T(8,128)} %shard_map.116.in_ref, f32[256,256]{1,0:T(8,128)} %get-tuple-element.17.rz_ref.ly_ref, f32[256,128]{1,0:T(8,128)} %pad_maximum_fusion.5.rz_ref), custom_call_target="tpu_custom_call" | custom-call | tf_op jit(solution)/shard_map/pallas_call | solution.py:149
  (58 shorter events, 9.5 us)
Async XLA Ops:
  0.6 14.9 %copy-start = (f32[3,128]{1,0:T(4,128)S(1)}, f32[3,128]{1,0:T(4,128)}, u32[]{:S(2)}) copy-start(f32[3,128]{1,0:T(4,128)} %param.14) | copy-start | bytes 4612
  0.6 14.9 %copy-start.4 = (s32[256,1]{0,1:T(1,128)S(1)}, s32[256,1]{0,1:T(1,128)}, u32[]{:S(2)}) copy-start(s32[256,1]{0,1:T(1,128)} %param.18) | copy-start | bytes 3076
  0.7 17.8 %copy-start.2 = (f32[2]{0:T(128)S(1)}, f32[2]{0:T(128)}, u32[]{:S(2)}) copy-start(f32[2]{0:T(128)} %param.12) | copy-start | bytes 28
  0.7 18.4 %copy-start.3 = (s32[256]{0:T(256)S(1)}, s32[256]{0:T(256)}, u32[]{:S(2)}) copy-start(s32[256]{0:T(256)} %param.19) | copy-start | bytes 3076
  0.7 46.9 %collective-permute-start.1 = (f32[2,1,2,8,32,32]{5,4,3,2,1,0:T(8,128)}, f32[2,1,2,8,32,32]{5,4,3,2,1,0:T(8,128)S(1)}, u32[]{:S(2)}, u32[]{:S(2)}) collective-permute-start(f32[2,1,2,8,32,32]{5,4,3,2,1,0:T(8,128)} %param.11), channel_id=1, source_target_pairs={{0,8},{8,0},{16,24},{24,16},{1,9},{9,1},{17,25},{25,17},{2,10},{10... | collective-permute-start | bytes 393224 | tf_op jit(solution)/shard_map/ppermute | solution.py:183
  1.2 103.9 %collective-permute-start = (f32[2,32,128,128]{3,2,1,0:T(8,128)}, f32[2,32,128,128]{3,2,1,0:T(8,128)}, u32[]{:S(2)}, u32[]{:S(2)}) collective-permute-start(f32[2,32,128,128]{3,2,1,0:T(8,128)} %in_ref.1), channel_id=1, source_target_pairs={{0,24},{8,0},{16,8},{24,16},{1,25},{9,1},{17,9},{25,17},{2,26},{10... | collective-permute-start | bytes 12582920 | tf_op jit(solution)/shard_map/ppermute | solution.py:209
  4.5 12.3 %collective-permute-start.3 = (f32[8,3,128]{2,1,0:T(4,128)S(1)}, f32[8,3,128]{2,1,0:T(4,128)S(1)}, u32[]{:S(2)}, u32[]{:S(2)}) collective-permute-start(f32[8,3,128]{2,1,0:T(4,128)S(1)} %copy.56), channel_id=1, source_target_pairs={{0,1},{1,0},{2,3},{3,2},{4,5},{5,4},{6,7},{7,6},{8,9},{9,8},{10,11... | collective-permute-start | bytes 36872 | tf_op jit(solution)/shard_map/ppermute | solution.py:183
  16.8 4.0 %collective-permute-start.4 = (f32[16,3,128]{2,1,0:T(4,128)S(1)}, f32[16,3,128]{2,1,0:T(4,128)S(1)}, u32[]{:S(2)}, u32[]{:S(2)}) collective-permute-start(f32[16,3,128]{2,1,0:T(4,128)S(1)} %maximum_select_fusion.5), channel_id=1, source_target_pairs={{0,2},{1,3},{2,0},{3,1},{4,6},{5,7},{6,4},{7,5},{8,10},{9,11},{10,... | collective-permute-start | bytes 73736 | tf_op jit(solution)/shard_map/ppermute | solution.py:183
  20.8 22.9 %collective-permute-start.5 = (f32[32,3,128]{2,1,0:T(4,128)S(1)}, f32[32,3,128]{2,1,0:T(4,128)S(1)}, u32[]{:S(2)}, u32[]{:S(2)}) collective-permute-start(f32[32,3,128]{2,1,0:T(4,128)S(1)} %maximum_select_fusion.4), channel_id=1, source_target_pairs={{0,4},{1,5},{2,6},{3,7},{4,0},{5,1},{6,2},{7,3},{8,12},{9,13},{10,... | collective-permute-start | bytes 147464 | tf_op jit(solution)/shard_map/ppermute | solution.py:183
  45.0 2.5 copy-start.1
  48.7 24.3 %collective-permute-start.2 = (f32[2,1,2,16,32,32]{5,4,3,2,1,0:T(8,128)}, f32[2,1,2,16,32,32]{5,4,3,2,1,0:T(8,128)S(1)}, u32[]{:S(2)}, u32[]{:S(2)}) collective-permute-start(f32[2,1,2,16,32,32]{5,4,3,2,1,0:T(8,128)} %maximum_select_fusion.2), channel_id=1, source_target_pairs={{0,16},{8,24},{16,0},{24,8},{1,17},{9,25},{17,1},{25,9},{2,18},{10... | collective-permute-start | bytes 786440 | tf_op jit(solution)/shard_map/ppermute | solution.py:183

commit v2 on v1

--- a/solution.py
+++ b/solution.py
@@ -43,21 +43,28 @@
 
 
 def forward_plane_kernel(in_ref, rz_ref, ly_ref, out_ref):
-    planes = in_ref.shape[1]
+    planes, rows, cols = in_ref.shape[1], in_ref.shape[2], in_ref.shape[3]
     size = out_ref.shape[3]
     rz_hi, rz_lo = hi_lo(rz_ref[...])
     ly_hi, ly_lo = hi_lo(ly_ref[...])
-
-    def body(p, carry):
-        joined = jnp.concatenate([in_ref[0, p], in_ref[1, p]], axis=1)
-        along_z = split_dot(joined, rz_hi, rz_lo, True)
-        stacked = jnp.concatenate([along_z[:, :size], along_z[:, size:]], axis=0)
-        along_y = split_dot(stacked, ly_hi, ly_lo, False)
-        out_ref[0, p] = along_y[:size]
-        out_ref[1, p] = along_y[size:]
-        return carry
-
-    lax.fori_loop(0, planes, body, 0)
+    joined = jnp.concatenate(
+        [in_ref[0].reshape(planes * rows, cols), in_ref[1].reshape(planes * rows, cols)], axis=1
+    )
+    along_z = split_dot(joined, rz_hi, rz_lo, True)
+    stacked = jnp.concatenate(
+        [
+            jnp.concatenate(
+                [along_z[p * rows : (p + 1) * rows, :size], along_z[p * rows : (p + 1) * rows, size:]],
+                axis=0,
+            )
+            for p in range(planes)
+        ],
+        axis=1,
+    )
+    along_y = split_dot(stacked, ly_hi, ly_lo, False)
+    for p in range(planes):
+        out_ref[0, p] = along_y[:size, p * size : (p + 1) * size]
+        out_ref[1, p] = along_y[size:, p * size : (p + 1) * size]
 
 
 def inverse_plane_kernel(in_ref, ly_ref, rz_ref, out_ref):
@@ -65,15 +72,21 @@
     size = in_ref.shape[4]
     ly_hi, ly_lo = hi_lo(ly_ref[...])
     rz_hi, rz_lo = hi_lo(rz_ref[...])
-
-    def body(p, carry):
-        stacked = jnp.concatenate([in_ref[0, 0, p], in_ref[0, 1, p]], axis=0)
-        along_y = split_dot(stacked, ly_hi, ly_lo, False)
-        joined = jnp.concatenate([along_y[:size], along_y[size:]], axis=1)
-        out_ref[0, p] = split_dot(joined, rz_hi, rz_lo, True)
-        return carry
-
-    lax.fori_loop(0, planes, body, 0)
+    stacked = jnp.concatenate(
+        [jnp.concatenate([in_ref[0, 0, p], in_ref[0, 1, p]], axis=0) for p in range(planes)], axis=1
+    )
+    along_y = split_dot(stacked, ly_hi, ly_lo, False)
+    joined = jnp.concatenate(
+        [
+            jnp.concatenate(
+                [along_y[:size, p * size : (p + 1) * size], along_y[size:, p * size : (p + 1) * size]],
+                axis=1,
+            )
+            for p in range(planes)
+        ],
+        axis=0,
+    )
+    out_ref[0] = split_dot(joined, rz_hi, rz_lo, True).reshape(planes, size, size)
 
 
 def forward_planes(block, tables, plane_step, size):
@@ -98,28 +111,28 @@
     rows = out_ref.shape[3]
     lanes = out_ref.shape[4]
 
-    def body(r, carry):
-        rec = None
-        for b in range(blocks):
-            piece = rec_refs[b][:, :, r, :].reshape(2 * part, lanes)
-            term = split_dot(piece, g_tables[b][0], g_tables[b][1], False)
-            rec = term if rec is None else rec + term
-        rec_real = rec[:window]
-        rec_imag = rec[window:]
-        for s in range(sets):
-            piece = lig_ref[:, s * box : (s + 1) * box, r, :].reshape(2 * box, lanes)
-            lig = split_dot(piece, gl_hi, gl_lo, False)
-            lig_real = lig[:window]
-            lig_imag = lig[window:]
-            prod = jnp.concatenate(
-                [rec_real * lig_real + rec_imag * lig_imag, rec_imag * lig_real - rec_real * lig_imag],
-                axis=0,
-            )
-            back = split_dot(prod, h_hi, h_lo, False)
-            out_ref[s, :, :, r, :] = back.reshape(2, part, lanes)
-        return carry
-
-    lax.fori_loop(0, rows, body, 0)
+    def gathered(ref, lo, count):
+        return jnp.concatenate(
+            [ref[:, lo : lo + count, r, :].reshape(2 * count, lanes) for r in range(rows)], axis=1
+        )
+
+    rec = None
+    for b in range(blocks):
+        term = split_dot(gathered(rec_refs[b], 0, part), g_tables[b][0], g_tables[b][1], False)
+        rec = term if rec is None else rec + term
+    rec_real = rec[:window]
+    rec_imag = rec[window:]
+    for s in range(sets):
+        lig = split_dot(gathered(lig_ref, s * box, box), gl_hi, gl_lo, False)
+        lig_real = lig[:window]
+        lig_imag = lig[window:]
+        prod = jnp.concatenate(
+            [rec_real * lig_real + rec_imag * lig_imag, rec_imag * lig_real - rec_real * lig_imag],
+            axis=0,
+        )
+        back = split_dot(prod, h_hi, h_lo, False)
+        for r in range(rows):
+            out_ref[s, :, :, r, :] = back[:, r * lanes : (r + 1) * lanes].reshape(2, part, lanes)
 
 
 def cross_spectra(rec_blocks, lig_yz, g_tables, gl, hx, sets, box, window, row_step):
@@ -203,10 +216,11 @@
     row_step = 8
 
     full_box = gather_pieces(ligand_box, "slab", 3)
+    full_box, outgoing = lax.optimization_barrier((full_box, receptor))
     blocks = [receptor]
     for hop in range(1, extra + 1):
         pairs = [(i, (i - hop) % slab_count) for i in range(slab_count)]
-        blocks.append(lax.ppermute(receptor, "slab", perm=pairs))
+        blocks.append(lax.ppermute(outgoing, "slab", perm=pairs))
 
     cos_n, sin_n = phase_tables(size, size, size)
     rz = block2(cos_n, -sin_n, sin_n, cos_n)

time: 266 us -> 139 us (0.52)
  Pallas kernels: 209 us -> 74.1 us
  waiting for transfers between devices: 24.5 us -> 29.7 us
    pallas_call x1, Pallas kernels: 109 us -> 33.3 us  [cross_spectra(): pl.pallas_call(kernel, grid=(size // row_step,), in_specs=[pl.BlockSpec((...]
    pallas_call x3, Pallas kernels: 69.1 us -> 29.1 us  [forward_planes(): pl.pallas_call(forward_plane_kernel, grid=(planes // plane_step,), in_spe...]
    pallas_call x1, Pallas kernels: 31.5 us -> 11.8 us  [inverse_planes(): pl.pallas_call(inverse_plane_kernel, grid=(sets, planes // plane_step), i...]
    ppermute x1, waiting for transfers between devices: 0.01 us -> 5.46 us  [score_grids(): blocks.append(lax.ppermute(outgoing, 'slab', perm=pairs))]
  transfers between devices with their start and end apart: 6 -> 6, of which waited for: 2 -> 3; matrix products, arithmetic and copies ran while one was open for 8% -> 17% of each run, Pallas kernels for 18% -> 14%
where the time goes in v2:
time: 139 us; the launch traced here: 138 us
  Pallas kernels  74.1 us (53%)
  waiting for transfers between devices  29.7 us (21%)
  other arithmetic  15.1 us (11%)
  starting transfers between devices  9.59 us (7%)
  local copies, waits for them, and re-layouts  4.71 us (3%)
  matrix products  3.43 us (2%)
    pallas_call x1, Pallas kernels, cross_spectra(): pl.pallas_call(kernel, grid=(size // row_step,), in_specs=[pl.BlockSpec((...  33.3 us
    pallas_call x3, Pallas kernels, forward_planes(): pl.pallas_call(forward_plane_kernel, grid=(planes // plane_step,), in_spe...  29.1 us
    ppermute x5, waiting for transfers between devices, gather_pieces(): other = lax.ppermute(held, axis_name, perm=pairs)  24.2 us
    pallas_call x1, Pallas kernels, inverse_planes(): pl.pallas_call(inverse_plane_kernel, grid=(sets, planes // plane_step), i...  11.8 us
    ppermute x5, starting transfers between devices, gather_pieces(): other = lax.ppermute(held, axis_name, perm=pairs)  8.84 us
    ppermute x1, waiting for transfers between devices, score_grids(): blocks.append(lax.ppermute(outgoing, 'slab', perm=pairs))  5.46 us
    concatenate x5, other arithmetic, block2(): return jnp.concatenate([top, bottom], axis=0)  3.72 us
    dot_general x1, matrix products, pose_statistics(): jnp.einsum('pja,pka->pjk', moved_centred, center_centred, precision=PRECISE)  2.92 us
  transfers between devices with their start and end apart: 6, of which 3 were waited for; matrix products, arithmetic and copies ran while one was open for 17% of the time, Pallas kernels for 14%

profile of v2, /device:TPU:0, one launch (start us, length us, event | category | flops | bytes accessed | tf_op | source)
XLA Modules:
  0.0 137.6 jit_solution(10953686620987474497)
XLA Ops:
  1.2 0.7 copy.56
  1.9 2.5 %collective-permute-start.3 = (f32[8,3,128]{2,1,0:T(4,128)S(1)}, f32[8,3,128]{2,1,0:T(4,128)S(1)}, u32[]{:S(2)}, u32[]{:S(2)}) collective-permute-start(f32[8,3,128]{2,1,0:T(4,128)S(1)} %copy.56), channel_id=1, source_target_pairs={{0,1},{1,0},{2,3},{3,2},{4,5},{5,4},{6,7},{7,6},{8,9},{9,8},{10,11... | collective-permute-start | bytes 36872 | tf_op jit(solution)/shard_map/ppermute | solution.py:196
  7.9 2.4 %maximum_select_fusion.2 = f32[2,1,2,16,32,32]{5,4,3,2,1,0:T(8,128)} fusion(f32[2,1,2,8,32,32]{5,4,3,2,1,0:T(8,128)S(1)} %collective-permute-done, f32[2,1,2,8,32,32]{5,4,3,2,1,0:T(8,128)} %param.11, pred[]{:T(512)S(6)} %eq.37), kind=kLoop, calls=%fused_computation.7 | loop fusion | flops 196608 | bytes 524289 | tf_op jit(solution)/shard_map/jit(_where)/select_n | solution.py:198
  10.3 1.5 %collective-permute-start.1 = (f32[2,1,2,16,32,32]{5,4,3,2,1,0:T(8,128)}, f32[2,1,2,16,32,32]{5,4,3,2,1,0:T(8,128)S(1)}, u32[]{:S(2)}, u32[]{:S(2)}) collective-permute-start(f32[2,1,2,16,32,32]{5,4,3,2,1,0:T(8,128)} %maximum_select_fusion.2), channel_id=1, source_target_pairs={{0,16},{8,24},{16,0},{24,8},{1,17},{9,25},{17,1},{25,9},{2,18},{10... | collective-permute-start | bytes 786440 | tf_op jit(solution)/shard_map/ppermute | solution.py:196
  12.0 0.7 gather_fusion
  13.2 22.5 %collective-permute-done.1 = f32[2,1,2,16,32,32]{5,4,3,2,1,0:T(8,128)S(1)} collective-permute-done((f32[2,1,2,16,32,32]{5,4,3,2,1,0:T(8,128)}, f32[2,1,2,16,32,32]{5,4,3,2,1,0:T(8,128)S(1)}, u32[]{:S(2)}, u32[]{:S(2)}) %collective-permute-start.1) | collective-permute-done | bytes 262176 | tf_op jit(solution)/shard_map/ppermute | solution.py:196
  36.3 0.8 collective-permute-start.2
  38.0 0.8 maximum_maximum_fusion.ly_ref
  38.9 0.8 maximum_maximum_fusion.2
  39.7 0.9 fusion.4
  41.8 1.6 %collective-permute-start.4 = (f32[16,3,128]{2,1,0:T(4,128)S(1)}, f32[16,3,128]{2,1,0:T(4,128)S(1)}, u32[]{:S(2)}, u32[]{:S(2)}) collective-permute-start(f32[16,3,128]{2,1,0:T(4,128)S(1)} %maximum_select_fusion.5), channel_id=1, source_target_pairs={{0,2},{1,3},{2,0},{3,1},{4,6},{5,7},{6,4},{7,5},{8,10},{9,11},{10,... | collective-permute-start | bytes 73736 | tf_op jit(solution)/shard_map/ppermute | solution.py:196
  44.1 1.7 %collective-permute-done.4 = f32[16,3,128]{2,1,0:T(4,128)S(1)} collective-permute-done((f32[16,3,128]{2,1,0:T(4,128)S(1)}, f32[16,3,128]{2,1,0:T(4,128)S(1)}, u32[]{:S(2)}, u32[]{:S(2)}) %collective-permute-start.4) | collective-permute-done | bytes 24608 | tf_op jit(solution)/shard_map/ppermute | solution.py:196
  45.8 2.7 %collective-permute-start.5 = (f32[32,3,128]{2,1,0:T(4,128)S(1)}, f32[32,3,128]{2,1,0:T(4,128)S(1)}, u32[]{:S(2)}, u32[]{:S(2)}) collective-permute-start(f32[32,3,128]{2,1,0:T(4,128)S(1)} %maximum_select_fusion.4), channel_id=1, source_target_pairs={{0,4},{1,5},{2,6},{3,7},{4,0},{5,1},{6,2},{7,3},{8,12},{9,13},{10,... | collective-permute-start | bytes 147464 | tf_op jit(solution)/shard_map/ppermute | solution.py:196
  48.5 9.2 %shard_map.113.refs_0_ = f32[2,32,128,128]{3,2,1,0:T(8,128)} custom-call(f32[2,32,128,128]{3,2,1,0:T(8,128)} %in_ref.1, f32[256,256]{1,0:T(8,128)} %get-tuple-element.21.rz_ref.ly_ref, f32[256,256]{1,0:T(8,128)} %get-tuple-element.20.ly_ref), custom_call_target="tpu_custom_call" | custom-call | tf_op jit(solution)/shard_map/pallas_call | solution.py:95
  57.7 1.0 gather_fusion.1
  59.0 1.0 copy.60
  60.4 2.9 %fusion.1 = f32[256,3,3]{2,1,0:T(4,128)S(1)} fusion(f32[256,3,128]{2,1,0:T(4,128)} %copy.60, f32[256,3,128]{2,1,0:T(4,128)S(1)} %gather_fusion.1, f32[256,3]{1,0:T(8,128)S(1)} %broadcast_multiply_fusion), kind=kOutput, calls=%fused_computation.10 | convolution fusion | flops 3637248 | bytes 798720 | tf_op jit(solution)/shard_map/pja,pka->pjk/dot_general | solution.py:286
  64.1 1.5 %slice_multiply_fusion.1 = (f32[2,1,1,32,32,32]{5,4,3,2,1,0:T(8,128)S(1)}, f32[2,1,1,32,32,32]{5,4,3,2,1,0:T(8,128)S(1)}) fusion(f32[2,1,2,32,32,32]{5,4,3,2,1,0:T(8,128)S(1)} %maximum_select_fusion, f32[]{:T(128)} %bitcast.3, f32[]{:T(128)} %bitcast.5), kind=kLoop, calls=%fused_computation.9 | loop fusion | flops 131072 | bytes 1048584 | tf_op jit(solution)/shard_map/mul | solution.py:231
  65.7 1.6 %pad_maximum_fusion.in_ref = f32[2,64,32,32]{3,2,1,0:T(8,128)} fusion(f32[1,64,32,32]{3,2,1,0:T(8,128)S(1)} %bitcast.29, f32[1,64,32,32]{3,2,1,0:T(8,128)S(1)} %bitcast.28), kind=kLoop, calls=%fused_computation.3 | loop fusion | flops 131072 | bytes 1048576 | tf_op jit(solution)/shard_map/stack | solution.py:230
  67.2 10.7 %shard_map.115.refs_2_ = f32[2,64,128,128]{3,2,1,0:T(8,128)} custom-call(f32[2,64,32,32]{3,2,1,0:T(8,128)} %pad_maximum_fusion.in_ref, f32[64,256]{1,0:T(8,128)} %maximum_maximum_fusion.1.rz_ref, f32[256,64]{1,0:T(8,128)} %maximum_maximum_fusion.ly_ref), custom_call_target="tpu_custom_call" | custom-call | tf_op jit(solution)/shard_map/pallas_call | solution.py:95
  77.9 5.5 %collective-permute-done.2.in_ref = f32[2,32,128,128]{3,2,1,0:T(8,128)} collective-permute-done((f32[2,32,128,128]{3,2,1,0:T(8,128)}, f32[2,32,128,128]{3,2,1,0:T(8,128)}, u32[]{:S(2)}, u32[]{:S(2)}) %collective-permute-start.2) | collective-permute-done | bytes 4194336 | tf_op jit(solution)/shard_map/ppermute | solution.py:223
  83.4 9.2 %shard_map.114.refs_1_ = f32[2,32,128,128]{3,2,1,0:T(8,128)} custom-call(f32[2,32,128,128]{3,2,1,0:T(8,128)} %collective-permute-done.2.in_ref, f32[256,256]{1,0:T(8,128)} %get-tuple-element.21.rz_ref.ly_ref, f32[256,256]{1,0:T(8,128)} %get-tuple-element.20.ly_ref), custom_call_target="tpu_custom_call" | custom-call | tf_op jit(solution)/shard_map/pallas_call | solution.py:95
  92.6 33.3 %shard_map.116.in_ref = f32[2,2,32,128,128]{4,3,2,1,0:T(8,128)} custom-call(f32[2,32,128,128]{3,2,1,0:T(8,128)} %shard_map.113.refs_0_, f32[2,32,128,128]{3,2,1,0:T(8,128)} %shard_map.114.refs_1_, f32[2,64,128,128]{3,2,1,0:T(8,128)} %shard_map.115.refs_2_, f32[128,64]{1,0:T(8,128)} %get-tuple-element.39.refs_3_, f32[128,64]{1,0:T(8,128)} %get-tuple-element.40.refs_4_, ...), custom_call_target="tpu_custom_call" | custom-call | tf_op jit(solution)/shard_map/pallas_call | solution.py:147
  125.8 11.8 %shard_map.117 = f32[2,32,128,128]{3,2,1,0:T(8,128)} custom-call(f32[2,2,32,128,128]{4,3,2,1,0:T(8,128)} %shard_map.116.in_ref, f32[256,256]{1,0:T(8,128)} %get-tuple-element.21.rz_ref.ly_ref, f32[256,128]{1,0:T(8,128)} %pad_maximum_fusion.5.rz_ref), custom_call_target="tpu_custom_call" | custom-call | tf_op jit(solution)/shard_map/pallas_call | solution.py:162
  (62 shorter events, 9.6 us)
Async XLA Ops:
  0.6 39.9 %copy-start = (f32[3,128]{1,0:T(4,128)S(1)}, f32[3,128]{1,0:T(4,128)}, u32[]{:S(2)}) copy-start(f32[3,128]{1,0:T(4,128)} %param.14) | copy-start | bytes 4612
  0.6 12.4 %copy-start.1 = (f32[2,1,2,8,32,32]{5,4,3,2,1,0:T(8,128)S(1)}, f32[2,1,2,8,32,32]{5,4,3,2,1,0:T(8,128)}, u32[]{:S(2)}) copy-start(f32[2,1,2,8,32,32]{5,4,3,2,1,0:T(8,128)} %param.11) | copy-start | bytes 393220
  0.7 11.2 %copy-start.4 = (s32[256]{0:T(256)S(1)}, s32[256]{0:T(256)}, u32[]{:S(2)}) copy-start(s32[256]{0:T(256)} %param.16) | copy-start | bytes 3076
  0.7 11.2 %copy-start.2 = (f32[9,16]{1,0:T(8,128)S(1)}, f32[9,16]{1,0:T(8,128)}, u32[]{:S(2)}) copy-start(f32[9,16]{1,0:T(8,128)} %param.13) | copy-start | bytes 1732
  0.7 7.2 %collective-permute-start = (f32[2,1,2,8,32,32]{5,4,3,2,1,0:T(8,128)}, f32[2,1,2,8,32,32]{5,4,3,2,1,0:T(8,128)S(1)}, u32[]{:S(2)}, u32[]{:S(2)}) collective-permute-start(f32[2,1,2,8,32,32]{5,4,3,2,1,0:T(8,128)} %param.11), channel_id=1, source_target_pairs={{0,8},{8,0},{16,24},{24,16},{1,9},{9,1},{17,25},{25,17},{2,10},{10... | collective-permute-start | bytes 393224 | tf_op jit(solution)/shard_map/ppermute | solution.py:196
  1.9 39.9 %collective-permute-start.3 = (f32[8,3,128]{2,1,0:T(4,128)S(1)}, f32[8,3,128]{2,1,0:T(4,128)S(1)}, u32[]{:S(2)}, u32[]{:S(2)}) collective-permute-start(f32[8,3,128]{2,1,0:T(4,128)S(1)} %copy.56), channel_id=1, source_target_pairs={{0,1},{1,0},{2,3},{3,2},{4,5},{5,4},{6,7},{7,6},{8,9},{9,8},{10,11... | collective-permute-start | bytes 36872 | tf_op jit(solution)/shard_map/ppermute | solution.py:196
  10.3 25.5 %collective-permute-start.1 = (f32[2,1,2,16,32,32]{5,4,3,2,1,0:T(8,128)}, f32[2,1,2,16,32,32]{5,4,3,2,1,0:T(8,128)S(1)}, u32[]{:S(2)}, u32[]{:S(2)}) collective-permute-start(f32[2,1,2,16,32,32]{5,4,3,2,1,0:T(8,128)} %maximum_select_fusion.2), channel_id=1, source_target_pairs={{0,16},{8,24},{16,0},{24,8},{1,17},{9,25},{17,1},{25,9},{2,18},{10... | collective-permute-start | bytes 786440 | tf_op jit(solution)/shard_map/ppermute | solution.py:196
  36.2 4.3 %copy-start.6 = (s32[256,1]{0,1:T(1,128)S(1)}, s32[256,1]{0,1:T(1,128)}, u32[]{:S(2)}) copy-start(s32[256,1]{0,1:T(1,128)} %param.18) | copy-start | bytes 3076
  36.3 7.2 %copy-start.3 = (f32[2]{0:T(128)S(1)}, f32[2]{0:T(128)}, u32[]{:S(2)}) copy-start(f32[2]{0:T(128)} %param.12) | copy-start | bytes 28
  36.3 7.8 %copy-start.5 = (s32[256]{0:T(256)S(1)}, s32[256]{0:T(256)}, u32[]{:S(2)}) copy-start(s32[256]{0:T(256)} %param.19) | copy-start | bytes 3076
  36.3 47.1 %collective-permute-start.2 = (f32[2,32,128,128]{3,2,1,0:T(8,128)}, f32[2,32,128,128]{3,2,1,0:T(8,128)}, u32[]{:S(2)}, u32[]{:S(2)}) collective-permute-start(f32[2,32,128,128]{3,2,1,0:T(8,128)} %in_ref.1), channel_id=1, source_target_pairs={{0,24},{8,0},{16,8},{24,16},{1,25},{9,1},{17,9},{25,17},{2,26},{10... | collective-permute-start | bytes 12582920 | tf_op jit(solution)/shard_map/ppermute | solution.py:223
  41.8 4.0 %collective-permute-start.4 = (f32[16,3,128]{2,1,0:T(4,128)S(1)}, f32[16,3,128]{2,1,0:T(4,128)S(1)}, u32[]{:S(2)}, u32[]{:S(2)}) collective-permute-start(f32[16,3,128]{2,1,0:T(4,128)S(1)} %maximum_select_fusion.5), channel_id=1, source_target_pairs={{0,2},{1,3},{2,0},{3,1},{4,6},{5,7},{6,4},{7,5},{8,10},{9,11},{10,... | collective-permute-start | bytes 73736 | tf_op jit(solution)/shard_map/ppermute | solution.py:196
  45.8 11.9 %collective-permute-start.5 = (f32[32,3,128]{2,1,0:T(4,128)S(1)}, f32[32,3,128]{2,1,0:T(4,128)S(1)}, u32[]{:S(2)}, u32[]{:S(2)}) collective-permute-start(f32[32,3,128]{2,1,0:T(4,128)S(1)} %maximum_select_fusion.4), channel_id=1, source_target_pairs={{0,4},{1,5},{2,6},{3,7},{4,0},{5,1},{6,2},{7,3},{8,12},{9,13},{10,... | collective-permute-start | bytes 147464 | tf_op jit(solution)/shard_map/ppermute | solution.py:196

commit v3 on v2

--- a/solution.py
+++ b/solution.py
@@ -213,9 +213,11 @@
     extra = -(-(box - 1) // part)
     window = part * (1 + extra)
     plane_step = 8
-    row_step = 8
-
-    full_box = gather_pieces(ligand_box, "slab", 3)
+    row_step = 16
+
+    lead = ligand_box.shape[:4]
+    dense = ligand_box.reshape(lead + (box * box,))
+    full_box = gather_pieces(dense, "slab", 3)
     full_box, outgoing = lax.optimization_barrier((full_box, receptor))
     blocks = [receptor]
     for hop in range(1, extra + 1):

time: 139 us -> 121 us (0.87)
  waiting for transfers between devices: 29.7 us -> 12 us
  local copies, waits for them, and re-layouts: 4.71 us -> 7.21 us
  other arithmetic: 15.1 us -> 12.7 us
    ppermute x5, waiting for transfers between devices: 24.2 us -> 6.6 us  [gather_pieces(): other = lax.ppermute(held, axis_name, perm=pairs)]
    select_n x5, other arithmetic: 2.88 us -> 0.12 us  [gather_pieces(): jnp.where(low_half, jnp.concatenate([held, other], axis=dim), jnp.concate...]
  transfers between devices with their start and end apart: 6 -> 6, of which waited for: 3 -> 3; matrix products, arithmetic and copies ran while one was open for 17% -> 18% of each run, Pallas kernels for 14% -> 17%
where the time goes in v3:
time: 121 us; the launch traced here: 119 us
  Pallas kernels  74.3 us (61%)
  other arithmetic  12.7 us (10%)
  waiting for transfers between devices  12 us (10%)
  starting transfers between devices  9.47 us (8%)
  local copies, waits for them, and re-layouts  7.21 us (6%)
  matrix products  2.4 us (2%)
    pallas_call x1, Pallas kernels, cross_spectra(): pl.pallas_call(kernel, grid=(size // row_step,), in_specs=[pl.BlockSpec((...  33.3 us
    pallas_call x3, Pallas kernels, forward_planes(): pl.pallas_call(forward_plane_kernel, grid=(planes // plane_step,), in_spe...  29.3 us
    pallas_call x1, Pallas kernels, inverse_planes(): pl.pallas_call(inverse_plane_kernel, grid=(sets, planes // plane_step), i...  11.8 us
    ppermute x5, starting transfers between devices, gather_pieces(): other = lax.ppermute(held, axis_name, perm=pairs)  8.9 us
    ppermute x5, waiting for transfers between devices, gather_pieces(): other = lax.ppermute(held, axis_name, perm=pairs)  6.6 us
    ppermute x1, waiting for transfers between devices, score_grids(): blocks.append(lax.ppermute(outgoing, 'slab', perm=pairs))  5.41 us
    concatenate x5, other arithmetic, block2(): return jnp.concatenate([top, bottom], axis=0)  3.68 us
  transfers between devices with their start and end apart: 6, of which 3 were waited for; matrix products, arithmetic and copies ran while one was open for 18% of the time, Pallas kernels for 17%

profile of v3, /device:TPU:0, one launch (start us, length us, event | category | flops | bytes accessed | tf_op | source)
XLA Modules:
  0.0 119.0 jit_solution(9922384177129717771)
XLA Ops:
  0.7 1.3 %reshape.287 = f32[2,1,2,8,1024]{4,3,2,0,1:T(8,128)S(1)} reshape(f32[2,1,2,8,32,32]{5,4,3,2,1,0:T(8,128)} %param.11) | data formatting | bytes 262144 | tf_op jit(solution)/shard_map/reshape | solution.py:219
  2.5 0.7 copy.81
  3.2 2.5 %collective-permute-start.3 = (f32[8,3,128]{2,1,0:T(4,128)S(1)}, f32[8,3,128]{2,1,0:T(4,128)S(1)}, u32[]{:S(2)}, u32[]{:S(2)}) collective-permute-start(f32[8,3,128]{2,1,0:T(4,128)S(1)} %copy.81), channel_id=1, source_target_pairs={{0,1},{1,0},{2,3},{3,2},{4,5},{5,4},{6,7},{7,6},{8,9},{9,8},{10,11... | collective-permute-start | bytes 36872 | tf_op jit(solution)/shard_map/ppermute | solution.py:196
  8.6 0.7 maximum_maximum_fusion.4.refs_5_
  9.3 1.6 %collective-permute-start.1 = (f32[2,1,2,16,1024]{4,3,0,2,1:T(8,128)S(1)}, f32[2,1,2,16,1024]{4,3,0,2,1:T(8,128)S(1)}, u32[]{:S(2)}, u32[]{:S(2)}) collective-permute-start(f32[2,1,2,16,1024]{4,3,0,2,1:T(8,128)S(1)} %maximum_select_fusion.2), channel_id=1, source_target_pairs={{0,16},{8,24},{16,0},{24,8},{1,17},{9,25},{17,1},{25,9},{2,18},{10... | collective-permute-start | bytes 786440 | tf_op jit(solution)/shard_map/ppermute | solution.py:196
  11.6 1.3 %concatenate.186 = f32[2,2,8,1024]{3,2,1,0:T(8,128)S(1)} reshape(f32[2,1,2,8,32,32]{5,4,3,2,1,0:T(8,128)} %param.11) | data formatting | bytes 262144 | tf_op jit(solution)/shard_map/concatenate | solution.py:200
  12.9 4.9 %collective-permute-done.1 = f32[2,1,2,16,1024]{4,3,0,2,1:T(8,128)S(1)} collective-permute-done((f32[2,1,2,16,1024]{4,3,0,2,1:T(8,128)S(1)}, f32[2,1,2,16,1024]{4,3,0,2,1:T(8,128)S(1)}, u32[]{:S(2)}, u32[]{:S(2)}) %collective-permute-start.1) | collective-permute-done | bytes 262176 | tf_op jit(solution)/shard_map/ppermute | solution.py:196
  18.5 0.7 gather_fusion
  20.6 0.8 maximum_maximum_fusion.ly_ref
  21.5 0.8 maximum_maximum_fusion.2
  22.2 0.8 fusion.3
  24.3 1.6 %collective-permute-start.4 = (f32[16,3,128]{2,1,0:T(4,128)S(1)}, f32[16,3,128]{2,1,0:T(4,128)S(1)}, u32[]{:S(2)}, u32[]{:S(2)}) collective-permute-start(f32[16,3,128]{2,1,0:T(4,128)S(1)} %maximum_select_fusion.5), channel_id=1, source_target_pairs={{0,2},{1,3},{2,0},{3,1},{4,6},{5,7},{6,4},{7,5},{8,10},{9,11},{10,... | collective-permute-start | bytes 73736 | tf_op jit(solution)/shard_map/ppermute | solution.py:196
  26.6 1.7 %collective-permute-done.4 = f32[16,3,128]{2,1,0:T(4,128)S(1)} collective-permute-done((f32[16,3,128]{2,1,0:T(4,128)S(1)}, f32[16,3,128]{2,1,0:T(4,128)S(1)}, u32[]{:S(2)}, u32[]{:S(2)}) %collective-permute-start.4) | collective-permute-done | bytes 24608 | tf_op jit(solution)/shard_map/ppermute | solution.py:196
  28.3 2.7 %collective-permute-start.5 = (f32[32,3,128]{2,1,0:T(4,128)S(1)}, f32[32,3,128]{2,1,0:T(4,128)S(1)}, u32[]{:S(2)}, u32[]{:S(2)}) collective-permute-start(f32[32,3,128]{2,1,0:T(4,128)S(1)} %maximum_select_fusion.4), channel_id=1, source_target_pairs={{0,4},{1,5},{2,6},{3,7},{4,0},{5,1},{6,2},{7,3},{8,12},{9,13},{10,... | collective-permute-start | bytes 147464 | tf_op jit(solution)/shard_map/ppermute | solution.py:196
  31.0 9.4 %shard_map.113.refs_0_ = f32[2,32,128,128]{3,2,1,0:T(8,128)} custom-call(f32[2,32,128,128]{3,2,1,0:T(8,128)} %in_ref.1, f32[256,256]{1,0:T(8,128)} %get-tuple-element.21.rz_ref.ly_ref, f32[256,256]{1,0:T(8,128)} %get-tuple-element.20.ly_ref), custom_call_target="tpu_custom_call" | custom-call | tf_op jit(solution)/shard_map/pallas_call | solution.py:95
  40.4 1.0 gather_fusion.1
  42.4 1.9 %fusion = f32[256,3,3]{2,1,0:T(4,128)S(1)} fusion(f32[256,3,128]{2,1,0:T(4,128)S(1)} %copy.85, f32[256,3,128]{2,1,0:T(4,128)S(1)} %gather_fusion.1, f32[256,3]{1,0:T(8,128)S(1)} %broadcast_multiply_fusion), kind=kOutput, calls=%fused_computation.5 | convolution fusion | flops 3637248 | bytes 798720 | tf_op jit(solution)/shard_map/pja,pka->pjk/dot_general | solution.py:288
  45.0 1.4 %slice_multiply_fusion.1 = (f32[2,1,1,32,1024]{4,3,0,2,1:T(8,128)S(1)}, f32[2,1,1,32,1024]{4,3,0,2,1:T(8,128)S(1)}) fusion(f32[2,1,2,32,1024]{4,3,0,2,1:T(8,128)S(1)} %maximum_select_fusion, f32[]{:T(128)} %bitcast.2, f32[]{:T(128)} %bitcast.3), kind=kLoop, calls=%fused_computation.19 | loop fusion | flops 131072 | bytes 1048584 | tf_op jit(solution)/shard_map/mul | solution.py:233
  47.1 1.6 %pad_maximum_fusion.in_ref = f32[2,64,32,32]{3,2,1,0:T(8,128)} fusion(f32[1,64,32,32]{3,2,1,0:T(8,128)S(1)} %mul.227, f32[1,64,32,32]{3,2,1,0:T(8,128)S(1)} %mul.224), kind=kLoop, calls=%fused_computation.2 | loop fusion | flops 131072 | bytes 1048576 | tf_op jit(solution)/shard_map/stack | solution.py:232
  48.7 10.6 %shard_map.115.refs_2_ = f32[2,64,128,128]{3,2,1,0:T(8,128)} custom-call(f32[2,64,32,32]{3,2,1,0:T(8,128)} %pad_maximum_fusion.in_ref, f32[64,256]{1,0:T(8,128)} %maximum_maximum_fusion.1.rz_ref, f32[256,64]{1,0:T(8,128)} %maximum_maximum_fusion.ly_ref), custom_call_target="tpu_custom_call" | custom-call | tf_op jit(solution)/shard_map/pallas_call | solution.py:95
  59.3 5.4 %collective-permute-done.2.in_ref = f32[2,32,128,128]{3,2,1,0:T(8,128)} collective-permute-done((f32[2,32,128,128]{3,2,1,0:T(8,128)}, f32[2,32,128,128]{3,2,1,0:T(8,128)}, u32[]{:S(2)}, u32[]{:S(2)}) %collective-permute-start.2) | collective-permute-done | bytes 4194336 | tf_op jit(solution)/shard_map/ppermute | solution.py:225
  64.7 9.2 %shard_map.114.refs_1_ = f32[2,32,128,128]{3,2,1,0:T(8,128)} custom-call(f32[2,32,128,128]{3,2,1,0:T(8,128)} %collective-permute-done.2.in_ref, f32[256,256]{1,0:T(8,128)} %get-tuple-element.21.rz_ref.ly_ref, f32[256,256]{1,0:T(8,128)} %get-tuple-element.20.ly_ref), custom_call_target="tpu_custom_call" | custom-call | tf_op jit(solution)/shard_map/pallas_call | solution.py:95
  74.0 33.3 %shard_map.116.in_ref = f32[2,2,32,128,128]{4,3,2,1,0:T(8,128)} custom-call(f32[2,32,128,128]{3,2,1,0:T(8,128)} %shard_map.113.refs_0_, f32[2,32,128,128]{3,2,1,0:T(8,128)} %shard_map.114.refs_1_, f32[2,64,128,128]{3,2,1,0:T(8,128)} %shard_map.115.refs_2_, f32[128,64]{1,0:T(8,128)} %get-tuple-element.39.refs_3_, f32[128,64]{1,0:T(8,128)} %get-tuple-element.40.refs_4_, ...), custom_call_target="tpu_custom_call" | custom-call | tf_op jit(solution)/shard_map/pallas_call | solution.py:147
  107.2 11.8 %shard_map.117 = f32[2,32,128,128]{3,2,1,0:T(8,128)} custom-call(f32[2,2,32,128,128]{4,3,2,1,0:T(8,128)} %shard_map.116.in_ref, f32[256,256]{1,0:T(8,128)} %get-tuple-element.21.rz_ref.ly_ref, f32[256,128]{1,0:T(8,128)} %pad_maximum_fusion.5.rz_ref), custom_call_target="tpu_custom_call" | custom-call | tf_op jit(solution)/shard_map/pallas_call | solution.py:162
  (63 shorter events, 10.5 us)
Async XLA Ops:
  0.6 22.5 %copy-start = (f32[3,128]{1,0:T(4,128)S(1)}, f32[3,128]{1,0:T(4,128)}, u32[]{:S(2)}) copy-start(f32[3,128]{1,0:T(4,128)} %param.14) | copy-start | bytes 4612
  0.6 17.8 %copy-start.1 = (f32[9,16]{1,0:T(8,128)S(1)}, f32[9,16]{1,0:T(8,128)}, u32[]{:S(2)}) copy-start(f32[9,16]{1,0:T(8,128)} %param.13) | copy-start | bytes 1732
  0.7 22.4 %copy-start.4 = (s32[256,1]{0,1:T(1,128)S(1)}, s32[256,1]{0,1:T(1,128)}, u32[]{:S(2)}) copy-start(s32[256,1]{0,1:T(1,128)} %param.18) | copy-start | bytes 3076
  0.7 25.3 %copy-start.2 = (f32[2]{0:T(128)S(1)}, f32[2]{0:T(128)}, u32[]{:S(2)}) copy-start(f32[2]{0:T(128)} %param.12) | copy-start | bytes 28
  0.7 25.9 %copy-start.3 = (s32[256]{0:T(256)S(1)}, s32[256]{0:T(256)}, u32[]{:S(2)}) copy-start(s32[256]{0:T(256)} %param.19) | copy-start | bytes 3076
  2.0 7.2 %collective-permute-start = (f32[2,1,2,8,1024]{4,3,0,2,1:T(8,128)S(1)}, f32[2,1,2,8,1024]{4,3,0,2,1:T(8,128)S(1)}, u32[]{:S(2)}, u32[]{:S(2)}) collective-permute-start(f32[2,1,2,8,1024]{4,3,0,2,1:T(8,128)S(1)} %copy.73), channel_id=1, source_target_pairs={{0,8},{8,0},{16,24},{24,16},{1,9},{9,1},{17,25},{25,17},{2,10},{10... | collective-permute-start | bytes 393224 | tf_op jit(solution)/shard_map/ppermute | solution.py:196
  3.2 21.1 %collective-permute-start.3 = (f32[8,3,128]{2,1,0:T(4,128)S(1)}, f32[8,3,128]{2,1,0:T(4,128)S(1)}, u32[]{:S(2)}, u32[]{:S(2)}) collective-permute-start(f32[8,3,128]{2,1,0:T(4,128)S(1)} %copy.81), channel_id=1, source_target_pairs={{0,1},{1,0},{2,3},{3,2},{4,5},{5,4},{6,7},{7,6},{8,9},{9,8},{10,11... | collective-permute-start | bytes 36872 | tf_op jit(solution)/shard_map/ppermute | solution.py:196
  9.3 8.5 %collective-permute-start.1 = (f32[2,1,2,16,1024]{4,3,0,2,1:T(8,128)S(1)}, f32[2,1,2,16,1024]{4,3,0,2,1:T(8,128)S(1)}, u32[]{:S(2)}, u32[]{:S(2)}) collective-permute-start(f32[2,1,2,16,1024]{4,3,0,2,1:T(8,128)S(1)} %maximum_select_fusion.2), channel_id=1, source_target_pairs={{0,16},{8,24},{16,0},{24,8},{1,17},{9,25},{17,1},{25,9},{2,18},{10... | collective-permute-start | bytes 786440 | tf_op jit(solution)/shard_map/ppermute | solution.py:196
  17.8 46.9 %collective-permute-start.2 = (f32[2,32,128,128]{3,2,1,0:T(8,128)}, f32[2,32,128,128]{3,2,1,0:T(8,128)}, u32[]{:S(2)}, u32[]{:S(2)}) collective-permute-start(f32[2,32,128,128]{3,2,1,0:T(8,128)} %in_ref.1), channel_id=1, source_target_pairs={{0,24},{8,0},{16,8},{24,16},{1,25},{9,1},{17,9},{25,17},{2,26},{10... | collective-permute-start | bytes 12582920 | tf_op jit(solution)/shard_map/ppermute | solution.py:225
  24.3 4.0 %collective-permute-start.4 = (f32[16,3,128]{2,1,0:T(4,128)S(1)}, f32[16,3,128]{2,1,0:T(4,128)S(1)}, u32[]{:S(2)}, u32[]{:S(2)}) collective-permute-start(f32[16,3,128]{2,1,0:T(4,128)S(1)} %maximum_select_fusion.5), channel_id=1, source_target_pairs={{0,2},{1,3},{2,0},{3,1},{4,6},{5,7},{6,4},{7,5},{8,10},{9,11},{10,... | collective-permute-start | bytes 73736 | tf_op jit(solution)/shard_map/ppermute | solution.py:196
  28.3 12.1 %collective-permute-start.5 = (f32[32,3,128]{2,1,0:T(4,128)S(1)}, f32[32,3,128]{2,1,0:T(4,128)S(1)}, u32[]{:S(2)}, u32[]{:S(2)}) collective-permute-start(f32[32,3,128]{2,1,0:T(4,128)S(1)} %maximum_select_fusion.4), channel_id=1, source_target_pairs={{0,4},{1,5},{2,6},{3,7},{4,0},{5,1},{6,2},{7,3},{8,12},{9,13},{10,... | collective-permute-start | bytes 147464 | tf_op jit(solution)/shard_map/ppermute | solution.py:196

commit v4 on v3

--- a/solution.py
+++ b/solution.py
@@ -104,35 +104,44 @@
 def cross_kernel(*refs, blocks, sets, box, window, part):
     rec_refs = refs[:blocks]
     lig_ref = refs[blocks]
-    g_tables = [hi_lo(t[...]) for t in refs[blocks + 1 : 2 * blocks + 1]]
-    gl_hi, gl_lo = hi_lo(refs[2 * blocks + 1][...])
-    h_hi, h_lo = hi_lo(refs[2 * blocks + 2][...])
+    g_hi, g_lo = hi_lo(refs[blocks + 1][...])
+    gl_hi, gl_lo = hi_lo(refs[blocks + 2][...])
+    h_hi, h_lo = hi_lo(refs[blocks + 3][...])
     out_ref = refs[-1]
     rows = out_ref.shape[3]
     lanes = out_ref.shape[4]
 
     def gathered(ref, lo, count):
+        turned = [jnp.swapaxes(ref[c, lo : lo + count], 0, 1) for c in range(2)]
         return jnp.concatenate(
-            [ref[:, lo : lo + count, r, :].reshape(2 * count, lanes) for r in range(rows)], axis=1
+            [jnp.concatenate([turned[0][r], turned[1][r]], axis=0) for r in range(rows)], axis=1
         )
 
-    rec = None
-    for b in range(blocks):
-        term = split_dot(gathered(rec_refs[b], 0, part), g_tables[b][0], g_tables[b][1], False)
-        rec = term if rec is None else rec + term
+    rec_in = jnp.concatenate([gathered(rec_refs[b], 0, part) for b in range(blocks)], axis=0)
+    rec = split_dot(rec_in, g_hi, g_lo, False)
+    rec = jnp.concatenate([rec] * sets, axis=1)
+    lig_in = jnp.concatenate([gathered(lig_ref, s * box, box) for s in range(sets)], axis=1)
+    lig = split_dot(lig_in, gl_hi, gl_lo, False)
     rec_real = rec[:window]
     rec_imag = rec[window:]
+    lig_real = lig[:window]
+    lig_imag = lig[window:]
+    prod = jnp.concatenate(
+        [rec_real * lig_real + rec_imag * lig_imag, rec_imag * lig_real - rec_real * lig_imag],
+        axis=0,
+    )
+    back = split_dot(prod, h_hi, h_lo, False)
+    width = rows * lanes
     for s in range(sets):
-        lig = split_dot(gathered(lig_ref, s * box, box), gl_hi, gl_lo, False)
-        lig_real = lig[:window]
-        lig_imag = lig[window:]
-        prod = jnp.concatenate(
-            [rec_real * lig_real + rec_imag * lig_imag, rec_imag * lig_real - rec_real * lig_imag],
-            axis=0,
-        )
-        back = split_dot(prod, h_hi, h_lo, False)
-        for r in range(rows):
-            out_ref[s, :, :, r, :] = back[:, r * lanes : (r + 1) * lanes].reshape(2, part, lanes)
+        for c in range(2):
+            pieces = jnp.stack(
+                [
+                    back[c * part : (c + 1) * part, s * width + r * lanes : s * width + (r + 1) * lanes]
+                    for r in range(rows)
+                ],
+                axis=0,
+            )
+            out_ref[s, c] = jnp.swapaxes(pieces, 0, 1)
 
 
 def cross_spectra(rec_blocks, lig_yz, g_tables, gl, hx, sets, box, window, row_step):
@@ -140,7 +149,7 @@
     size = rec_blocks[0].shape[2]
     lanes = rec_blocks[0].shape[3]
     blocks = len(rec_blocks)
-    tables = list(g_tables) + [gl, hx]
+    tables = [jnp.concatenate(g_tables, axis=1), gl, hx]
     kernel = functools.partial(
         cross_kernel, blocks=blocks, sets=sets, box=box, window=window, part=part
     )

time: 121 us -> 108 us (0.89)
  Pallas kernels: 74.3 us -> 62.6 us
    pallas_call x1, Pallas kernels: 33.3 us -> 21.5 us  [cross_spectra(): pl.pallas_call(kernel, grid=(size // row_step,), in_specs=[pl.BlockSpec((...]
    concatenate x5 -> x4, other arithmetic: 3.68 us -> 2.93 us  [block2(): return jnp.concatenate([top, bottom], axis=0)]
  transfers between devices with their start and end apart: 6 -> 6, of which waited for: 3 -> 3; matrix products, arithmetic and copies ran while one was open for 18% -> 20% of each run, Pallas kernels for 17% -> 19%
where the time goes in v4:
time: 108 us; the launch traced here: 106 us
  Pallas kernels  62.6 us (58%)
  other arithmetic  12.6 us (12%)
  waiting for transfers between devices  10.9 us (10%)
  starting transfers between devices  9.48 us (9%)
  local copies, waits for them, and re-layouts  7.1 us (7%)
  matrix products  2.39 us (2%)
    pallas_call x3, Pallas kernels, forward_planes(): pl.pallas_call(forward_plane_kernel, grid=(planes // plane_step,), in_spe...  29.3 us
    pallas_call x1, Pallas kernels, cross_spectra(): pl.pallas_call(kernel, grid=(size // row_step,), in_specs=[pl.BlockSpec((...  21.5 us
    pallas_call x1, Pallas kernels, inverse_planes(): pl.pallas_call(inverse_plane_kernel, grid=(sets, planes // plane_step), i...  11.8 us
    ppermute x5, starting transfers between devices, gather_pieces(): other = lax.ppermute(held, axis_name, perm=pairs)  8.91 us
    ppermute x5, waiting for transfers between devices, gather_pieces(): other = lax.ppermute(held, axis_name, perm=pairs)  6.63 us
    ppermute x1, waiting for transfers between devices, score_grids(): blocks.append(lax.ppermute(outgoing, 'slab', perm=pairs))  4.24 us
    concatenate x4, other arithmetic, block2(): return jnp.concatenate([top, bottom], axis=0)  2.93 us
  transfers between devices with their start and end apart: 6, of which 3 were waited for; matrix products, arithmetic and copies ran while one was open for 20% of the time, Pallas kernels for 19%

profile of v4, /device:TPU:0, one launch (start us, length us, event | category | flops | bytes accessed | tf_op | source)
XLA Modules:
  0.0 105.9 jit_solution(10622698617541909386)
XLA Ops:
  0.7 1.3 %reshape.287 = f32[2,1,2,8,1024]{4,3,2,0,1:T(8,128)S(1)} reshape(f32[2,1,2,8,32,32]{5,4,3,2,1,0:T(8,128)} %param.11) | data formatting | bytes 262144 | tf_op jit(solution)/shard_map/reshape | solution.py:228
  2.5 0.7 copy.81
  3.2 2.5 %collective-permute-start.3 = (f32[8,3,128]{2,1,0:T(4,128)S(1)}, f32[8,3,128]{2,1,0:T(4,128)S(1)}, u32[]{:S(2)}, u32[]{:S(2)}) collective-permute-start(f32[8,3,128]{2,1,0:T(4,128)S(1)} %copy.81), channel_id=1, source_target_pairs={{0,1},{1,0},{2,3},{3,2},{4,5},{5,4},{6,7},{7,6},{8,9},{9,8},{10,11... | collective-permute-start | bytes 36872 | tf_op jit(solution)/shard_map/ppermute | solution.py:205
  8.0 1.6 %collective-permute-start.1 = (f32[2,1,2,16,1024]{4,3,0,2,1:T(8,128)S(1)}, f32[2,1,2,16,1024]{4,3,0,2,1:T(8,128)S(1)}, u32[]{:S(2)}, u32[]{:S(2)}) collective-permute-start(f32[2,1,2,16,1024]{4,3,0,2,1:T(8,128)S(1)} %maximum_select_fusion.2), channel_id=1, source_target_pairs={{0,16},{8,24},{16,0},{24,8},{1,17},{9,25},{17,1},{25,9},{2,18},{10... | collective-permute-start | bytes 786440 | tf_op jit(solution)/shard_map/ppermute | solution.py:205
  10.2 1.3 %concatenate.189 = f32[2,2,8,1024]{3,2,1,0:T(8,128)S(1)} reshape(f32[2,1,2,8,32,32]{5,4,3,2,1,0:T(8,128)} %param.11) | data formatting | bytes 262144 | tf_op jit(solution)/shard_map/concatenate | solution.py:209
  11.6 4.9 %collective-permute-done.1 = f32[2,1,2,16,1024]{4,3,0,2,1:T(8,128)S(1)} collective-permute-done((f32[2,1,2,16,1024]{4,3,0,2,1:T(8,128)S(1)}, f32[2,1,2,16,1024]{4,3,0,2,1:T(8,128)S(1)}, u32[]{:S(2)}, u32[]{:S(2)}) %collective-permute-start.1) | collective-permute-done | bytes 262176 | tf_op jit(solution)/shard_map/ppermute | solution.py:205
  17.2 0.7 gather_fusion
  18.7 0.7 maximum_maximum_fusion.3.refs_4_
  19.4 0.8 maximum_maximum_fusion.2.refs_3_
  21.4 0.7 maximum_maximum_fusion.ly_ref
  22.2 0.8 fusion.3
  24.3 1.6 %collective-permute-start.4 = (f32[16,3,128]{2,1,0:T(4,128)S(1)}, f32[16,3,128]{2,1,0:T(4,128)S(1)}, u32[]{:S(2)}, u32[]{:S(2)}) collective-permute-start(f32[16,3,128]{2,1,0:T(4,128)S(1)} %maximum_select_fusion.5), channel_id=1, source_target_pairs={{0,2},{1,3},{2,0},{3,1},{4,6},{5,7},{6,4},{7,5},{8,10},{9,11},{10,... | collective-permute-start | bytes 73736 | tf_op jit(solution)/shard_map/ppermute | solution.py:205
  26.5 1.7 %collective-permute-done.4 = f32[16,3,128]{2,1,0:T(4,128)S(1)} collective-permute-done((f32[16,3,128]{2,1,0:T(4,128)S(1)}, f32[16,3,128]{2,1,0:T(4,128)S(1)}, u32[]{:S(2)}, u32[]{:S(2)}) %collective-permute-start.4) | collective-permute-done | bytes 24608 | tf_op jit(solution)/shard_map/ppermute | solution.py:205
  28.3 2.7 %collective-permute-start.5 = (f32[32,3,128]{2,1,0:T(4,128)S(1)}, f32[32,3,128]{2,1,0:T(4,128)S(1)}, u32[]{:S(2)}, u32[]{:S(2)}) collective-permute-start(f32[32,3,128]{2,1,0:T(4,128)S(1)} %maximum_select_fusion.4), channel_id=1, source_target_pairs={{0,4},{1,5},{2,6},{3,7},{4,0},{5,1},{6,2},{7,3},{8,12},{9,13},{10,... | collective-permute-start | bytes 147464 | tf_op jit(solution)/shard_map/ppermute | solution.py:205
  30.9 9.4 %shard_map.113.refs_0_ = f32[2,32,128,128]{3,2,1,0:T(8,128)} custom-call(f32[2,32,128,128]{3,2,1,0:T(8,128)} %in_ref.1, f32[256,256]{1,0:T(8,128)} %get-tuple-element.21.rz_ref.ly_ref, f32[256,256]{1,0:T(8,128)} %get-tuple-element.20.ly_ref), custom_call_target="tpu_custom_call" | custom-call | tf_op jit(solution)/shard_map/pallas_call | solution.py:95
  40.4 1.0 gather_fusion.1
  42.3 1.9 %fusion = f32[256,3,3]{2,1,0:T(4,128)S(1)} fusion(f32[256,3,128]{2,1,0:T(4,128)S(1)} %copy.85, f32[256,3,128]{2,1,0:T(4,128)S(1)} %gather_fusion.1, f32[256,3]{1,0:T(8,128)S(1)} %broadcast_multiply_fusion), kind=kOutput, calls=%fused_computation.5 | convolution fusion | flops 3637248 | bytes 798720 | tf_op jit(solution)/shard_map/pja,pka->pjk/dot_general | solution.py:297
  45.0 1.3 %slice_multiply_fusion.1 = (f32[2,1,1,32,1024]{4,3,0,2,1:T(8,128)S(1)}, f32[2,1,1,32,1024]{4,3,0,2,1:T(8,128)S(1)}) fusion(f32[2,1,2,32,1024]{4,3,0,2,1:T(8,128)S(1)} %maximum_select_fusion, f32[]{:T(128)} %bitcast.2, f32[]{:T(128)} %bitcast.3), kind=kLoop, calls=%fused_computation.19 | loop fusion | flops 131072 | bytes 1048584 | tf_op jit(solution)/shard_map/mul | solution.py:242
  47.0 1.6 %pad_maximum_fusion.in_ref = f32[2,64,32,32]{3,2,1,0:T(8,128)} fusion(f32[1,64,32,32]{3,2,1,0:T(8,128)S(1)} %mul.227, f32[1,64,32,32]{3,2,1,0:T(8,128)S(1)} %mul.224), kind=kLoop, calls=%fused_computation.2 | loop fusion | flops 131072 | bytes 1048576 | tf_op jit(solution)/shard_map/stack | solution.py:241
  48.5 10.7 %shard_map.115.refs_2_ = f32[2,64,128,128]{3,2,1,0:T(8,128)} custom-call(f32[2,64,32,32]{3,2,1,0:T(8,128)} %pad_maximum_fusion.in_ref, f32[64,256]{1,0:T(8,128)} %maximum_maximum_fusion.1.rz_ref, f32[256,64]{1,0:T(8,128)} %maximum_maximum_fusion.ly_ref), custom_call_target="tpu_custom_call" | custom-call | tf_op jit(solution)/shard_map/pallas_call | solution.py:95
  59.2 4.2 %collective-permute-done.2.in_ref = f32[2,32,128,128]{3,2,1,0:T(8,128)} collective-permute-done((f32[2,32,128,128]{3,2,1,0:T(8,128)}, f32[2,32,128,128]{3,2,1,0:T(8,128)}, u32[]{:S(2)}, u32[]{:S(2)}) %collective-permute-start.2) | collective-permute-done | bytes 4194336 | tf_op jit(solution)/shard_map/ppermute | solution.py:234
  63.4 9.2 %shard_map.114.refs_1_ = f32[2,32,128,128]{3,2,1,0:T(8,128)} custom-call(f32[2,32,128,128]{3,2,1,0:T(8,128)} %collective-permute-done.2.in_ref, f32[256,256]{1,0:T(8,128)} %get-tuple-element.21.rz_ref.ly_ref, f32[256,256]{1,0:T(8,128)} %get-tuple-element.20.ly_ref), custom_call_target="tpu_custom_call" | custom-call | tf_op jit(solution)/shard_map/pallas_call | solution.py:95
  72.7 21.5 %shard_map.116.in_ref = f32[2,2,32,128,128]{4,3,2,1,0:T(8,128)} custom-call(f32[2,32,128,128]{3,2,1,0:T(8,128)} %shard_map.113.refs_0_, f32[2,32,128,128]{3,2,1,0:T(8,128)} %shard_map.114.refs_1_, f32[2,64,128,128]{3,2,1,0:T(8,128)} %shard_map.115.refs_2_, f32[128,128]{1,0:T(8,128)} %maximum_maximum_fusion.2.refs_3_, ...), custom_call_target="tpu_custom_call" | custom-call | tf_op jit(solution)/shard_map/pallas_call | solution.py:156
  94.2 11.8 %shard_map.117 = f32[2,32,128,128]{3,2,1,0:T(8,128)} custom-call(f32[2,2,32,128,128]{4,3,2,1,0:T(8,128)} %shard_map.116.in_ref, f32[256,256]{1,0:T(8,128)} %get-tuple-element.21.rz_ref.ly_ref, f32[256,128]{1,0:T(8,128)} %pad_maximum_fusion.5.rz_ref), custom_call_target="tpu_custom_call" | custom-call | tf_op jit(solution)/shard_map/pallas_call | solution.py:171
  (62 shorter events, 10.4 us)
Async XLA Ops:
  0.6 22.4 %copy-start = (f32[3,128]{1,0:T(4,128)S(1)}, f32[3,128]{1,0:T(4,128)}, u32[]{:S(2)}) copy-start(f32[3,128]{1,0:T(4,128)} %param.14) | copy-start | bytes 4612
  0.6 16.5 %copy-start.1 = (f32[9,16]{1,0:T(8,128)S(1)}, f32[9,16]{1,0:T(8,128)}, u32[]{:S(2)}) copy-start(f32[9,16]{1,0:T(8,128)} %param.13) | copy-start | bytes 1732
  0.7 22.4 %copy-start.4 = (s32[256,1]{0,1:T(1,128)S(1)}, s32[256,1]{0,1:T(1,128)}, u32[]{:S(2)}) copy-start(s32[256,1]{0,1:T(1,128)} %param.18) | copy-start | bytes 3076
  0.7 25.3 %copy-start.2 = (f32[2]{0:T(128)S(1)}, f32[2]{0:T(128)}, u32[]{:S(2)}) copy-start(f32[2]{0:T(128)} %param.12) | copy-start | bytes 28
  0.7 25.9 %copy-start.3 = (s32[256]{0:T(256)S(1)}, s32[256]{0:T(256)}, u32[]{:S(2)}) copy-start(s32[256]{0:T(256)} %param.19) | copy-start | bytes 3076
  2.0 5.9 %collective-permute-start = (f32[2,1,2,8,1024]{4,3,0,2,1:T(8,128)S(1)}, f32[2,1,2,8,1024]{4,3,0,2,1:T(8,128)S(1)}, u32[]{:S(2)}, u32[]{:S(2)}) collective-permute-start(f32[2,1,2,8,1024]{4,3,0,2,1:T(8,128)S(1)} %copy.73), channel_id=1, source_target_pairs={{0,8},{8,0},{16,24},{24,16},{1,9},{9,1},{17,25},{25,17},{2,10},{10... | collective-permute-start | bytes 393224 | tf_op jit(solution)/shard_map/ppermute | solution.py:205
  3.2 21.0 %collective-permute-start.3 = (f32[8,3,128]{2,1,0:T(4,128)S(1)}, f32[8,3,128]{2,1,0:T(4,128)S(1)}, u32[]{:S(2)}, u32[]{:S(2)}) collective-permute-start(f32[8,3,128]{2,1,0:T(4,128)S(1)} %copy.81), channel_id=1, source_target_pairs={{0,1},{1,0},{2,3},{3,2},{4,5},{5,4},{6,7},{7,6},{8,9},{9,8},{10,11... | collective-permute-start | bytes 36872 | tf_op jit(solution)/shard_map/ppermute | solution.py:205
  8.0 8.5 %collective-permute-start.1 = (f32[2,1,2,16,1024]{4,3,0,2,1:T(8,128)S(1)}, f32[2,1,2,16,1024]{4,3,0,2,1:T(8,128)S(1)}, u32[]{:S(2)}, u32[]{:S(2)}) collective-permute-start(f32[2,1,2,16,1024]{4,3,0,2,1:T(8,128)S(1)} %maximum_select_fusion.2), channel_id=1, source_target_pairs={{0,16},{8,24},{16,0},{24,8},{1,17},{9,25},{17,1},{25,9},{2,18},{10... | collective-permute-start | bytes 786440 | tf_op jit(solution)/shard_map/ppermute | solution.py:205
  16.5 46.9 %collective-permute-start.2 = (f32[2,32,128,128]{3,2,1,0:T(8,128)}, f32[2,32,128,128]{3,2,1,0:T(8,128)}, u32[]{:S(2)}, u32[]{:S(2)}) collective-permute-start(f32[2,32,128,128]{3,2,1,0:T(8,128)} %in_ref.1), channel_id=1, source_target_pairs={{0,24},{8,0},{16,8},{24,16},{1,25},{9,1},{17,9},{25,17},{2,26},{10... | collective-permute-start | bytes 12582920 | tf_op jit(solution)/shard_map/ppermute | solution.py:234
  24.3 4.0 %collective-permute-start.4 = (f32[16,3,128]{2,1,0:T(4,128)S(1)}, f32[16,3,128]{2,1,0:T(4,128)S(1)}, u32[]{:S(2)}, u32[]{:S(2)}) collective-permute-start(f32[16,3,128]{2,1,0:T(4,128)S(1)} %maximum_select_fusion.5), channel_id=1, source_target_pairs={{0,2},{1,3},{2,0},{3,1},{4,6},{5,7},{6,4},{7,5},{8,10},{9,11},{10,... | collective-permute-start | bytes 73736 | tf_op jit(solution)/shard_map/ppermute | solution.py:205
  28.3 12.1 %collective-permute-start.5 = (f32[32,3,128]{2,1,0:T(4,128)S(1)}, f32[32,3,128]{2,1,0:T(4,128)S(1)}, u32[]{:S(2)}, u32[]{:S(2)}) collective-permute-start(f32[32,3,128]{2,1,0:T(4,128)S(1)} %maximum_select_fusion.4), channel_id=1, source_target_pairs={{0,4},{1,5},{2,6},{3,7},{4,0},{5,1},{6,2},{7,3},{8,12},{9,13},{10,... | collective-permute-start | bytes 147464 | tf_op jit(solution)/shard_map/ppermute | solution.py:205

commit v5 on v4

--- a/solution.py
+++ b/solution.py
@@ -117,7 +117,9 @@
             [jnp.concatenate([turned[0][r], turned[1][r]], axis=0) for r in range(rows)], axis=1
         )
 
-    rec_in = jnp.concatenate([gathered(rec_refs[b], 0, part) for b in range(blocks)], axis=0)
+    rec_in = jnp.concatenate(
+        [gathered(rec_refs[b], 0, rec_refs[b].shape[1]) for b in range(blocks)], axis=0
+    )
     rec = split_dot(rec_in, g_hi, g_lo, False)
     rec = jnp.concatenate([rec] * sets, axis=1)
     lig_in = jnp.concatenate([gathered(lig_ref, s * box, box) for s in range(sets)], axis=1)
@@ -156,7 +158,7 @@
     return pl.pallas_call(
         kernel,
         grid=(size // row_step,),
-        in_specs=[pl.BlockSpec((2, part, row_step, lanes), lambda i: (0, 0, i, 0))] * blocks
+        in_specs=[pl.BlockSpec((2, b.shape[1], row_step, lanes), lambda i: (0, 0, i, 0)) for b in rec_blocks]
         + [pl.BlockSpec((2, sets * box, row_step, lanes), lambda i: (0, 0, i, 0))]
         + [pl.BlockSpec(t.shape, lambda i: (0, 0)) for t in tables],
         out_specs=pl.BlockSpec((sets, 2, part, row_step, lanes), lambda i: (0, 0, 0, i, 0)),
@@ -227,11 +229,14 @@
     lead = ligand_box.shape[:4]
     dense = ligand_box.reshape(lead + (box * box,))
     full_box = gather_pieces(dense, "slab", 3)
-    full_box, outgoing = lax.optimization_barrier((full_box, receptor))
+    chunks = 1
+    chunk = part // chunks
     blocks = [receptor]
     for hop in range(1, extra + 1):
         pairs = [(i, (i - hop) % slab_count) for i in range(slab_count)]
-        blocks.append(lax.ppermute(outgoing, "slab", perm=pairs))
+        for piece in range(chunks):
+            sent = receptor[:, piece * chunk : (piece + 1) * chunk]
+            blocks.append(lax.ppermute(sent, "slab", perm=pairs))
 
     cos_n, sin_n = phase_tables(size, size, size)
     rz = block2(cos_n, -sin_n, sin_n, cos_n)
@@ -248,8 +253,10 @@
 
     cos_w, sin_w = phase_tables(window, window, window)
     g_tables = []
-    for index in range(len(blocks)):
-        cols = slice(index * part, (index + 1) * part)
+    first = 0
+    for planes in blocks:
+        cols = slice(first, first + planes.shape[1])
+        first += planes.shape[1]
         g_tables.append(block2(cos_w[:, cols], sin_w[:, cols], -sin_w[:, cols], cos_w[:, cols]))
     cos_xb, sin_xb = phase_tables(window, box, window)
     gl = block2(cos_xb, sin_xb, -sin_xb, cos_xb)

time: 108 us -> 115 us (1.065); the launches traced: 106 us -> 114 us
  waiting for transfers between devices: 10.9 us -> 18.8 us
    ppermute x5, waiting for transfers between devices: 6.63 us -> 18.8 us  [gather_pieces(): other = lax.ppermute(held, axis_name, perm=pairs)]
    ppermute x1, waiting for transfers between devices: 4.24 us -> 0.01 us  [score_grids(): blocks.append(lax.ppermute(sent, 'slab', perm=pairs))]
    ppermute x1, starting transfers between devices: 0.57 us -> 2.63 us  [score_grids(): blocks.append(lax.ppermute(sent, 'slab', perm=pairs))]
    ppermute x5, starting transfers between devices: 8.91 us -> 6.87 us  [gather_pieces(): other = lax.ppermute(held, axis_name, perm=pairs)]
  transfers between devices with their start and end apart: 6 -> 6, of which waited for: 3 -> 2; matrix products, arithmetic and copies ran while one was open for 20% -> 18% of each run, Pallas kernels for 19% -> 18%
where the time goes in v5:
time: 115 us; the launch traced here: 114 us
  Pallas kernels  62.6 us (54%)
  waiting for transfers between devices  18.8 us (16%)
  other arithmetic  13.3 us (12%)
  starting transfers between devices  9.5 us (8%)
  local copies, waits for them, and re-layouts  6.75 us (6%)
  matrix products  2.39 us (2%)
    pallas_call x3, Pallas kernels, forward_planes(): pl.pallas_call(forward_plane_kernel, grid=(planes // plane_step,), in_spe...  29.3 us
    pallas_call x1, Pallas kernels, cross_spectra(): pl.pallas_call(kernel, grid=(size // row_step,), in_specs=[pl.BlockSpec((...  21.5 us
    ppermute x5, waiting for transfers between devices, gather_pieces(): other = lax.ppermute(held, axis_name, perm=pairs)  18.8 us
    pallas_call x1, Pallas kernels, inverse_planes(): pl.pallas_call(inverse_plane_kernel, grid=(sets, planes // plane_step), i...  11.8 us
    ppermute x5, starting transfers between devices, gather_pieces(): other = lax.ppermute(held, axis_name, perm=pairs)  6.87 us
    concatenate x4, other arithmetic, block2(): return jnp.concatenate([top, bottom], axis=0)  2.93 us
    ppermute x1, starting transfers between devices, score_grids(): blocks.append(lax.ppermute(sent, 'slab', perm=pairs))  2.63 us
  transfers between devices with their start and end apart: 6, of which 2 were waited for; matrix products, arithmetic and copies ran while one was open for 18% of the time, Pallas kernels for 18%

profile of v5, /device:TPU:0, one launch (start us, length us, event | category | flops | bytes accessed | tf_op | source)
XLA Modules:
  0.0 114.2 jit_solution(9010046677310602721)
XLA Ops:
  0.7 1.3 %reshape.287 = f32[2,1,2,8,1024]{4,3,2,0,1:T(8,128)S(1)} reshape(f32[2,1,2,8,32,32]{5,4,3,2,1,0:T(8,128)} %param.11) | data formatting | bytes 262144 | tf_op jit(solution)/shard_map/reshape | solution.py:230
  2.5 2.6 %collective-permute-start = (f32[2,32,128,128]{3,2,1,0:T(8,128)}, f32[2,32,128,128]{3,2,1,0:T(8,128)}, u32[]{:S(2)}, u32[]{:S(2)}) collective-permute-start(f32[2,32,128,128]{3,2,1,0:T(8,128)} %in_ref.1), channel_id=1, source_target_pairs={{0,24},{8,0},{16,8},{24,16},{1,25},{9,1},{17,9},{25,17},{2,26},{10... | collective-permute-start | bytes 12582920 | tf_op jit(solution)/shard_map/ppermute | solution.py:239
  5.2 0.7 copy.81
  5.9 1.5 %collective-permute-start.3 = (f32[8,3,128]{2,1,0:T(4,128)S(1)}, f32[8,3,128]{2,1,0:T(4,128)S(1)}, u32[]{:S(2)}, u32[]{:S(2)}) collective-permute-start(f32[8,3,128]{2,1,0:T(4,128)S(1)} %copy.81), channel_id=1, source_target_pairs={{0,1},{1,0},{2,3},{3,2},{4,5},{5,4},{6,7},{7,6},{8,9},{9,8},{10,11... | collective-permute-start | bytes 36872 | tf_op jit(solution)/shard_map/ppermute | solution.py:207
  8.8 0.7 and_select_fusion.3
  11.0 0.7 maximum_maximum_fusion.3.refs_4_
  11.7 0.8 maximum_maximum_fusion.2.refs_3_
  12.4 0.8 copy.78
  13.2 0.7 gather_fusion
  15.3 0.7 maximum_maximum_fusion.ly_ref
  16.0 0.8 fusion.3
  18.8 1.6 %collective-permute-start.4 = (f32[16,3,128]{2,1,0:T(4,128)S(1)}, f32[16,3,128]{2,1,0:T(4,128)S(1)}, u32[]{:S(2)}, u32[]{:S(2)}) collective-permute-start(f32[16,3,128]{2,1,0:T(4,128)S(1)} %maximum_select_fusion.5), channel_id=1, source_target_pairs={{0,2},{1,3},{2,0},{3,1},{4,6},{5,7},{6,4},{7,5},{8,10},{9,11},{10,... | collective-permute-start | bytes 73736 | tf_op jit(solution)/shard_map/ppermute | solution.py:207
  21.0 1.7 %collective-permute-done.4 = f32[16,3,128]{2,1,0:T(4,128)S(1)} collective-permute-done((f32[16,3,128]{2,1,0:T(4,128)S(1)}, f32[16,3,128]{2,1,0:T(4,128)S(1)}, u32[]{:S(2)}, u32[]{:S(2)}) %collective-permute-start.4) | collective-permute-done | bytes 24608 | tf_op jit(solution)/shard_map/ppermute | solution.py:207
  22.8 2.6 %collective-permute-start.5 = (f32[32,3,128]{2,1,0:T(4,128)S(1)}, f32[32,3,128]{2,1,0:T(4,128)S(1)}, u32[]{:S(2)}, u32[]{:S(2)}) collective-permute-start(f32[32,3,128]{2,1,0:T(4,128)S(1)} %maximum_select_fusion.4), channel_id=1, source_target_pairs={{0,4},{1,5},{2,6},{3,7},{4,0},{5,1},{6,2},{7,3},{8,12},{9,13},{10,... | collective-permute-start | bytes 147464 | tf_op jit(solution)/shard_map/ppermute | solution.py:207
  25.7 9.4 %shard_map.113.refs_0_ = f32[2,32,128,128]{3,2,1,0:T(8,128)} custom-call(f32[2,32,128,128]{3,2,1,0:T(8,128)} %in_ref.1, f32[256,256]{1,0:T(8,128)} %get-tuple-element.17.rz_ref.ly_ref, f32[256,256]{1,0:T(8,128)} %get-tuple-element.16.ly_ref), custom_call_target="tpu_custom_call" | custom-call | tf_op jit(solution)/shard_map/pallas_call | solution.py:95
  35.2 1.0 gather_fusion.1
  37.1 1.9 %fusion = f32[256,3,3]{2,1,0:T(4,128)S(1)} fusion(f32[256,3,128]{2,1,0:T(4,128)S(1)} %copy.85, f32[256,3,128]{2,1,0:T(4,128)S(1)} %gather_fusion.1, f32[256,3]{1,0:T(8,128)S(1)} %broadcast_multiply_fusion), kind=kOutput, calls=%fused_computation.5 | convolution fusion | flops 3637248 | bytes 798720 | tf_op jit(solution)/shard_map/pja,pka->pjk/dot_general | solution.py:304
  40.4 17.0 %collective-permute-done.2 = f32[2,1,2,16,1024]{4,3,0,2,1:T(8,128)S(1)} collective-permute-done((f32[2,1,2,16,1024]{4,3,0,2,1:T(8,128)S(1)}, f32[2,1,2,16,1024]{4,3,0,2,1:T(8,128)S(1)}, u32[]{:S(2)}, u32[]{:S(2)}) %collective-permute-start.2) | collective-permute-done | bytes 262176 | tf_op jit(solution)/shard_map/ppermute | solution.py:207
  57.5 1.3 %slice_multiply_fusion.1 = (f32[2,1,1,32,1024]{4,3,0,2,1:T(8,128)S(1)}, f32[2,1,1,32,1024]{4,3,0,2,1:T(8,128)S(1)}) fusion(f32[2,1,2,32,1024]{4,3,0,2,1:T(8,128)S(1)} %maximum_select_fusion, f32[]{:T(128)} %bitcast.2, f32[]{:T(128)} %bitcast.3), kind=kLoop, calls=%fused_computation.15 | loop fusion | flops 131072 | bytes 1048584 | tf_op jit(solution)/shard_map/mul | solution.py:247
  59.5 1.5 %pad_maximum_fusion.in_ref = f32[2,64,32,32]{3,2,1,0:T(8,128)} fusion(f32[1,64,32,32]{3,2,1,0:T(8,128)S(1)} %mul.227, f32[1,64,32,32]{3,2,1,0:T(8,128)S(1)} %mul.224), kind=kLoop, calls=%fused_computation.2 | loop fusion | flops 131072 | bytes 1048576 | tf_op jit(solution)/shard_map/stack | solution.py:246
  61.0 10.7 %shard_map.115.refs_2_ = f32[2,64,128,128]{3,2,1,0:T(8,128)} custom-call(f32[2,64,32,32]{3,2,1,0:T(8,128)} %pad_maximum_fusion.in_ref, f32[64,256]{1,0:T(8,128)} %maximum_maximum_fusion.1.rz_ref, f32[256,64]{1,0:T(8,128)} %maximum_maximum_fusion.ly_ref), custom_call_target="tpu_custom_call" | custom-call | tf_op jit(solution)/shard_map/pallas_call | solution.py:95
  71.7 9.2 %shard_map.114.refs_1_ = f32[2,32,128,128]{3,2,1,0:T(8,128)} custom-call(f32[2,32,128,128]{3,2,1,0:T(8,128)} %collective-permute-done.in_ref, f32[256,256]{1,0:T(8,128)} %get-tuple-element.17.rz_ref.ly_ref, f32[256,256]{1,0:T(8,128)} %get-tuple-element.16.ly_ref), custom_call_target="tpu_custom_call" | custom-call | tf_op jit(solution)/shard_map/pallas_call | solution.py:95
  81.0 21.5 %shard_map.116.in_ref = f32[2,2,32,128,128]{4,3,2,1,0:T(8,128)} custom-call(f32[2,32,128,128]{3,2,1,0:T(8,128)} %shard_map.113.refs_0_, f32[2,32,128,128]{3,2,1,0:T(8,128)} %shard_map.114.refs_1_, f32[2,64,128,128]{3,2,1,0:T(8,128)} %shard_map.115.refs_2_, f32[128,128]{1,0:T(8,128)} %maximum_maximum_fusion.2.refs_3_, ...), custom_call_target="tpu_custom_call" | custom-call | tf_op jit(solution)/shard_map/pallas_call | solution.py:158
  102.5 11.8 %shard_map.117 = f32[2,32,128,128]{3,2,1,0:T(8,128)} custom-call(f32[2,2,32,128,128]{4,3,2,1,0:T(8,128)} %shard_map.116.in_ref, f32[256,256]{1,0:T(8,128)} %get-tuple-element.17.rz_ref.ly_ref, f32[256,128]{1,0:T(8,128)} %pad_maximum_fusion.5.rz_ref), custom_call_target="tpu_custom_call" | custom-call | tf_op jit(solution)/shard_map/pallas_call | solution.py:173
  (60 shorter events, 10.5 us)
Async XLA Ops:
  0.6 16.9 %copy-start = (f32[3,128]{1,0:T(4,128)S(1)}, f32[3,128]{1,0:T(4,128)}, u32[]{:S(2)}) copy-start(f32[3,128]{1,0:T(4,128)} %param.14) | copy-start | bytes 4612
  0.6 24.8 %copy-start.1 = (f32[2,1,2,8,32,32]{5,4,3,2,1,0:T(8,128)S(1)}, f32[2,1,2,8,32,32]{5,4,3,2,1,0:T(8,128)}, u32[]{:S(2)}) copy-start(f32[2,1,2,8,32,32]{5,4,3,2,1,0:T(8,128)} %param.11) | copy-start | bytes 393220
  0.7 19.8 %copy-start.2 = (f32[2]{0:T(128)S(1)}, f32[2]{0:T(128)}, u32[]{:S(2)}) copy-start(f32[2]{0:T(128)} %param.12) | copy-start | bytes 28
  0.7 20.3 %copy-start.3 = (s32[256]{0:T(256)S(1)}, s32[256]{0:T(256)}, u32[]{:S(2)}) copy-start(s32[256]{0:T(256)} %param.19) | copy-start | bytes 3076
  2.0 37.2 %collective-permute-start.1 = (f32[2,1,2,8,1024]{4,3,0,2,1:T(8,128)S(1)}, f32[2,1,2,8,1024]{4,3,0,2,1:T(8,128)S(1)}, u32[]{:S(2)}, u32[]{:S(2)}) collective-permute-start(f32[2,1,2,8,1024]{4,3,0,2,1:T(8,128)S(1)} %copy.73), channel_id=1, source_target_pairs={{0,8},{8,0},{16,24},{24,16},{1,9},{9,1},{17,25},{25,17},{2,10},{10... | collective-permute-start | bytes 393224 | tf_op jit(solution)/shard_map/ppermute | solution.py:207
  2.5 69.2 %collective-permute-start = (f32[2,32,128,128]{3,2,1,0:T(8,128)}, f32[2,32,128,128]{3,2,1,0:T(8,128)}, u32[]{:S(2)}, u32[]{:S(2)}) collective-permute-start(f32[2,32,128,128]{3,2,1,0:T(8,128)} %in_ref.1), channel_id=1, source_target_pairs={{0,24},{8,0},{16,8},{24,16},{1,25},{9,1},{17,9},{25,17},{2,26},{10... | collective-permute-start | bytes 12582920 | tf_op jit(solution)/shard_map/ppermute | solution.py:239
  5.9 12.9 %collective-permute-start.3 = (f32[8,3,128]{2,1,0:T(4,128)S(1)}, f32[8,3,128]{2,1,0:T(4,128)S(1)}, u32[]{:S(2)}, u32[]{:S(2)}) collective-permute-start(f32[8,3,128]{2,1,0:T(4,128)S(1)} %copy.81), channel_id=1, source_target_pairs={{0,1},{1,0},{2,3},{3,2},{4,5},{5,4},{6,7},{7,6},{8,9},{9,8},{10,11... | collective-permute-start | bytes 36872 | tf_op jit(solution)/shard_map/ppermute | solution.py:207
  18.8 4.0 %collective-permute-start.4 = (f32[16,3,128]{2,1,0:T(4,128)S(1)}, f32[16,3,128]{2,1,0:T(4,128)S(1)}, u32[]{:S(2)}, u32[]{:S(2)}) collective-permute-start(f32[16,3,128]{2,1,0:T(4,128)S(1)} %maximum_select_fusion.5), channel_id=1, source_target_pairs={{0,2},{1,3},{2,0},{3,1},{4,6},{5,7},{6,4},{7,5},{8,10},{9,11},{10,... | collective-permute-start | bytes 73736 | tf_op jit(solution)/shard_map/ppermute | solution.py:207
  22.8 12.4 %collective-permute-start.5 = (f32[32,3,128]{2,1,0:T(4,128)S(1)}, f32[32,3,128]{2,1,0:T(4,128)S(1)}, u32[]{:S(2)}, u32[]{:S(2)}) collective-permute-start(f32[32,3,128]{2,1,0:T(4,128)S(1)} %maximum_select_fusion.4), channel_id=1, source_target_pairs={{0,4},{1,5},{2,6},{3,7},{4,0},{5,1},{6,2},{7,3},{8,12},{9,13},{10,... | collective-permute-start | bytes 147464 | tf_op jit(solution)/shard_map/ppermute | solution.py:207
  39.2 18.2 %collective-permute-start.2 = (f32[2,1,2,16,1024]{4,3,0,2,1:T(8,128)S(1)}, f32[2,1,2,16,1024]{4,3,0,2,1:T(8,128)S(1)}, u32[]{:S(2)}, u32[]{:S(2)}) collective-permute-start(f32[2,1,2,16,1024]{4,3,0,2,1:T(8,128)S(1)} %maximum_select_fusion.2), channel_id=1, source_target_pairs={{0,16},{8,24},{16,0},{24,8},{1,17},{9,25},{17,1},{25,9},{2,18},{10... | collective-permute-start | bytes 786440 | tf_op jit(solution)/shard_map/ppermute | solution.py:207

commit v6 on v5

--- a/solution.py
+++ b/solution.py
@@ -215,6 +215,22 @@
     return held
 
 
+def gather_direct(piece, axis_name, dim):
+    count = lax.axis_size(axis_name)
+    index = lax.axis_index(axis_name)
+    held = [piece]
+    for hop in range(1, count):
+        pairs = [(i, (i + hop) % count) for i in range(count)]
+        held.append(lax.ppermute(piece, axis_name, perm=pairs))
+    stacked = jnp.stack(held, axis=0)
+    order = (index - jnp.arange(count)) % count
+    ordered = jnp.take(stacked, order, axis=0, mode="clip")
+    ordered = jnp.moveaxis(ordered, 0, dim)
+    shape = list(piece.shape)
+    shape[dim] = shape[dim] * count
+    return ordered.reshape(shape)
+
+
 def score_grids(receptor, ligand_box, channel_weight):
     size = receptor.shape[2]
     slab_count = lax.axis_size("slab")
@@ -228,14 +244,15 @@
 
     lead = ligand_box.shape[:4]
     dense = ligand_box.reshape(lead + (box * box,))
-    full_box = gather_pieces(dense, "slab", 3)
+    full_box = gather_direct(dense, "slab", 3)
+    full_box, outgoing = lax.optimization_barrier((full_box, receptor))
     chunks = 1
     chunk = part // chunks
     blocks = [receptor]
     for hop in range(1, extra + 1):
         pairs = [(i, (i - hop) % slab_count) for i in range(slab_count)]
         for piece in range(chunks):
-            sent = receptor[:, piece * chunk : (piece + 1) * chunk]
+            sent = outgoing[:, piece * chunk : (piece + 1) * chunk]
             blocks.append(lax.ppermute(sent, "slab", perm=pairs))
 
     cos_n, sin_n = phase_tables(size, size, size)

time: 115 us -> 104 us (0.904)
  waiting for transfers between devices: 18.8 us -> 6.19 us
    ppermute x5 -> x3, waiting for transfers between devices: 18.8 us -> 1.67 us  [gather_pieces(): other = lax.ppermute(held, axis_name, perm=pairs)]
    ppermute x1, waiting for transfers between devices: 0.01 us -> 4.16 us  [score_grids(): blocks.append(lax.ppermute(sent, 'slab', perm=pairs))]
    ppermute x0 -> x3, starting transfers between devices: none -> 3.26 us  [gather_direct(): held.append(lax.ppermute(piece, axis_name, perm=pairs))]
    ppermute x1, starting transfers between devices: 2.63 us -> 1.02 us  [score_grids(): blocks.append(lax.ppermute(sent, 'slab', perm=pairs))]
    another operation x0 -> x1, local copies, waits for them, and re-layouts: none -> 1.27 us  [gather_direct(): stacked = jnp.stack(held, axis=0)]
    ppermute x5 -> x3, starting transfers between devices: 6.87 us -> 5.79 us  [gather_pieces(): other = lax.ppermute(held, axis_name, perm=pairs)]
  transfers between devices with their start and end apart: 6 -> 7, of which waited for: 2 -> 3; matrix products, arithmetic and copies ran while one was open for 18% -> 21% of each run, Pallas kernels for 18% -> 20%
where the time goes in v6:
time: 104 us; the launch traced here: 102 us
  Pallas kernels  62.5 us (60%)
  other arithmetic  12.7 us (12%)
  starting transfers between devices  10.1 us (10%)
  local copies, waits for them, and re-layouts  7.77 us (7%)
  waiting for transfers between devices  6.19 us (6%)
  matrix products  2.39 us (2%)
    pallas_call x3, Pallas kernels, forward_planes(): pl.pallas_call(forward_plane_kernel, grid=(planes // plane_step,), in_spe...  29.3 us
    pallas_call x1, Pallas kernels, cross_spectra(): pl.pallas_call(kernel, grid=(size // row_step,), in_specs=[pl.BlockSpec((...  21.4 us
    pallas_call x1, Pallas kernels, inverse_planes(): pl.pallas_call(inverse_plane_kernel, grid=(sets, planes // plane_step), i...  11.8 us
    ppermute x3, starting transfers between devices, gather_pieces(): other = lax.ppermute(held, axis_name, perm=pairs)  5.79 us
    ppermute x1, waiting for transfers between devices, score_grids(): blocks.append(lax.ppermute(sent, 'slab', perm=pairs))  4.16 us
    ppermute x3, starting transfers between devices, gather_direct(): held.append(lax.ppermute(piece, axis_name, perm=pairs))  3.26 us
    concatenate x4, other arithmetic, block2(): return jnp.concatenate([top, bottom], axis=0)  2.95 us
  transfers between devices with their start and end apart: 7, of which 3 were waited for; matrix products, arithmetic and copies ran while one was open for 21% of the time, Pallas kernels for 20%

profile of v6, /device:TPU:0, one launch (start us, length us, event | category | flops | bytes accessed | tf_op | source)
XLA Modules:
  0.0 102.5 jit_solution(16684532985034852603)
XLA Ops:
  0.7 1.3 %reshape.146 = f32[2,1,2,8,1024]{4,3,2,0,1:T(8,128)S(1)} reshape(f32[2,1,2,8,32,32]{5,4,3,2,1,0:T(8,128)} %param.11) | data formatting | bytes 262144 | tf_op jit(solution)/shard_map/reshape | solution.py:246
  2.0 2.5 %collective-permute-start.2 = (f32[2,1,2,8,1024]{4,3,2,0,1:T(8,128)S(1)}, f32[2,1,2,8,1024]{4,3,2,0,1:T(8,128)S(1)}, u32[]{:S(2)}, u32[]{:S(2)}) collective-permute-start(f32[2,1,2,8,1024]{4,3,2,0,1:T(8,128)S(1)} %reshape.146), channel_id=1, source_target_pairs={{0,24},{8,0},{16,8},{24,16},{1,25},{9,1},{17,9},{25,17},{2,26},{10... | collective-permute-start | bytes 393224 | tf_op jit(solution)/shard_map/ppermute | solution.py:224
  5.3 0.7 copy.61
  6.0 1.5 %collective-permute-start.4 = (f32[8,3,128]{2,1,0:T(4,128)S(1)}, f32[8,3,128]{2,1,0:T(4,128)S(1)}, u32[]{:S(2)}, u32[]{:S(2)}) collective-permute-start(f32[8,3,128]{2,1,0:T(4,128)S(1)} %copy.61), channel_id=1, source_target_pairs={{0,1},{1,0},{2,3},{3,2},{4,5},{5,4},{6,7},{7,6},{8,9},{9,8},{10,11... | collective-permute-start | bytes 36872 | tf_op jit(solution)/shard_map/ppermute | solution.py:207
  10.2 1.3 %stack_reshape.3 = f32[1,2,1,2,8,1024]{5,4,3,1,2,0:T(8,128)S(1)} reshape(f32[2,1,2,8,32,32]{5,4,3,2,1,0:T(8,128)} %param.11) | data formatting | bytes 262144 | tf_op jit(solution)/shard_map/stack;reshape | solution.py:225
  12.7 1.0 collective-permute-start.3
  13.8 0.7 gather_fusion.1
  15.3 0.7 maximum_maximum_fusion.3.refs_4_
  16.1 0.8 maximum_maximum_fusion.2.refs_3_
  18.1 0.8 maximum_maximum_fusion.ly_ref
  18.8 0.8 fusion.3
  20.9 1.6 %collective-permute-start.5 = (f32[16,3,128]{2,1,0:T(4,128)S(1)}, f32[16,3,128]{2,1,0:T(4,128)S(1)}, u32[]{:S(2)}, u32[]{:S(2)}) collective-permute-start(f32[16,3,128]{2,1,0:T(4,128)S(1)} %maximum_select_fusion.2), channel_id=1, source_target_pairs={{0,2},{1,3},{2,0},{3,1},{4,6},{5,7},{6,4},{7,5},{8,10},{9,11},{10,... | collective-permute-start | bytes 73736 | tf_op jit(solution)/shard_map/ppermute | solution.py:207
  23.2 1.7 %collective-permute-done.5 = f32[16,3,128]{2,1,0:T(4,128)S(1)} collective-permute-done((f32[16,3,128]{2,1,0:T(4,128)S(1)}, f32[16,3,128]{2,1,0:T(4,128)S(1)}, u32[]{:S(2)}, u32[]{:S(2)}) %collective-permute-start.5) | collective-permute-done | bytes 24608 | tf_op jit(solution)/shard_map/ppermute | solution.py:207
  24.9 2.7 %collective-permute-start.6 = (f32[32,3,128]{2,1,0:T(4,128)S(1)}, f32[32,3,128]{2,1,0:T(4,128)S(1)}, u32[]{:S(2)}, u32[]{:S(2)}) collective-permute-start(f32[32,3,128]{2,1,0:T(4,128)S(1)} %maximum_select_fusion.1), channel_id=1, source_target_pairs={{0,4},{1,5},{2,6},{3,7},{4,0},{5,1},{6,2},{7,3},{8,12},{9,13},{10,... | collective-permute-start | bytes 147464 | tf_op jit(solution)/shard_map/ppermute | solution.py:207
  27.6 9.4 %shard_map.113.refs_0_ = f32[2,32,128,128]{3,2,1,0:T(8,128)} custom-call(f32[2,32,128,128]{3,2,1,0:T(8,128)} %in_ref.1, f32[256,256]{1,0:T(8,128)} %get-tuple-element.21.rz_ref.ly_ref, f32[256,256]{1,0:T(8,128)} %get-tuple-element.20.ly_ref), custom_call_target="tpu_custom_call" | custom-call | tf_op jit(solution)/shard_map/pallas_call | solution.py:95
  37.0 1.0 gather_fusion.2
  39.0 1.9 %fusion = f32[256,3,3]{2,1,0:T(4,128)S(1)} fusion(f32[256,3,128]{2,1,0:T(4,128)S(1)} %copy.65, f32[256,3,128]{2,1,0:T(4,128)S(1)} %gather_fusion.2, f32[256,3]{1,0:T(8,128)S(1)} %broadcast_multiply_fusion), kind=kOutput, calls=%fused_computation.7 | convolution fusion | flops 3637248 | bytes 798720 | tf_op jit(solution)/shard_map/pja,pka->pjk/dot_general | solution.py:321
  41.6 1.3 %slice_multiply_fusion.1 = (f32[2,1,1,32,1024]{4,3,0,2,1:T(8,128)S(1)}, f32[2,1,1,32,1024]{4,3,0,2,1:T(8,128)S(1)}) fusion(f32[2,1,2,32,1024]{4,3,0,2,1:T(8,128)S(1)} %copy_bitcast_fusion, f32[]{:T(128)} %bitcast.8, f32[]{:T(128)} %bitcast.9), kind=kLoop, calls=%fused_computation.18 | loop fusion | flops 131072 | bytes 1048584 | tf_op jit(solution)/shard_map/mul | solution.py:264
  43.7 1.6 %pad_maximum_fusion.in_ref = f32[2,64,32,32]{3,2,1,0:T(8,128)} fusion(f32[1,64,32,32]{3,2,1,0:T(8,128)S(1)} %mul.227, f32[1,64,32,32]{3,2,1,0:T(8,128)S(1)} %mul.224), kind=kLoop, calls=%fused_computation.3 | loop fusion | flops 131072 | bytes 1048576 | tf_op jit(solution)/shard_map/stack | solution.py:263
  45.2 10.6 %shard_map.115.refs_2_ = f32[2,64,128,128]{3,2,1,0:T(8,128)} custom-call(f32[2,64,32,32]{3,2,1,0:T(8,128)} %pad_maximum_fusion.in_ref, f32[64,256]{1,0:T(8,128)} %maximum_maximum_fusion.1.rz_ref, f32[256,64]{1,0:T(8,128)} %maximum_maximum_fusion.ly_ref), custom_call_target="tpu_custom_call" | custom-call | tf_op jit(solution)/shard_map/pallas_call | solution.py:95
  55.9 4.2 %collective-permute-done.3.in_ref = f32[2,32,128,128]{3,2,1,0:T(8,128)} collective-permute-done((f32[2,32,128,128]{3,2,1,0:T(8,128)}, f32[2,32,128,128]{3,2,1,0:T(8,128)}, u32[]{:S(2)}, u32[]{:S(2)}) %collective-permute-start.3) | collective-permute-done | bytes 4194336 | tf_op jit(solution)/shard_map/ppermute | solution.py:256
  60.0 9.2 %shard_map.114.refs_1_ = f32[2,32,128,128]{3,2,1,0:T(8,128)} custom-call(f32[2,32,128,128]{3,2,1,0:T(8,128)} %collective-permute-done.3.in_ref, f32[256,256]{1,0:T(8,128)} %get-tuple-element.21.rz_ref.ly_ref, f32[256,256]{1,0:T(8,128)} %get-tuple-element.20.ly_ref), custom_call_target="tpu_custom_call" | custom-call | tf_op jit(solution)/shard_map/pallas_call | solution.py:95
  69.3 21.4 %shard_map.116.in_ref = f32[2,2,32,128,128]{4,3,2,1,0:T(8,128)} custom-call(f32[2,32,128,128]{3,2,1,0:T(8,128)} %shard_map.113.refs_0_, f32[2,32,128,128]{3,2,1,0:T(8,128)} %shard_map.114.refs_1_, f32[2,64,128,128]{3,2,1,0:T(8,128)} %shard_map.115.refs_2_, f32[128,128]{1,0:T(8,128)} %maximum_maximum_fusion.2.refs_3_, ...), custom_call_target="tpu_custom_call" | custom-call | tf_op jit(solution)/shard_map/pallas_call | solution.py:158
  90.7 11.8 %shard_map.117 = f32[2,32,128,128]{3,2,1,0:T(8,128)} custom-call(f32[2,2,32,128,128]{4,3,2,1,0:T(8,128)} %shard_map.116.in_ref, f32[256,256]{1,0:T(8,128)} %get-tuple-element.21.rz_ref.ly_ref, f32[256,128]{1,0:T(8,128)} %pad_maximum_fusion.5.rz_ref), custom_call_target="tpu_custom_call" | custom-call | tf_op jit(solution)/shard_map/pallas_call | solution.py:173
  (65 shorter events, 11.2 us)
Async XLA Ops:
  0.6 19.0 %copy-start = (f32[3,128]{1,0:T(4,128)S(1)}, f32[3,128]{1,0:T(4,128)}, u32[]{:S(2)}) copy-start(f32[3,128]{1,0:T(4,128)} %param.14) | copy-start | bytes 4612
  0.6 13.1 %copy-start.1 = (f32[9,16]{1,0:T(8,128)S(1)}, f32[9,16]{1,0:T(8,128)}, u32[]{:S(2)}) copy-start(f32[9,16]{1,0:T(8,128)} %param.13) | copy-start | bytes 1732
  0.7 19.0 %copy-start.4 = (s32[256,1]{0,1:T(1,128)S(1)}, s32[256,1]{0,1:T(1,128)}, u32[]{:S(2)}) copy-start(s32[256,1]{0,1:T(1,128)} %param.18) | copy-start | bytes 3076
  0.7 21.9 %copy-start.2 = (f32[2]{0:T(128)S(1)}, f32[2]{0:T(128)}, u32[]{:S(2)}) copy-start(f32[2]{0:T(128)} %param.12) | copy-start | bytes 28
  0.7 22.6 %copy-start.3 = (s32[256]{0:T(256)S(1)}, s32[256]{0:T(256)}, u32[]{:S(2)}) copy-start(s32[256]{0:T(256)} %param.19) | copy-start | bytes 3076
  2.0 9.6 %collective-permute-start.2 = (f32[2,1,2,8,1024]{4,3,2,0,1:T(8,128)S(1)}, f32[2,1,2,8,1024]{4,3,2,0,1:T(8,128)S(1)}, u32[]{:S(2)}, u32[]{:S(2)}) collective-permute-start(f32[2,1,2,8,1024]{4,3,2,0,1:T(8,128)S(1)} %reshape.146), channel_id=1, source_target_pairs={{0,24},{8,0},{16,8},{24,16},{1,25},{9,1},{17,9},{25,17},{2,26},{10... | collective-permute-start | bytes 393224 | tf_op jit(solution)/shard_map/ppermute | solution.py:224
  4.5 7.5 %collective-permute-start.1 = (f32[2,1,2,8,1024]{4,3,2,0,1:T(8,128)S(1)}, f32[2,1,2,8,1024]{4,3,2,0,1:T(8,128)S(1)}, u32[]{:S(2)}, u32[]{:S(2)}) collective-permute-start(f32[2,1,2,8,1024]{4,3,2,0,1:T(8,128)S(1)} %reshape.146), channel_id=1, source_target_pairs={{0,16},{8,24},{16,0},{24,8},{1,17},{9,25},{17,1},{25,9},{2,18},{10... | collective-permute-start | bytes 393224 | tf_op jit(solution)/shard_map/ppermute | solution.py:224
  5.1 6.9 %collective-permute-start = (f32[2,1,2,8,1024]{4,3,2,0,1:T(8,128)S(1)}, f32[2,1,2,8,1024]{4,3,2,0,1:T(8,128)S(1)}, u32[]{:S(2)}, u32[]{:S(2)}) collective-permute-start(f32[2,1,2,8,1024]{4,3,2,0,1:T(8,128)S(1)} %reshape.146), channel_id=1, source_target_pairs={{0,8},{8,16},{16,24},{24,0},{1,9},{9,17},{17,25},{25,1},{2,10},{10... | collective-permute-start | bytes 393224 | tf_op jit(solution)/shard_map/ppermute | solution.py:224
  6.0 14.9 %collective-permute-start.4 = (f32[8,3,128]{2,1,0:T(4,128)S(1)}, f32[8,3,128]{2,1,0:T(4,128)S(1)}, u32[]{:S(2)}, u32[]{:S(2)}) collective-permute-start(f32[8,3,128]{2,1,0:T(4,128)S(1)} %copy.61), channel_id=1, source_target_pairs={{0,1},{1,0},{2,3},{3,2},{4,5},{5,4},{6,7},{7,6},{8,9},{9,8},{10,11... | collective-permute-start | bytes 36872 | tf_op jit(solution)/shard_map/ppermute | solution.py:207
  12.7 47.4 %collective-permute-start.3 = (f32[2,32,128,128]{3,2,1,0:T(8,128)}, f32[2,32,128,128]{3,2,1,0:T(8,128)}, u32[]{:S(2)}, u32[]{:S(2)}) collective-permute-start(f32[2,32,128,128]{3,2,1,0:T(8,128)} %in_ref.1), channel_id=1, source_target_pairs={{0,24},{8,0},{16,8},{24,16},{1,25},{9,1},{17,9},{25,17},{2,26},{10... | collective-permute-start | bytes 12582920 | tf_op jit(solution)/shard_map/ppermute | solution.py:256
  20.9 4.0 %collective-permute-start.5 = (f32[16,3,128]{2,1,0:T(4,128)S(1)}, f32[16,3,128]{2,1,0:T(4,128)S(1)}, u32[]{:S(2)}, u32[]{:S(2)}) collective-permute-start(f32[16,3,128]{2,1,0:T(4,128)S(1)} %maximum_select_fusion.2), channel_id=1, source_target_pairs={{0,2},{1,3},{2,0},{3,1},{4,6},{5,7},{6,4},{7,5},{8,10},{9,11},{10,... | collective-permute-start | bytes 73736 | tf_op jit(solution)/shard_map/ppermute | solution.py:207
  24.9 12.1 %collective-permute-start.6 = (f32[32,3,128]{2,1,0:T(4,128)S(1)}, f32[32,3,128]{2,1,0:T(4,128)S(1)}, u32[]{:S(2)}, u32[]{:S(2)}) collective-permute-start(f32[32,3,128]{2,1,0:T(4,128)S(1)} %maximum_select_fusion.1), channel_id=1, source_target_pairs={{0,4},{1,5},{2,6},{3,7},{4,0},{5,1},{6,2},{7,3},{8,12},{9,13},{10,... | collective-permute-start | bytes 147464 | tf_op jit(solution)/shard_map/ppermute | solution.py:207

commit v7 on v6

--- a/solution.py
+++ b/solution.py
@@ -245,20 +245,15 @@
     lead = ligand_box.shape[:4]
     dense = ligand_box.reshape(lead + (box * box,))
     full_box = gather_direct(dense, "slab", 3)
-    full_box, outgoing = lax.optimization_barrier((full_box, receptor))
-    chunks = 1
-    chunk = part // chunks
-    blocks = [receptor]
-    for hop in range(1, extra + 1):
-        pairs = [(i, (i - hop) % slab_count) for i in range(slab_count)]
-        for piece in range(chunks):
-            sent = outgoing[:, piece * chunk : (piece + 1) * chunk]
-            blocks.append(lax.ppermute(sent, "slab", perm=pairs))
-
     cos_n, sin_n = phase_tables(size, size, size)
     rz = block2(cos_n, -sin_n, sin_n, cos_n)
     ly = block2(cos_n, sin_n, -sin_n, cos_n)
-    rec_blocks = [forward_planes(planes, (rz, ly), plane_step, size) for planes in blocks]
+    own = forward_planes(receptor, (rz, ly), plane_step, size)
+    full_box, outgoing = lax.optimization_barrier((full_box, own))
+    rec_blocks = [own]
+    for hop in range(1, extra + 1):
+        pairs = [(i, (i - hop) % slab_count) for i in range(slab_count)]
+        rec_blocks.append(lax.ppermute(outgoing, "slab", perm=pairs))
 
     lig = jnp.stack(
         [full_box[:, 0, 0] * channel_weight[0], full_box[:, 0, 1] * channel_weight[1]], axis=0
@@ -271,7 +266,7 @@
     cos_w, sin_w = phase_tables(window, window, window)
     g_tables = []
     first = 0
-    for planes in blocks:
+    for planes in rec_blocks:
         cols = slice(first, first + planes.shape[1])
         first += planes.shape[1]
         g_tables.append(block2(cos_w[:, cols], sin_w[:, cols], -sin_w[:, cols], cos_w[:, cols]))

time: 104 us -> 105 us (level)
  waiting for transfers between devices: 6.19 us -> 16 us
  Pallas kernels: 62.5 us -> 53.1 us
    pallas_call x3 -> x2, Pallas kernels: 29.3 us -> 19.9 us  [forward_planes(): pl.pallas_call(forward_plane_kernel, grid=(planes // plane_step,), in_spe...]
    ppermute x1, waiting for transfers between devices: 4.16 us -> 11.7 us  [score_grids(): rec_blocks.append(lax.ppermute(outgoing, 'slab', perm=pairs))]
    ppermute x3, waiting for transfers between devices: 1.67 us -> 4.3 us  [gather_pieces(): other = lax.ppermute(held, axis_name, perm=pairs)]
  transfers between devices with their start and end apart: 7 -> 7, of which waited for: 3 -> 3; matrix products, arithmetic and copies ran while one was open for 21% -> 21% of each run, Pallas kernels for 20% -> 19%
where the time goes in v7:
time: 105 us; the launch traced here: 103 us
  Pallas kernels  53.1 us (51%)
  waiting for transfers between devices  16 us (15%)
  other arithmetic  12.7 us (12%)
  starting transfers between devices  10.6 us (10%)
  local copies, waits for them, and re-layouts  7.66 us (7%)
  matrix products  2.39 us (2%)
    pallas_call x1, Pallas kernels, cross_spectra(): pl.pallas_call(kernel, grid=(size // row_step,), in_specs=[pl.BlockSpec((...  21.4 us
    pallas_call x2, Pallas kernels, forward_planes(): pl.pallas_call(forward_plane_kernel, grid=(planes // plane_step,), in_spe...  19.9 us
    pallas_call x1, Pallas kernels, inverse_planes(): pl.pallas_call(inverse_plane_kernel, grid=(sets, planes // plane_step), i...  11.8 us
    ppermute x1, waiting for transfers between devices, score_grids(): rec_blocks.append(lax.ppermute(outgoing, 'slab', perm=pairs))  11.7 us
    ppermute x3, starting transfers between devices, gather_pieces(): other = lax.ppermute(held, axis_name, perm=pairs)  5.8 us
    ppermute x3, waiting for transfers between devices, gather_pieces(): other = lax.ppermute(held, axis_name, perm=pairs)  4.3 us
    ppermute x3, starting transfers between devices, gather_direct(): held.append(lax.ppermute(piece, axis_name, perm=pairs))  3.26 us
    concatenate x4, other arithmetic, block2(): return jnp.concatenate([top, bottom], axis=0)  2.92 us
  transfers between devices with their start and end apart: 7, of which 3 were waited for; matrix products, arithmetic and copies ran while one was open for 21% of the time, Pallas kernels for 19%

profile of v7, /device:TPU:0, one launch (start us, length us, event | category | flops | bytes accessed | tf_op | source)
XLA Modules:
  0.0 103.3 jit_solution(4924735512788991955)
XLA Ops:
  0.6 1.3 %reshape.146 = f32[2,1,2,8,1024]{4,3,2,0,1:T(8,128)S(1)} reshape(f32[2,1,2,8,32,32]{5,4,3,2,1,0:T(8,128)} %param.11) | data formatting | bytes 262144 | tf_op jit(solution)/shard_map/reshape | solution.py:246
  1.9 2.5 %collective-permute-start.2 = (f32[2,1,2,8,1024]{4,3,2,0,1:T(8,128)S(1)}, f32[2,1,2,8,1024]{4,3,2,0,1:T(8,128)S(1)}, u32[]{:S(2)}, u32[]{:S(2)}) collective-permute-start(f32[2,1,2,8,1024]{4,3,2,0,1:T(8,128)S(1)} %reshape.146), channel_id=1, source_target_pairs={{0,24},{8,0},{16,8},{24,16},{1,25},{9,1},{17,9},{25,17},{2,26},{10... | collective-permute-start | bytes 393224 | tf_op jit(solution)/shard_map/ppermute | solution.py:224
  5.2 0.7 copy.61
  5.9 1.5 %collective-permute-start.4 = (f32[8,3,128]{2,1,0:T(4,128)S(1)}, f32[8,3,128]{2,1,0:T(4,128)S(1)}, u32[]{:S(2)}, u32[]{:S(2)}) collective-permute-start(f32[8,3,128]{2,1,0:T(4,128)S(1)} %copy.61), channel_id=1, source_target_pairs={{0,1},{1,0},{2,3},{3,2},{4,5},{5,4},{6,7},{7,6},{8,9},{9,8},{10,11... | collective-permute-start | bytes 36872 | tf_op jit(solution)/shard_map/ppermute | solution.py:207
  9.4 0.8 fusion.3
  10.9 1.3 %stack_reshape.3 = f32[1,2,1,2,8,1024]{5,4,3,1,2,0:T(8,128)S(1)} reshape(f32[2,1,2,8,32,32]{5,4,3,2,1,0:T(8,128)} %param.11) | data formatting | bytes 262144 | tf_op jit(solution)/shard_map/stack;reshape | solution.py:225
  12.2 9.2 %shard_map.113.refs_0_ = f32[2,32,128,128]{3,2,1,0:T(8,128)} custom-call(f32[2,32,128,128]{3,2,1,0:T(8,128)} %in_ref.1, f32[256,256]{1,0:T(8,128)} %get-tuple-element.21.rz_ref.ly_ref, f32[256,256]{1,0:T(8,128)} %get-tuple-element.20.ly_ref), custom_call_target="tpu_custom_call" | custom-call | tf_op jit(solution)/shard_map/pallas_call | solution.py:95
  22.2 1.5 %collective-permute-start.3 = (f32[2,32,128,128]{3,2,1,0:T(8,128)}, f32[2,32,128,128]{3,2,1,0:T(8,128)}, u32[]{:S(2)}, u32[]{:S(2)}) collective-permute-start(f32[2,32,128,128]{3,2,1,0:T(8,128)} %shard_map.113.refs_0_), channel_id=1, source_target_pairs={{0,24},{8,0},{16,8},{24,16},{1,25},{9,1},{17,9},{25,17},{2,26},{10... | collective-permute-start | bytes 12582920 | tf_op jit(solution)/shard_map/ppermute | solution.py:256
  23.9 0.7 gather_fusion.1
  25.7 0.7 maximum_maximum_fusion.3.refs_4_
  26.5 0.8 maximum_maximum_fusion.2.refs_3_
  28.2 0.8 maximum_maximum_fusion.ly_ref
  30.2 1.6 %collective-permute-start.5 = (f32[16,3,128]{2,1,0:T(4,128)S(1)}, f32[16,3,128]{2,1,0:T(4,128)S(1)}, u32[]{:S(2)}, u32[]{:S(2)}) collective-permute-start(f32[16,3,128]{2,1,0:T(4,128)S(1)} %maximum_select_fusion.2), channel_id=1, source_target_pairs={{0,2},{1,3},{2,0},{3,1},{4,6},{5,7},{6,4},{7,5},{8,10},{9,11},{10,... | collective-permute-start | bytes 73736 | tf_op jit(solution)/shard_map/ppermute | solution.py:207
  32.5 1.7 %collective-permute-done.5 = f32[16,3,128]{2,1,0:T(4,128)S(1)} collective-permute-done((f32[16,3,128]{2,1,0:T(4,128)S(1)}, f32[16,3,128]{2,1,0:T(4,128)S(1)}, u32[]{:S(2)}, u32[]{:S(2)}) %collective-permute-start.5) | collective-permute-done | bytes 24608 | tf_op jit(solution)/shard_map/ppermute | solution.py:207
  34.2 2.7 %collective-permute-start.6 = (f32[32,3,128]{2,1,0:T(4,128)S(1)}, f32[32,3,128]{2,1,0:T(4,128)S(1)}, u32[]{:S(2)}, u32[]{:S(2)}) collective-permute-start(f32[32,3,128]{2,1,0:T(4,128)S(1)} %maximum_select_fusion.1), channel_id=1, source_target_pairs={{0,4},{1,5},{2,6},{3,7},{4,0},{5,1},{6,2},{7,3},{8,12},{9,13},{10,... | collective-permute-start | bytes 147464 | tf_op jit(solution)/shard_map/ppermute | solution.py:207
  36.9 2.6 %collective-permute-done.6 = f32[32,3,128]{2,1,0:T(4,128)S(1)} collective-permute-done((f32[32,3,128]{2,1,0:T(4,128)S(1)}, f32[32,3,128]{2,1,0:T(4,128)S(1)}, u32[]{:S(2)}, u32[]{:S(2)}) %collective-permute-start.6) | collective-permute-done | bytes 49184 | tf_op jit(solution)/shard_map/ppermute | solution.py:207
  39.5 1.0 gather_fusion.2
  41.4 1.9 %fusion = f32[256,3,3]{2,1,0:T(4,128)S(1)} fusion(f32[256,3,128]{2,1,0:T(4,128)S(1)} %copy.65, f32[256,3,128]{2,1,0:T(4,128)S(1)} %gather_fusion.2, f32[256,3]{1,0:T(8,128)S(1)} %broadcast_multiply_fusion), kind=kOutput, calls=%fused_computation.7 | convolution fusion | flops 3637248 | bytes 798720 | tf_op jit(solution)/shard_map/pja,pka->pjk/dot_general | solution.py:316
  44.1 1.3 %slice_multiply_fusion.1 = (f32[2,1,1,32,1024]{4,3,0,2,1:T(8,128)S(1)}, f32[2,1,1,32,1024]{4,3,0,2,1:T(8,128)S(1)}) fusion(f32[2,1,2,32,1024]{4,3,0,2,1:T(8,128)S(1)} %copy_bitcast_fusion, f32[]{:T(128)} %bitcast.8, f32[]{:T(128)} %bitcast.9), kind=kLoop, calls=%fused_computation.18 | loop fusion | flops 131072 | bytes 1048584 | tf_op jit(solution)/shard_map/mul | solution.py:259
  46.2 1.6 %pad_maximum_fusion.in_ref = f32[2,64,32,32]{3,2,1,0:T(8,128)} fusion(f32[1,64,32,32]{3,2,1,0:T(8,128)S(1)} %mul.227, f32[1,64,32,32]{3,2,1,0:T(8,128)S(1)} %mul.224), kind=kLoop, calls=%fused_computation.3 | loop fusion | flops 131072 | bytes 1048576 | tf_op jit(solution)/shard_map/stack | solution.py:258
  47.8 10.6 %shard_map.114.refs_2_ = f32[2,64,128,128]{3,2,1,0:T(8,128)} custom-call(f32[2,64,32,32]{3,2,1,0:T(8,128)} %pad_maximum_fusion.in_ref, f32[64,256]{1,0:T(8,128)} %maximum_maximum_fusion.1.rz_ref, f32[256,64]{1,0:T(8,128)} %maximum_maximum_fusion.ly_ref), custom_call_target="tpu_custom_call" | custom-call | tf_op jit(solution)/shard_map/pallas_call | solution.py:95
  58.4 11.7 %collective-permute-done.3.refs_1_ = f32[2,32,128,128]{3,2,1,0:T(8,128)} collective-permute-done((f32[2,32,128,128]{3,2,1,0:T(8,128)}, f32[2,32,128,128]{3,2,1,0:T(8,128)}, u32[]{:S(2)}, u32[]{:S(2)}) %collective-permute-start.3) | collective-permute-done | bytes 4194336 | tf_op jit(solution)/shard_map/ppermute | solution.py:256
  70.1 21.4 %shard_map.115.in_ref = f32[2,2,32,128,128]{4,3,2,1,0:T(8,128)} custom-call(f32[2,32,128,128]{3,2,1,0:T(8,128)} %shard_map.113.refs_0_, f32[2,32,128,128]{3,2,1,0:T(8,128)} %collective-permute-done.3.refs_1_, f32[2,64,128,128]{3,2,1,0:T(8,128)} %shard_map.114.refs_2_, f32[128,128]{1,0:T(8,128)} %maximum_maximum_fusion.2.refs_3_, ...), custom_call_target="tpu_custom_call" | custom-call | tf_op jit(solution)/shard_map/pallas_call | solution.py:158
  91.5 11.8 %shard_map.116 = f32[2,32,128,128]{3,2,1,0:T(8,128)} custom-call(f32[2,2,32,128,128]{4,3,2,1,0:T(8,128)} %shard_map.115.in_ref, f32[256,256]{1,0:T(8,128)} %get-tuple-element.21.rz_ref.ly_ref, f32[256,128]{1,0:T(8,128)} %pad_maximum_fusion.5.rz_ref), custom_call_target="tpu_custom_call" | custom-call | tf_op jit(solution)/shard_map/pallas_call | solution.py:173
  (64 shorter events, 10.7 us)
Async XLA Ops:
  0.6 28.4 %copy-start = (f32[3,128]{1,0:T(4,128)S(1)}, f32[3,128]{1,0:T(4,128)}, u32[]{:S(2)}) copy-start(f32[3,128]{1,0:T(4,128)} %param.14) | copy-start | bytes 4612
  1.9 19.6 %collective-permute-start.2 = (f32[2,1,2,8,1024]{4,3,2,0,1:T(8,128)S(1)}, f32[2,1,2,8,1024]{4,3,2,0,1:T(8,128)S(1)}, u32[]{:S(2)}, u32[]{:S(2)}) collective-permute-start(f32[2,1,2,8,1024]{4,3,2,0,1:T(8,128)S(1)} %reshape.146), channel_id=1, source_target_pairs={{0,24},{8,0},{16,8},{24,16},{1,25},{9,1},{17,9},{25,17},{2,26},{10... | collective-permute-start | bytes 393224 | tf_op jit(solution)/shard_map/ppermute | solution.py:224
  4.4 17.1 %collective-permute-start.1 = (f32[2,1,2,8,1024]{4,3,2,0,1:T(8,128)S(1)}, f32[2,1,2,8,1024]{4,3,2,0,1:T(8,128)S(1)}, u32[]{:S(2)}, u32[]{:S(2)}) collective-permute-start(f32[2,1,2,8,1024]{4,3,2,0,1:T(8,128)S(1)} %reshape.146), channel_id=1, source_target_pairs={{0,16},{8,24},{16,0},{24,8},{1,17},{9,25},{17,1},{25,9},{2,18},{10... | collective-permute-start | bytes 393224 | tf_op jit(solution)/shard_map/ppermute | solution.py:224
  5.0 16.5 %collective-permute-start = (f32[2,1,2,8,1024]{4,3,2,0,1:T(8,128)S(1)}, f32[2,1,2,8,1024]{4,3,2,0,1:T(8,128)S(1)}, u32[]{:S(2)}, u32[]{:S(2)}) collective-permute-start(f32[2,1,2,8,1024]{4,3,2,0,1:T(8,128)S(1)} %reshape.146), channel_id=1, source_target_pairs={{0,8},{8,16},{16,24},{24,0},{1,9},{9,17},{17,25},{25,1},{2,10},{10... | collective-permute-start | bytes 393224 | tf_op jit(solution)/shard_map/ppermute | solution.py:224
  5.9 24.3 %collective-permute-start.4 = (f32[8,3,128]{2,1,0:T(4,128)S(1)}, f32[8,3,128]{2,1,0:T(4,128)S(1)}, u32[]{:S(2)}, u32[]{:S(2)}) collective-permute-start(f32[8,3,128]{2,1,0:T(4,128)S(1)} %copy.61), channel_id=1, source_target_pairs={{0,1},{1,0},{2,3},{3,2},{4,5},{5,4},{6,7},{7,6},{8,9},{9,8},{10,11... | collective-permute-start | bytes 36872 | tf_op jit(solution)/shard_map/ppermute | solution.py:207
  12.2 11.6 %copy-start.1 = (f32[9,16]{1,0:T(8,128)S(1)}, f32[9,16]{1,0:T(8,128)}, u32[]{:S(2)}) copy-start(f32[9,16]{1,0:T(8,128)} %param.13) | copy-start | bytes 1732
  21.4 7.6 %copy-start.4 = (s32[256,1]{0,1:T(1,128)S(1)}, s32[256,1]{0,1:T(1,128)}, u32[]{:S(2)}) copy-start(s32[256,1]{0,1:T(1,128)} %param.18) | copy-start | bytes 3076
  21.4 10.5 %copy-start.2 = (f32[2]{0:T(128)S(1)}, f32[2]{0:T(128)}, u32[]{:S(2)}) copy-start(f32[2]{0:T(128)} %param.12) | copy-start | bytes 28
  21.4 11.1 %copy-start.3 = (s32[256]{0:T(256)S(1)}, s32[256]{0:T(256)}, u32[]{:S(2)}) copy-start(s32[256]{0:T(256)} %param.19) | copy-start | bytes 3076
  22.2 47.9 %collective-permute-start.3 = (f32[2,32,128,128]{3,2,1,0:T(8,128)}, f32[2,32,128,128]{3,2,1,0:T(8,128)}, u32[]{:S(2)}, u32[]{:S(2)}) collective-permute-start(f32[2,32,128,128]{3,2,1,0:T(8,128)} %shard_map.113.refs_0_), channel_id=1, source_target_pairs={{0,24},{8,0},{16,8},{24,16},{1,25},{9,1},{17,9},{25,17},{2,26},{10... | collective-permute-start | bytes 12582920 | tf_op jit(solution)/shard_map/ppermute | solution.py:256
  30.2 4.0 %collective-permute-start.5 = (f32[16,3,128]{2,1,0:T(4,128)S(1)}, f32[16,3,128]{2,1,0:T(4,128)S(1)}, u32[]{:S(2)}, u32[]{:S(2)}) collective-permute-start(f32[16,3,128]{2,1,0:T(4,128)S(1)} %maximum_select_fusion.2), channel_id=1, source_target_pairs={{0,2},{1,3},{2,0},{3,1},{4,6},{5,7},{6,4},{7,5},{8,10},{9,11},{10,... | collective-permute-start | bytes 73736 | tf_op jit(solution)/shard_map/ppermute | solution.py:207
  34.2 5.2 %collective-permute-start.6 = (f32[32,3,128]{2,1,0:T(4,128)S(1)}, f32[32,3,128]{2,1,0:T(4,128)S(1)}, u32[]{:S(2)}, u32[]{:S(2)}) collective-permute-start(f32[32,3,128]{2,1,0:T(4,128)S(1)} %maximum_select_fusion.1), channel_id=1, source_target_pairs={{0,4},{1,5},{2,6},{3,7},{4,0},{5,1},{6,2},{7,3},{8,12},{9,13},{10,... | collective-permute-start | bytes 147464 | tf_op jit(solution)/shard_map/ppermute | solution.py:207

commit v8 on v7

--- a/solution.py
+++ b/solution.py
@@ -147,7 +147,7 @@
 
 
 def cross_spectra(rec_blocks, lig_yz, g_tables, gl, hx, sets, box, window, row_step):
-    part = rec_blocks[0].shape[1]
+    part = hx.shape[0] // 2
     size = rec_blocks[0].shape[2]
     lanes = rec_blocks[0].shape[3]
     blocks = len(rec_blocks)
@@ -249,11 +249,10 @@
     rz = block2(cos_n, -sin_n, sin_n, cos_n)
     ly = block2(cos_n, sin_n, -sin_n, cos_n)
     own = forward_planes(receptor, (rz, ly), plane_step, size)
-    full_box, outgoing = lax.optimization_barrier((full_box, own))
     rec_blocks = [own]
     for hop in range(1, extra + 1):
         pairs = [(i, (i - hop) % slab_count) for i in range(slab_count)]
-        rec_blocks.append(lax.ppermute(outgoing, "slab", perm=pairs))
+        rec_blocks.append(lax.ppermute(own, "slab", perm=pairs))
 
     lig = jnp.stack(
         [full_box[:, 0, 0] * channel_weight[0], full_box[:, 0, 1] * channel_weight[1]], axis=0

time: 105 us -> 98.8 us (0.941)
  waiting for transfers between devices: 16 us -> 12.7 us
  local copies, waits for them, and re-layouts: 7.66 us -> 5.9 us
  other arithmetic: 12.7 us -> 11.2 us
    ppermute x1, waiting for transfers between devices: 11.7 us -> 8.11 us  [score_grids(): rec_blocks.append(lax.ppermute(own, 'slab', perm=pairs))]
  transfers between devices with their start and end apart: 7 -> 7, of which waited for: 3 -> 3; matrix products, arithmetic and copies ran while one was open for 21% -> 19% of each run, Pallas kernels for 19% -> 21%
where the time goes in v8:
time: 98.8 us; the launch traced here: 97 us
  Pallas kernels  53.2 us (54%)
  waiting for transfers between devices  12.7 us (13%)
  other arithmetic  11.2 us (11%)
  starting transfers between devices  10.7 us (11%)
  local copies, waits for them, and re-layouts  5.9 us (6%)
  matrix products  2.39 us (2%)
  between operations  0.99 us (1%)
    pallas_call x1, Pallas kernels, cross_spectra(): pl.pallas_call(kernel, grid=(size // row_step,), in_specs=[pl.BlockSpec((...  21.4 us
    pallas_call x2, Pallas kernels, forward_planes(): pl.pallas_call(forward_plane_kernel, grid=(planes // plane_step,), in_spe...  20 us
    pallas_call x1, Pallas kernels, inverse_planes(): pl.pallas_call(inverse_plane_kernel, grid=(sets, planes // plane_step), i...  11.8 us
    ppermute x1, waiting for transfers between devices, score_grids(): rec_blocks.append(lax.ppermute(own, 'slab', perm=pairs))  8.11 us
    ppermute x3, starting transfers between devices, gather_pieces(): other = lax.ppermute(held, axis_name, perm=pairs)  5.85 us
    ppermute x3, waiting for transfers between devices, gather_pieces(): other = lax.ppermute(held, axis_name, perm=pairs)  4.61 us
    ppermute x3, starting transfers between devices, gather_direct(): held.append(lax.ppermute(piece, axis_name, perm=pairs))  3.26 us
    concatenate x4, other arithmetic, block2(): return jnp.concatenate([top, bottom], axis=0)  2.93 us
  transfers between devices with their start and end apart: 7, of which 3 were waited for; matrix products, arithmetic and copies ran while one was open for 19% of the time, Pallas kernels for 21%

profile of v8, /device:TPU:0, one launch (start us, length us, event | category | flops | bytes accessed | tf_op | source)
XLA Modules:
  0.0 97.0 jit_solution(12250227861542043770)
XLA Ops:
  0.6 1.3 %reshape.146 = f32[2,1,2,8,1024]{4,3,2,0,1:T(8,128)S(1)} reshape(f32[2,1,2,8,32,32]{5,4,3,2,1,0:T(8,128)} %param.11) | data formatting | bytes 262144 | tf_op jit(solution)/shard_map/reshape | solution.py:246
  1.9 2.5 %collective-permute-start.3 = (f32[2,1,2,8,1024]{4,3,2,0,1:T(8,128)S(1)}, f32[2,1,2,8,1024]{4,3,2,0,1:T(8,128)S(1)}, u32[]{:S(2)}, u32[]{:S(2)}) collective-permute-start(f32[2,1,2,8,1024]{4,3,2,0,1:T(8,128)S(1)} %reshape.146), channel_id=1, source_target_pairs={{0,24},{8,0},{16,8},{24,16},{1,25},{9,1},{17,9},{25,17},{2,26},{10... | collective-permute-start | bytes 393224 | tf_op jit(solution)/shard_map/ppermute | solution.py:224
  5.7 0.8 fusion.3
  6.6 9.3 %shard_map.113.refs_0_ = f32[2,32,128,128]{3,2,1,0:T(8,128)} custom-call(f32[2,32,128,128]{3,2,1,0:T(8,128)} %in_ref.1, f32[256,256]{1,0:T(8,128)} %get-tuple-element.17.rz_ref.ly_ref, f32[256,256]{1,0:T(8,128)} %get-tuple-element.16.ly_ref), custom_call_target="tpu_custom_call" | custom-call | tf_op jit(solution)/shard_map/pallas_call | solution.py:95
  15.9 1.6 %collective-permute-start = (f32[2,32,128,128]{3,2,1,0:T(8,128)}, f32[2,32,128,128]{3,2,1,0:T(8,128)}, u32[]{:S(2)}, u32[]{:S(2)}) collective-permute-start(f32[2,32,128,128]{3,2,1,0:T(8,128)} %shard_map.113.refs_0_), channel_id=1, source_target_pairs={{0,24},{8,0},{16,8},{24,16},{1,25},{9,1},{17,9},{25,17},{2,26},{10... | collective-permute-start | bytes 12582920 | tf_op jit(solution)/shard_map/ppermute | solution.py:255
  17.5 1.6 %collective-permute-start.4 = (f32[8,3,128]{2,1,0:T(4,128)S(1)}, f32[8,3,128]{2,1,0:T(4,128)S(1)}, u32[]{:S(2)}, u32[]{:S(2)}) collective-permute-start(f32[8,3,128]{2,1,0:T(4,128)S(1)} %copy.61), channel_id=1, source_target_pairs={{0,1},{1,0},{2,3},{3,2},{4,5},{5,4},{6,7},{7,6},{8,9},{9,8},{10,11... | collective-permute-start | bytes 36872 | tf_op jit(solution)/shard_map/ppermute | solution.py:207
  21.5 0.7 maximum_multiply_fusion.refs_5_
  22.3 0.7 gather_fusion.1
  23.1 0.7 maximum_maximum_fusion.3.refs_4_
  24.0 0.8 maximum_maximum_fusion.2.refs_3_
  25.0 0.7 pad_maximum_fusion.5.rz_ref
  25.6 0.8 maximum_maximum_fusion.ly_ref
  27.0 1.6 %collective-permute-start.5 = (f32[16,3,128]{2,1,0:T(4,128)S(1)}, f32[16,3,128]{2,1,0:T(4,128)S(1)}, u32[]{:S(2)}, u32[]{:S(2)}) collective-permute-start(f32[16,3,128]{2,1,0:T(4,128)S(1)} %maximum_select_fusion.2), channel_id=1, source_target_pairs={{0,2},{1,3},{2,0},{3,1},{4,6},{5,7},{6,4},{7,5},{8,10},{9,11},{10,... | collective-permute-start | bytes 73736 | tf_op jit(solution)/shard_map/ppermute | solution.py:207
  28.7 2.3 %collective-permute-done.5 = f32[16,3,128]{2,1,0:T(4,128)S(1)} collective-permute-done((f32[16,3,128]{2,1,0:T(4,128)S(1)}, f32[16,3,128]{2,1,0:T(4,128)S(1)}, u32[]{:S(2)}, u32[]{:S(2)}) %collective-permute-start.5) | collective-permute-done | bytes 24608 | tf_op jit(solution)/shard_map/ppermute | solution.py:207
  31.0 2.7 %collective-permute-start.6 = (f32[32,3,128]{2,1,0:T(4,128)S(1)}, f32[32,3,128]{2,1,0:T(4,128)S(1)}, u32[]{:S(2)}, u32[]{:S(2)}) collective-permute-start(f32[32,3,128]{2,1,0:T(4,128)S(1)} %maximum_select_fusion.1), channel_id=1, source_target_pairs={{0,4},{1,5},{2,6},{3,7},{4,0},{5,1},{6,2},{7,3},{8,12},{9,13},{10,... | collective-permute-start | bytes 147464 | tf_op jit(solution)/shard_map/ppermute | solution.py:207
  33.9 2.3 %collective-permute-done.6 = f32[32,3,128]{2,1,0:T(4,128)S(1)} collective-permute-done((f32[32,3,128]{2,1,0:T(4,128)S(1)}, f32[32,3,128]{2,1,0:T(4,128)S(1)}, u32[]{:S(2)}, u32[]{:S(2)}) %collective-permute-start.6) | collective-permute-done | bytes 49184 | tf_op jit(solution)/shard_map/ppermute | solution.py:207
  36.3 1.0 %gather_fusion.2 = f32[256,3,128]{2,1,0:T(4,128)S(1)} fusion(f32[64,3,128]{2,1,0:T(4,128)S(1)} %maximum_select_fusion, s32[1024]{0:T(1024)S(1)} %pad_clamp_fusion), kind=kCustom, calls=%fused_computation.2 | custom fusion | bytes 787456 | tf_op jit(solution)/shard_map/jit(_take)/gather | solution.py:309
  38.2 1.9 %fusion = f32[256,3,3]{2,1,0:T(4,128)S(1)} fusion(f32[256,3,128]{2,1,0:T(4,128)S(1)} %copy.65, f32[256,3,128]{2,1,0:T(4,128)S(1)} %gather_fusion.2, f32[256,3]{1,0:T(8,128)S(1)} %broadcast_multiply_fusion), kind=kOutput, calls=%fused_computation.7 | convolution fusion | flops 3637248 | bytes 798720 | tf_op jit(solution)/shard_map/pja,pka->pjk/dot_general | solution.py:315
  41.6 1.1 %slice_multiply_fusion.1 = (f32[2,1,1,32,1024]{4,3,0,2,1:T(8,128)S(1)}, f32[2,1,1,32,1024]{4,3,0,2,1:T(8,128)S(1)}) fusion(f32[2,1,2,32,1024]{4,3,0,2,1:T(8,128)S(1)} %copy_bitcast_fusion, f32[]{:T(128)} %bitcast.8, f32[]{:T(128)} %bitcast.9), kind=kLoop, calls=%fused_computation.17 | loop fusion | flops 131072 | bytes 1048584 | tf_op jit(solution)/shard_map/mul | solution.py:258
  43.4 1.6 %pad_maximum_fusion.in_ref = f32[2,64,32,32]{3,2,1,0:T(8,128)} fusion(f32[1,64,32,32]{3,2,1,0:T(8,128)S(1)} %mul.227, f32[1,64,32,32]{3,2,1,0:T(8,128)S(1)} %mul.224), kind=kLoop, calls=%fused_computation.3 | loop fusion | flops 131072 | bytes 1048576 | tf_op jit(solution)/shard_map/stack | solution.py:257
  45.1 10.7 %shard_map.114.refs_2_ = f32[2,64,128,128]{3,2,1,0:T(8,128)} custom-call(f32[2,64,32,32]{3,2,1,0:T(8,128)} %pad_maximum_fusion.in_ref, f32[64,256]{1,0:T(8,128)} %maximum_maximum_fusion.1.rz_ref, f32[256,64]{1,0:T(8,128)} %maximum_maximum_fusion.ly_ref), custom_call_target="tpu_custom_call" | custom-call | tf_op jit(solution)/shard_map/pallas_call | solution.py:95
  55.7 8.1 %collective-permute-done.refs_1_ = f32[2,32,128,128]{3,2,1,0:T(8,128)} collective-permute-done((f32[2,32,128,128]{3,2,1,0:T(8,128)}, f32[2,32,128,128]{3,2,1,0:T(8,128)}, u32[]{:S(2)}, u32[]{:S(2)}) %collective-permute-start) | collective-permute-done | bytes 4194336 | tf_op jit(solution)/shard_map/ppermute | solution.py:255
  63.8 21.4 %shard_map.115.in_ref = f32[2,2,32,128,128]{4,3,2,1,0:T(8,128)} custom-call(f32[2,32,128,128]{3,2,1,0:T(8,128)} %shard_map.113.refs_0_, f32[2,32,128,128]{3,2,1,0:T(8,128)} %collective-permute-done.refs_1_, f32[2,64,128,128]{3,2,1,0:T(8,128)} %shard_map.114.refs_2_, f32[128,128]{1,0:T(8,128)} %maximum_maximum_fusion.2.refs_3_, ...), custom_call_target="tpu_custom_call" | custom-call | tf_op jit(solution)/shard_map/pallas_call | solution.py:158
  85.3 11.8 %shard_map.116 = f32[2,32,128,128]{3,2,1,0:T(8,128)} custom-call(f32[2,2,32,128,128]{4,3,2,1,0:T(8,128)} %shard_map.115.in_ref, f32[256,256]{1,0:T(8,128)} %get-tuple-element.17.rz_ref.ly_ref, f32[256,128]{1,0:T(8,128)} %pad_maximum_fusion.5.rz_ref), custom_call_target="tpu_custom_call" | custom-call | tf_op jit(solution)/shard_map/pallas_call | solution.py:173
  (72 shorter events, 8.2 us)
Async XLA Ops:
  0.6 25.8 %copy-start = (f32[3,128]{1,0:T(4,128)S(1)}, f32[3,128]{1,0:T(4,128)}, u32[]{:S(2)}) copy-start(f32[3,128]{1,0:T(4,128)} %param.14) | copy-start | bytes 4612
  1.9 39.0 %collective-permute-start.3 = (f32[2,1,2,8,1024]{4,3,2,0,1:T(8,128)S(1)}, f32[2,1,2,8,1024]{4,3,2,0,1:T(8,128)S(1)}, u32[]{:S(2)}, u32[]{:S(2)}) collective-permute-start(f32[2,1,2,8,1024]{4,3,2,0,1:T(8,128)S(1)} %reshape.146), channel_id=1, source_target_pairs={{0,24},{8,0},{16,8},{24,16},{1,25},{9,1},{17,9},{25,17},{2,26},{10... | collective-permute-start | bytes 393224 | tf_op jit(solution)/shard_map/ppermute | solution.py:224
  4.4 36.5 %collective-permute-start.2 = (f32[2,1,2,8,1024]{4,3,2,0,1:T(8,128)S(1)}, f32[2,1,2,8,1024]{4,3,2,0,1:T(8,128)S(1)}, u32[]{:S(2)}, u32[]{:S(2)}) collective-permute-start(f32[2,1,2,8,1024]{4,3,2,0,1:T(8,128)S(1)} %reshape.146), channel_id=1, source_target_pairs={{0,16},{8,24},{16,0},{24,8},{1,17},{9,25},{17,1},{25,9},{2,18},{10... | collective-permute-start | bytes 393224 | tf_op jit(solution)/shard_map/ppermute | solution.py:224
  5.0 35.9 %collective-permute-start.1 = (f32[2,1,2,8,1024]{4,3,2,0,1:T(8,128)S(1)}, f32[2,1,2,8,1024]{4,3,2,0,1:T(8,128)S(1)}, u32[]{:S(2)}, u32[]{:S(2)}) collective-permute-start(f32[2,1,2,8,1024]{4,3,2,0,1:T(8,128)S(1)} %reshape.146), channel_id=1, source_target_pairs={{0,8},{8,16},{16,24},{24,0},{1,9},{9,17},{17,25},{25,1},{2,10},{10... | collective-permute-start | bytes 393224 | tf_op jit(solution)/shard_map/ppermute | solution.py:224
  6.6 11.0 %copy-start.2 = (f32[8,3,128]{2,0,1:T(8,128)S(1)}, f32[8,3,128]{2,0,1:T(8,128)}, u32[]{:S(2)}) copy-start(f32[8,3,128]{2,0,1:T(8,128)} %param.15) | copy-start | bytes 36868
  6.6 13.7 %copy-start.4 = (f32[2]{0:T(128)S(1)}, f32[2]{0:T(128)}, u32[]{:S(2)}) copy-start(f32[2]{0:T(128)} %param.12) | copy-start | bytes 28
  6.6 14.3 %copy-start.5 = (s32[256]{0:T(256)S(1)}, s32[256]{0:T(256)}, u32[]{:S(2)}) copy-start(s32[256]{0:T(256)} %param.16) | copy-start | bytes 3076
  6.6 14.3 %copy-start.8 = (s32[256]{0:T(256)S(1)}, s32[256]{0:T(256)}, u32[]{:S(2)}) copy-start(s32[256]{0:T(256)} %param.17) | copy-start | bytes 3076
  6.6 15.7 %copy-start.3 = (f32[9,16]{1,0:T(8,128)S(1)}, f32[9,16]{1,0:T(8,128)}, u32[]{:S(2)}) copy-start(f32[9,16]{1,0:T(8,128)} %param.13) | copy-start | bytes 1732
  6.6 19.8 %copy-start.7 = (s32[256,1]{0,1:T(1,128)S(1)}, s32[256,1]{0,1:T(1,128)}, u32[]{:S(2)}) copy-start(s32[256,1]{0,1:T(1,128)} %param.18) | copy-start | bytes 3076
  6.6 22.0 %copy-start.6 = (s32[256]{0:T(256)S(1)}, s32[256]{0:T(256)}, u32[]{:S(2)}) copy-start(s32[256]{0:T(256)} %param.19) | copy-start | bytes 3076
  6.6 27.1 %copy-start.1 = (f32[2,1,2,8,32,32]{5,4,3,2,1,0:T(8,128)S(1)}, f32[2,1,2,8,32,32]{5,4,3,2,1,0:T(8,128)}, u32[]{:S(2)}) copy-start(f32[2,1,2,8,32,32]{5,4,3,2,1,0:T(8,128)} %param.11) | copy-start | bytes 393220
  15.9 47.9 %collective-permute-start = (f32[2,32,128,128]{3,2,1,0:T(8,128)}, f32[2,32,128,128]{3,2,1,0:T(8,128)}, u32[]{:S(2)}, u32[]{:S(2)}) collective-permute-start(f32[2,32,128,128]{3,2,1,0:T(8,128)} %shard_map.113.refs_0_), channel_id=1, source_target_pairs={{0,24},{8,0},{16,8},{24,16},{1,25},{9,1},{17,9},{25,17},{2,26},{10... | collective-permute-start | bytes 12582920 | tf_op jit(solution)/shard_map/ppermute | solution.py:255
  17.5 9.5 %collective-permute-start.4 = (f32[8,3,128]{2,1,0:T(4,128)S(1)}, f32[8,3,128]{2,1,0:T(4,128)S(1)}, u32[]{:S(2)}, u32[]{:S(2)}) collective-permute-start(f32[8,3,128]{2,1,0:T(4,128)S(1)} %copy.61), channel_id=1, source_target_pairs={{0,1},{1,0},{2,3},{3,2},{4,5},{5,4},{6,7},{7,6},{8,9},{9,8},{10,11... | collective-permute-start | bytes 36872 | tf_op jit(solution)/shard_map/ppermute | solution.py:207
  27.0 4.0 %collective-permute-start.5 = (f32[16,3,128]{2,1,0:T(4,128)S(1)}, f32[16,3,128]{2,1,0:T(4,128)S(1)}, u32[]{:S(2)}, u32[]{:S(2)}) collective-permute-start(f32[16,3,128]{2,1,0:T(4,128)S(1)} %maximum_select_fusion.2), channel_id=1, source_target_pairs={{0,2},{1,3},{2,0},{3,1},{4,6},{5,7},{6,4},{7,5},{8,10},{9,11},{10,... | collective-permute-start | bytes 73736 | tf_op jit(solution)/shard_map/ppermute | solution.py:207
  31.0 5.2 %collective-permute-start.6 = (f32[32,3,128]{2,1,0:T(4,128)S(1)}, f32[32,3,128]{2,1,0:T(4,128)S(1)}, u32[]{:S(2)}, u32[]{:S(2)}) collective-permute-start(f32[32,3,128]{2,1,0:T(4,128)S(1)} %maximum_select_fusion.1), channel_id=1, source_target_pairs={{0,4},{1,5},{2,6},{3,7},{4,0},{5,1},{6,2},{7,3},{8,12},{9,13},{10,... | collective-permute-start | bytes 147464 | tf_op jit(solution)/shard_map/ppermute | solution.py:207

commit v9 on v8

--- a/solution.py
+++ b/solution.py
@@ -42,9 +42,9 @@
     return dot(b_high, a_high) + (dot(b_high, a_low) + dot(b_low, a_high))
 
 
-def forward_plane_kernel(in_ref, rz_ref, ly_ref, out_ref):
+def forward_plane_kernel(in_ref, rz_ref, ly_ref, *out_refs):
     planes, rows, cols = in_ref.shape[1], in_ref.shape[2], in_ref.shape[3]
-    size = out_ref.shape[3]
+    size = out_refs[0].shape[3]
     rz_hi, rz_lo = hi_lo(rz_ref[...])
     ly_hi, ly_lo = hi_lo(ly_ref[...])
     joined = jnp.concatenate(
@@ -62,18 +62,27 @@
         axis=1,
     )
     along_y = split_dot(stacked, ly_hi, ly_lo, False)
-    for p in range(planes):
-        out_ref[0, p] = along_y[:size, p * size : (p + 1) * size]
-        out_ref[1, p] = along_y[size:, p * size : (p + 1) * size]
-
-
-def inverse_plane_kernel(in_ref, ly_ref, rz_ref, out_ref):
-    planes = in_ref.shape[2]
-    size = in_ref.shape[4]
+    step = size // len(out_refs)
+    for q, out_ref in enumerate(out_refs):
+        for p in range(planes):
+            cols = slice(p * size, (p + 1) * size)
+            out_ref[0, p] = along_y[q * step : (q + 1) * step, cols]
+            out_ref[1, p] = along_y[size + q * step : size + (q + 1) * step, cols]
+
+
+def inverse_plane_kernel(*refs):
+    in_refs = refs[:-3]
+    ly_ref, rz_ref, out_ref = refs[-3:]
+    planes = in_refs[0].shape[2]
+    size = in_refs[0].shape[4]
     ly_hi, ly_lo = hi_lo(ly_ref[...])
     rz_hi, rz_lo = hi_lo(rz_ref[...])
+
+    def plane(c, p):
+        return jnp.concatenate([r[0, c, p] for r in in_refs], axis=0)
+
     stacked = jnp.concatenate(
-        [jnp.concatenate([in_ref[0, 0, p], in_ref[0, 1, p]], axis=0) for p in range(planes)], axis=1
+        [jnp.concatenate([plane(0, p), plane(1, p)], axis=0) for p in range(planes)], axis=1
     )
     along_y = split_dot(stacked, ly_hi, ly_lo, False)
     joined = jnp.concatenate(
@@ -89,16 +98,18 @@
     out_ref[0] = split_dot(joined, rz_hi, rz_lo, True).reshape(planes, size, size)
 
 
-def forward_planes(block, tables, plane_step, size):
+def forward_planes(block, tables, plane_step, size, splits=1):
     planes, rows, cols = block.shape[1], block.shape[2], block.shape[3]
     table_specs = [pl.BlockSpec(t.shape, lambda i: (0, 0)) for t in tables]
-    return pl.pallas_call(
+    step = size // splits
+    outs = pl.pallas_call(
         forward_plane_kernel,
         grid=(planes // plane_step,),
         in_specs=[pl.BlockSpec((2, plane_step, rows, cols), lambda i: (0, i, 0, 0))] + table_specs,
-        out_specs=pl.BlockSpec((2, plane_step, size, size), lambda i: (0, i, 0, 0)),
-        out_shape=jax.ShapeDtypeStruct((2, planes, size, size), F32),
+        out_specs=[pl.BlockSpec((2, plane_step, step, size), lambda i: (0, i, 0, 0))] * splits,
+        out_shape=[jax.ShapeDtypeStruct((2, planes, step, size), F32)] * splits,
     )(block, *tables)
+    return outs if splits > 1 else outs[0]
 
 
 def cross_kernel(*refs, blocks, sets, box, window, part):
@@ -146,9 +157,10 @@
             out_ref[s, c] = jnp.swapaxes(pieces, 0, 1)
 
 
-def cross_spectra(rec_blocks, lig_yz, g_tables, gl, hx, sets, box, window, row_step):
+def cross_spectra(rec_blocks, lig_yz, g_tables, gl, hx, sets, box, window, row_step, lig_from):
     part = hx.shape[0] // 2
     size = rec_blocks[0].shape[2]
+    offset = lig_from // row_step
     lanes = rec_blocks[0].shape[3]
     blocks = len(rec_blocks)
     tables = [jnp.concatenate(g_tables, axis=1), gl, hx]
@@ -159,7 +171,7 @@
         kernel,
         grid=(size // row_step,),
         in_specs=[pl.BlockSpec((2, b.shape[1], row_step, lanes), lambda i: (0, 0, i, 0)) for b in rec_blocks]
-        + [pl.BlockSpec((2, sets * box, row_step, lanes), lambda i: (0, 0, i, 0))]
+        + [pl.BlockSpec((2, sets * box, row_step, lanes), lambda i: (0, 0, i + offset, 0))]
         + [pl.BlockSpec(t.shape, lambda i: (0, 0)) for t in tables],
         out_specs=pl.BlockSpec((sets, 2, part, row_step, lanes), lambda i: (0, 0, 0, i, 0)),
         out_shape=jax.ShapeDtypeStruct((sets, 2, part, size, lanes), F32),
@@ -167,20 +179,20 @@
 
 
 def inverse_planes(spectra, tables, plane_step):
-    sets, planes, size = spectra.shape[0], spectra.shape[2], spectra.shape[4]
+    sets, planes, size = spectra[0].shape[0], spectra[0].shape[2], spectra[0].shape[4]
     ly_spec = pl.BlockSpec((2 * size, 2 * size), lambda s, i: (0, 0))
     rz_spec = pl.BlockSpec((2 * size, size), lambda s, i: (0, 0))
     return pl.pallas_call(
         inverse_plane_kernel,
         grid=(sets, planes // plane_step),
         in_specs=[
-            pl.BlockSpec((1, 2, plane_step, size, size), lambda s, i: (s, 0, i, 0, 0)),
-            ly_spec,
-            rz_spec,
-        ],
+            pl.BlockSpec((1, 2, plane_step, x.shape[3], size), lambda s, i: (s, 0, i, 0, 0))
+            for x in spectra
+        ]
+        + [ly_spec, rz_spec],
         out_specs=pl.BlockSpec((1, plane_step, size, size), lambda s, i: (s, i, 0, 0)),
         out_shape=jax.ShapeDtypeStruct((sets, planes, size, size), F32),
-    )(spectra, *tables)
+    )(*spectra, *tables)
 
 
 def gather_by_sum(piece, axis_name, dim):
@@ -248,11 +260,14 @@
     cos_n, sin_n = phase_tables(size, size, size)
     rz = block2(cos_n, -sin_n, sin_n, cos_n)
     ly = block2(cos_n, sin_n, -sin_n, cos_n)
-    own = forward_planes(receptor, (rz, ly), plane_step, size)
-    rec_blocks = [own]
+    splits = max(1, min(4, size // (2 * row_step)))
+    full_box, receptor = lax.optimization_barrier((full_box, receptor))
+    own = forward_planes(receptor, (rz, ly), plane_step, size, splits)
+    own = own if splits > 1 else [own]
+    arrived = []
     for hop in range(1, extra + 1):
         pairs = [(i, (i - hop) % slab_count) for i in range(slab_count)]
-        rec_blocks.append(lax.ppermute(own, "slab", perm=pairs))
+        arrived.append([lax.ppermute(rows, "slab", perm=pairs) for rows in own])
 
     lig = jnp.stack(
         [full_box[:, 0, 0] * channel_weight[0], full_box[:, 0, 1] * channel_weight[1]], axis=0
@@ -264,23 +279,27 @@
 
     cos_w, sin_w = phase_tables(window, window, window)
     g_tables = []
-    first = 0
-    for planes in rec_blocks:
-        cols = slice(first, first + planes.shape[1])
-        first += planes.shape[1]
+    for index in range(1 + extra):
+        cols = slice(index * part, (index + 1) * part)
         g_tables.append(block2(cos_w[:, cols], sin_w[:, cols], -sin_w[:, cols], cos_w[:, cols]))
     cos_xb, sin_xb = phase_tables(window, box, window)
     gl = block2(cos_xb, sin_xb, -sin_xb, cos_xb)
     cos_t, sin_t = phase_tables(part, window, window)
     scale = 1.0 / float(window * size * size)
     hx = block2(cos_t, -sin_t, sin_t, cos_t) * scale
-    back_x = cross_spectra(rec_blocks, lig_yz, g_tables, gl, hx, sets, box, window, row_step)
+    step = size // splits
+    back_x = []
+    for q in range(splits):
+        rec_blocks = [own[q]] + [hop_rows[q] for hop_rows in arrived]
+        back_x.append(
+            cross_spectra(rec_blocks, lig_yz, g_tables, gl, hx, sets, box, window, row_step, q * step)
+        )
 
     lyi = block2(cos_n, -sin_n, sin_n, cos_n)
     rzi = jnp.concatenate([cos_n, -sin_n], axis=0)
     inverse_tables = (lyi, rzi)
     grids = inverse_planes(back_x, inverse_tables, plane_step)
-    return grids.reshape(sets, 1, part, size, size)
+    return grids.reshape(sets, 1, part, size, size), own
 
 
 def pose_statistics(
@@ -330,7 +349,8 @@
     pose_member,
 ):
     size = receptor.shape[2]
-    scores = score_grids(receptor, ligand_box, channel_weight)
+    scores, own = score_grids(receptor, ligand_box, channel_weight)
+    cluster_center, own = lax.optimization_barrier((cluster_center, own))
     pose_stats = pose_statistics(
         rotation_table,
         ligand_atoms,

time: 98.8 us -> 104 us (1.053)
  waiting for transfers between devices: 12.7 us -> 0.03 us
  Pallas kernels: 53.2 us -> 60.7 us
  other arithmetic: 11.2 us -> 16.9 us
  local copies, waits for them, and re-layouts: 5.9 us -> 9.28 us
  starting transfers between devices: 10.7 us -> 12.5 us
    ppermute x1 -> x4, waiting for transfers between devices: 8.11 us -> 0.01 us  [score_grids(): arrived.append([lax.ppermute(rows, 'slab', perm=pairs) for rows in own])]
    pallas_call x1 -> x4, Pallas kernels: 21.4 us -> 29.1 us  [cross_spectra(): pl.pallas_call(kernel, grid=(size // row_step,), in_specs=[pl.BlockSpec((...]
    ppermute x3, waiting for transfers between devices: 4.61 us -> 0.01 us  [gather_pieces(): other = lax.ppermute(held, axis_name, perm=pairs)]
    select_n x3, other arithmetic: 0.06 us -> 3.12 us  [gather_pieces(): jnp.where(low_half, jnp.concatenate([held, other], axis=dim), jnp.concate...]
    unnamed x20 -> x11, local copies, waits for them, and re-layouts: 0.14 us -> 1.76 us
    ppermute x3, starting transfers between devices: 3.26 us -> 4.48 us  [gather_direct(): held.append(lax.ppermute(piece, axis_name, perm=pairs))]
    ppermute x1 -> x4, starting transfers between devices: 1.58 us -> 2.25 us  [score_grids(): arrived.append([lax.ppermute(rows, 'slab', perm=pairs) for rows in own])]
  transfers between devices with their start and end apart: 7 -> 10, of which waited for: 3 -> 0; matrix products, arithmetic and copies ran while one was open for 19% -> 25% of each run, Pallas kernels for 21% -> 32%
where the time goes in v9:
time: 104 us; the launch traced here: 103 us
  Pallas kernels  60.7 us (58%)
  other arithmetic  16.9 us (16%)
  starting transfers between devices  12.5 us (12%)
  local copies, waits for them, and re-layouts  9.28 us (9%)
  matrix products  2.39 us (2%)
    pallas_call x4, Pallas kernels, cross_spectra(): pl.pallas_call(kernel, grid=(size // row_step,), in_specs=[pl.BlockSpec((...  29.1 us
    pallas_call x2, Pallas kernels, forward_planes(): pl.pallas_call(forward_plane_kernel, grid=(planes // plane_step,), in_spe...  20 us
    pallas_call x1, Pallas kernels, inverse_planes(): pl.pallas_call(inverse_plane_kernel, grid=(sets, planes // plane_step), i...  11.7 us
    ppermute x3, starting transfers between devices, gather_pieces(): other = lax.ppermute(held, axis_name, perm=pairs)  5.72 us
    ppermute x3, starting transfers between devices, gather_direct(): held.append(lax.ppermute(piece, axis_name, perm=pairs))  4.48 us
    select_n x3, other arithmetic, gather_pieces(): jnp.where(low_half, jnp.concatenate([held, other], axis=dim), jnp.concate...  3.12 us
    concatenate x4, other arithmetic, block2(): return jnp.concatenate([top, bottom], axis=0)  2.92 us
    ppermute x4, starting transfers between devices, score_grids(): arrived.append([lax.ppermute(rows, 'slab', perm=pairs) for rows in own])  2.25 us
  transfers between devices with their start and end apart: 10, of which 0 were waited for; matrix products, arithmetic and copies ran while one was open for 25% of the time, Pallas kernels for 32%

profile of v9, /device:TPU:0, one launch (start us, length us, event | category | flops | bytes accessed | tf_op | source)
XLA Modules:
  0.0 102.7 jit_solution(7644944991978200307)
XLA Ops:
  0.7 1.3 %reshape.146 = f32[2,1,2,8,1024]{4,3,2,0,1:T(8,128)S(1)} reshape(f32[2,1,2,8,32,32]{5,4,3,2,1,0:T(8,128)} %param.11) | data formatting | bytes 262144 | tf_op jit(solution)/shard_map/reshape | solution.py:258
  2.5 2.6 %collective-permute-start.1 = (f32[2,1,2,8,1024]{4,3,2,0,1:T(8,128)S(1)}, f32[2,1,2,8,1024]{4,3,2,0,1:T(8,128)S(1)}, u32[]{:S(2)}, u32[]{:S(2)}) collective-permute-start(f32[2,1,2,8,1024]{4,3,2,0,1:T(8,128)S(1)} %reshape.146), channel_id=1, source_target_pairs={{0,16},{8,24},{16,0},{24,8},{1,17},{9,25},{17,1},{25,9},{2,18},{10... | collective-permute-start | bytes 393224 | tf_op jit(solution)/shard_map/ppermute | solution.py:236
  5.1 1.4 %collective-permute-start.2 = (f32[2,1,2,8,1024]{4,3,2,0,1:T(8,128)S(1)}, f32[2,1,2,8,1024]{4,3,2,0,1:T(8,128)S(1)}, u32[]{:S(2)}, u32[]{:S(2)}) collective-permute-start(f32[2,1,2,8,1024]{4,3,2,0,1:T(8,128)S(1)} %reshape.146), channel_id=1, source_target_pairs={{0,24},{8,0},{16,8},{24,16},{1,25},{9,1},{17,9},{25,17},{2,26},{10... | collective-permute-start | bytes 393224 | tf_op jit(solution)/shard_map/ppermute | solution.py:236
  12.2 1.3 %fusion.69 = (f32[1]{0:T(128)}, f32[1]{0:T(128)}) fusion(f32[2]{0:T(128)} %param.12), kind=kLoop, calls=%fused_computation.142 | loop fusion | bytes 16 | tf_op jit(solution)/shard_map/slice | solution.py:273
  18.6 0.8 fusion.3
  20.1 9.3 %shard_map.113 = (f32[2,32,32,128]{3,2,1,0:T(8,128)}, f32[2,32,32,128]{3,2,1,0:T(8,128)}, f32[2,32,32,128]{3,2,1,0:T(8,128)}, f32[2,32,32,128]{3,2,1,0:T(8,128)}) custom-call(f32[2,32,128,128]{3,2,1,0:T(8,128)} %in_ref, f32[256,256]{1,0:T(8,128)} %get-tuple-element.31.rz_ref.refs_4_, f32[256,256]{1,0:T(8,128)} %get-tuple-element.30.ly_ref), custom_call_target="tpu_custom_call" | custom-call | tf_op jit(solution)/shard_map/pallas_call | solution.py:105
  29.5 1.6 %collective-permute-start.7 = (f32[8,3,128]{2,1,0:T(4,128)S(1)}, f32[8,3,128]{2,1,0:T(4,128)S(1)}, u32[]{:S(2)}, u32[]{:S(2)}) collective-permute-start(f32[8,3,128]{2,1,0:T(4,128)S(1)} %copy.61), channel_id=1, source_target_pairs={{0,1},{1,0},{2,3},{3,2},{4,5},{5,4},{6,7},{7,6},{8,9},{9,8},{10,11... | collective-permute-start | bytes 36872 | tf_op jit(solution)/shard_map/ppermute | solution.py:219
  31.7 1.6 %collective-permute-start.3 = (f32[2,32,32,128]{3,2,1,0:T(8,128)}, f32[2,32,32,128]{3,2,1,0:T(8,128)S(1)}, u32[]{:S(2)}, u32[]{:S(2)}) collective-permute-start(f32[2,32,32,128]{3,2,1,0:T(8,128)} %get-tuple-element.10.refs_0_), channel_id=1, source_target_pairs={{0,24},{8,0},{16,8},{24,16},{1,25},{9,1},{17,9},{25,17},{2,26},{10... | collective-permute-start | bytes 3145736 | tf_op jit(solution)/shard_map/ppermute | solution.py:270
  33.9 1.6 %collective-permute-start.8 = (f32[16,3,128]{2,1,0:T(4,128)}, f32[16,3,128]{2,1,0:T(4,128)}, u32[]{:S(2)}, u32[]{:S(2)}) collective-permute-start(f32[16,3,128]{2,1,0:T(4,128)} %maximum_select_fusion.2), channel_id=1, source_target_pairs={{0,2},{1,3},{2,0},{3,1},{4,6},{5,7},{6,4},{7,5},{8,10},{9,11},{10,... | collective-permute-start | bytes 73736 | tf_op jit(solution)/shard_map/ppermute | solution.py:219
  35.5 1.9 %slice_multiply_fusion.1 = (f32[2,1,1,32,1024]{4,3,0,2,1:T(8,128)S(1)}, f32[2,1,1,32,1024]{4,3,0,2,1:T(8,128)}) fusion(f32[2,1,2,32,1024]{4,3,0,2,1:T(8,128)S(1)} %copy_bitcast_fusion, f32[]{:T(128)} %bitcast.8, f32[]{:T(128)} %bitcast.9), kind=kLoop, calls=%fused_computation.18 | loop fusion | flops 131072 | bytes 1048584 | tf_op jit(solution)/shard_map/mul | solution.py:273
  37.8 1.3 %mul.227 = f32[1,64,32,32]{3,2,1,0:T(8,128)S(1)} reshape(f32[2,1,1,32,1024]{4,3,0,2,1:T(8,128)} %get-tuple-element.29) | data formatting | bytes 524288 | tf_op jit(solution)/shard_map/mul | solution.py:273
  39.1 1.5 %maximum_select_fusion.1 = f32[32,3,128]{2,1,0:T(4,128)} fusion(f32[16,3,128]{2,1,0:T(4,128)} %collective-permute-done.8, f32[16,3,128]{2,1,0:T(4,128)} %maximum_select_fusion.2, pred[]{:T(512)S(6)} %eq.31), kind=kLoop, calls=%fused_computation.39 | loop fusion | flops 36864 | bytes 98305 | tf_op jit(solution)/shard_map/jit(_where)/select_n | solution.py:221
  40.6 2.6 %collective-permute-start.9 = (f32[32,3,128]{2,1,0:T(4,128)}, f32[32,3,128]{2,1,0:T(4,128)}, u32[]{:S(2)}, u32[]{:S(2)}) collective-permute-start(f32[32,3,128]{2,1,0:T(4,128)} %maximum_select_fusion.1), channel_id=1, source_target_pairs={{0,4},{1,5},{2,6},{3,7},{4,0},{5,1},{6,2},{7,3},{8,12},{9,13},{10,... | collective-permute-start | bytes 147464 | tf_op jit(solution)/shard_map/ppermute | solution.py:219
  43.2 1.5 %pad_maximum_fusion.in_ref = f32[2,64,32,32]{3,2,1,0:T(8,128)} fusion(f32[1,64,32,32]{3,2,1,0:T(8,128)S(1)} %mul.227, f32[1,64,32,32]{3,2,1,0:T(8,128)S(1)} %mul.224), kind=kLoop, calls=%fused_computation.3 | loop fusion | flops 131072 | bytes 1048576 | tf_op jit(solution)/shard_map/stack | solution.py:272
  44.7 10.7 %shard_map.114.refs_2_ = f32[2,64,128,128]{3,2,1,0:T(8,128)} custom-call(f32[2,64,32,32]{3,2,1,0:T(8,128)} %pad_maximum_fusion.in_ref, f32[64,256]{1,0:T(8,128)} %maximum_maximum_fusion.1.rz_ref, f32[256,64]{1,0:T(8,128)} %maximum_maximum_fusion.ly_ref), custom_call_target="tpu_custom_call" | custom-call | tf_op jit(solution)/shard_map/pallas_call | solution.py:105
  55.4 1.0 maximum_select_fusion
  56.4 1.0 gather_fusion.2
  58.3 1.9 %fusion = f32[256,3,3]{2,1,0:T(4,128)S(1)} fusion(f32[256,3,128]{2,1,0:T(4,128)S(1)} %copy.65, f32[256,3,128]{2,1,0:T(4,128)S(1)} %gather_fusion.2, f32[256,3]{1,0:T(8,128)S(1)} %broadcast_multiply_fusion), kind=kOutput, calls=%fused_computation.7 | convolution fusion | flops 3637248 | bytes 798720 | tf_op jit(solution)/shard_map/pja,pka->pjk/dot_general | solution.py:334
  61.0 7.3 %shard_map.118.refs_3_ = f32[2,2,32,32,128]{4,3,2,1,0:T(8,128)} custom-call(f32[2,32,32,128]{3,2,1,0:T(8,128)} %get-tuple-element.14.refs_0_, f32[2,32,32,128]{3,2,1,0:T(8,128)} %collective-permute-done.6.refs_1_, f32[2,64,128,128]{3,2,1,0:T(8,128)} %shard_map.114.refs_2_, f32[128,128]{1,0:T(8,128)} %maximum_maximum_fusion.2.refs_3_, ...), custom_call_target="tpu_custom_call" | custom-call | tf_op jit(solution)/shard_map/pallas_call | solution.py:170
  68.3 7.3 %shard_map.117.refs_2_ = f32[2,2,32,32,128]{4,3,2,1,0:T(8,128)} custom-call(f32[2,32,32,128]{3,2,1,0:T(8,128)} %get-tuple-element.13.refs_0_, f32[2,32,32,128]{3,2,1,0:T(8,128)} %collective-permute-done.5.refs_1_, f32[2,64,128,128]{3,2,1,0:T(8,128)} %shard_map.114.refs_2_, f32[128,128]{1,0:T(8,128)} %maximum_maximum_fusion.2.refs_3_, ...), custom_call_target="tpu_custom_call" | custom-call | tf_op jit(solution)/shard_map/pallas_call | solution.py:170
  75.6 7.3 %shard_map.116.refs_1_ = f32[2,2,32,32,128]{4,3,2,1,0:T(8,128)} custom-call(f32[2,32,32,128]{3,2,1,0:T(8,128)} %get-tuple-element.12.refs_0_, f32[2,32,32,128]{3,2,1,0:T(8,128)} %collective-permute-done.4.refs_1_, f32[2,64,128,128]{3,2,1,0:T(8,128)} %shard_map.114.refs_2_, f32[128,128]{1,0:T(8,128)} %maximum_maximum_fusion.2.refs_3_, ...), custom_call_target="tpu_custom_call" | custom-call | tf_op jit(solution)/shard_map/pallas_call | solution.py:170
  82.9 1.0 copy-done.2
  83.8 7.3 %shard_map.115.refs_0_ = f32[2,2,32,32,128]{4,3,2,1,0:T(8,128)} custom-call(f32[2,32,32,128]{3,2,1,0:T(8,128)} %get-tuple-element.10.refs_0_, f32[2,32,32,128]{3,2,1,0:T(8,128)} %copy-done.2, f32[2,64,128,128]{3,2,1,0:T(8,128)} %shard_map.114.refs_2_, f32[128,128]{1,0:T(8,128)} %maximum_maximum_fusion.2.refs_3_, f32[128,64]{1,0:T(8,128)} %maximum_maximum_fusion.3.refs_4_, ...), custom_call_target="tpu_custom_call" | custom-call | tf_op jit(solution)/shard_map/pallas_call | solution.py:170
  91.1 11.7 %shard_map.119 = f32[2,32,128,128]{3,2,1,0:T(8,128)} custom-call(f32[2,2,32,32,128]{4,3,2,1,0:T(8,128)} %shard_map.115.refs_0_, f32[2,2,32,32,128]{4,3,2,1,0:T(8,128)} %shard_map.116.refs_1_, f32[2,2,32,32,128]{4,3,2,1,0:T(8,128)} %shard_map.117.refs_2_, f32[2,2,32,32,128]{4,3,2,1,0:T(8,128)} %shard_map.118.refs_3_, ...), custom_call_target="tpu_custom_call" | custom-call | tf_op jit(solution)/shard_map/pallas_call | solution.py:185
  (73 shorter events, 15.3 us)
Async XLA Ops:
  0.6 13.6 %copy-start = (f32[3,128]{1,0:T(4,128)S(1)}, f32[3,128]{1,0:T(4,128)}, u32[]{:S(2)}) copy-start(f32[3,128]{1,0:T(4,128)} %param.14) | copy-start | bytes 4612
  0.6 17.7 %copy-start.1 = (f32[2,1,2,8,32,32]{5,4,3,2,1,0:T(8,128)S(1)}, f32[2,1,2,8,32,32]{5,4,3,2,1,0:T(8,128)}, u32[]{:S(2)}) copy-start(f32[2,1,2,8,32,32]{5,4,3,2,1,0:T(8,128)} %param.11) | copy-start | bytes 393220
  0.7 17.9 %copy-start.4 = (s32[256]{0:T(256)S(1)}, s32[256]{0:T(256)}, u32[]{:S(2)}) copy-start(s32[256]{0:T(256)} %param.19) | copy-start | bytes 3076
  2.0 17.4 %collective-permute-start = (f32[2,1,2,8,1024]{4,3,2,0,1:T(8,128)S(1)}, f32[2,1,2,8,1024]{4,3,2,0,1:T(8,128)S(1)}, u32[]{:S(2)}, u32[]{:S(2)}) collective-permute-start(f32[2,1,2,8,1024]{4,3,2,0,1:T(8,128)S(1)} %reshape.146), channel_id=1, source_target_pairs={{0,8},{8,16},{16,24},{24,0},{1,9},{9,17},{17,25},{25,1},{2,10},{10... | collective-permute-start | bytes 393224 | tf_op jit(solution)/shard_map/ppermute | solution.py:236
  2.5 16.9 %collective-permute-start.1 = (f32[2,1,2,8,1024]{4,3,2,0,1:T(8,128)S(1)}, f32[2,1,2,8,1024]{4,3,2,0,1:T(8,128)S(1)}, u32[]{:S(2)}, u32[]{:S(2)}) collective-permute-start(f32[2,1,2,8,1024]{4,3,2,0,1:T(8,128)S(1)} %reshape.146), channel_id=1, source_target_pairs={{0,16},{8,24},{16,0},{24,8},{1,17},{9,25},{17,1},{25,9},{2,18},{10... | collective-permute-start | bytes 393224 | tf_op jit(solution)/shard_map/ppermute | solution.py:236
  5.1 14.3 %collective-permute-start.2 = (f32[2,1,2,8,1024]{4,3,2,0,1:T(8,128)S(1)}, f32[2,1,2,8,1024]{4,3,2,0,1:T(8,128)S(1)}, u32[]{:S(2)}, u32[]{:S(2)}) collective-permute-start(f32[2,1,2,8,1024]{4,3,2,0,1:T(8,128)S(1)} %reshape.146), channel_id=1, source_target_pairs={{0,24},{8,0},{16,8},{24,16},{1,25},{9,1},{17,9},{25,17},{2,26},{10... | collective-permute-start | bytes 393224 | tf_op jit(solution)/shard_map/ppermute | solution.py:236
  20.1 9.3 %copy-start.3 = (f32[8,3,128]{2,0,1:T(8,128)S(1)}, f32[8,3,128]{2,0,1:T(8,128)}, u32[]{:S(2)}) copy-start(f32[8,3,128]{2,0,1:T(8,128)} %param.15) | copy-start | bytes 36868
  29.5 3.8 %collective-permute-start.7 = (f32[8,3,128]{2,1,0:T(4,128)S(1)}, f32[8,3,128]{2,1,0:T(4,128)S(1)}, u32[]{:S(2)}, u32[]{:S(2)}) collective-permute-start(f32[8,3,128]{2,1,0:T(4,128)S(1)} %copy.61), channel_id=1, source_target_pairs={{0,1},{1,0},{2,3},{3,2},{4,5},{5,4},{6,7},{7,6},{8,9},{9,8},{10,11... | collective-permute-start | bytes 36872 | tf_op jit(solution)/shard_map/ppermute | solution.py:219
  31.0 30.0 %collective-permute-start.6 = (f32[2,32,32,128]{3,2,1,0:T(8,128)}, f32[2,32,32,128]{3,2,1,0:T(8,128)}, u32[]{:S(2)}, u32[]{:S(2)}) collective-permute-start(f32[2,32,32,128]{3,2,1,0:T(8,128)} %get-tuple-element.14.refs_0_), channel_id=1, source_target_pairs={{0,24},{8,0},{16,8},{24,16},{1,25},{9,1},{17,9},{25,17},{2,26},{10... | collective-permute-start | bytes 3145736 | tf_op jit(solution)/shard_map/ppermute | solution.py:270
  31.0 37.2 %collective-permute-start.5 = (f32[2,32,32,128]{3,2,1,0:T(8,128)}, f32[2,32,32,128]{3,2,1,0:T(8,128)}, u32[]{:S(2)}, u32[]{:S(2)}) collective-permute-start(f32[2,32,32,128]{3,2,1,0:T(8,128)} %get-tuple-element.13.refs_0_), channel_id=1, source_target_pairs={{0,24},{8,0},{16,8},{24,16},{1,25},{9,1},{17,9},{25,17},{2,26},{10... | collective-permute-start | bytes 3145736 | tf_op jit(solution)/shard_map/ppermute | solution.py:270
  31.7 43.9 %collective-permute-start.4 = (f32[2,32,32,128]{3,2,1,0:T(8,128)}, f32[2,32,32,128]{3,2,1,0:T(8,128)}, u32[]{:S(2)}, u32[]{:S(2)}) collective-permute-start(f32[2,32,32,128]{3,2,1,0:T(8,128)} %get-tuple-element.12.refs_0_), channel_id=1, source_target_pairs={{0,24},{8,0},{16,8},{24,16},{1,25},{9,1},{17,9},{25,17},{2,26},{10... | collective-permute-start | bytes 3145736 | tf_op jit(solution)/shard_map/ppermute | solution.py:270
  31.7 51.1 %collective-permute-start.3 = (f32[2,32,32,128]{3,2,1,0:T(8,128)}, f32[2,32,32,128]{3,2,1,0:T(8,128)S(1)}, u32[]{:S(2)}, u32[]{:S(2)}) collective-permute-start(f32[2,32,32,128]{3,2,1,0:T(8,128)} %get-tuple-element.10.refs_0_), channel_id=1, source_target_pairs={{0,24},{8,0},{16,8},{24,16},{1,25},{9,1},{17,9},{25,17},{2,26},{10... | collective-permute-start | bytes 3145736 | tf_op jit(solution)/shard_map/ppermute | solution.py:270
  33.9 5.2 %collective-permute-start.8 = (f32[16,3,128]{2,1,0:T(4,128)}, f32[16,3,128]{2,1,0:T(4,128)}, u32[]{:S(2)}, u32[]{:S(2)}) collective-permute-start(f32[16,3,128]{2,1,0:T(4,128)} %maximum_select_fusion.2), channel_id=1, source_target_pairs={{0,2},{1,3},{2,0},{3,1},{4,6},{5,7},{6,4},{7,5},{8,10},{9,11},{10,... | collective-permute-start | bytes 73736 | tf_op jit(solution)/shard_map/ppermute | solution.py:219
  40.6 14.8 %collective-permute-start.9 = (f32[32,3,128]{2,1,0:T(4,128)}, f32[32,3,128]{2,1,0:T(4,128)}, u32[]{:S(2)}, u32[]{:S(2)}) collective-permute-start(f32[32,3,128]{2,1,0:T(4,128)} %maximum_select_fusion.1), channel_id=1, source_target_pairs={{0,4},{1,5},{2,6},{3,7},{4,0},{5,1},{6,2},{7,3},{8,12},{9,13},{10,... | collective-permute-start | bytes 147464 | tf_op jit(solution)/shard_map/ppermute | solution.py:219
  82.8 1.0 copy-start.2

commit v10 on v9

--- a/solution.py
+++ b/solution.py
@@ -260,8 +260,7 @@
     cos_n, sin_n = phase_tables(size, size, size)
     rz = block2(cos_n, -sin_n, sin_n, cos_n)
     ly = block2(cos_n, sin_n, -sin_n, cos_n)
-    splits = max(1, min(4, size // (2 * row_step)))
-    full_box, receptor = lax.optimization_barrier((full_box, receptor))
+    splits = max(1, min(2, size // (2 * row_step)))
     own = forward_planes(receptor, (rz, ly), plane_step, size, splits)
     own = own if splits > 1 else [own]
     arrived = []
@@ -299,7 +298,7 @@
     rzi = jnp.concatenate([cos_n, -sin_n], axis=0)
     inverse_tables = (lyi, rzi)
     grids = inverse_planes(back_x, inverse_tables, plane_step)
-    return grids.reshape(sets, 1, part, size, size), own
+    return grids.reshape(sets, 1, part, size, size), arrived[0][0]
 
 
 def pose_statistics(
@@ -349,8 +348,8 @@
     pose_member,
 ):
     size = receptor.shape[2]
-    scores, own = score_grids(receptor, ligand_box, channel_weight)
-    cluster_center, own = lax.optimization_barrier((cluster_center, own))
+    scores, first_rows = score_grids(receptor, ligand_box, channel_weight)
+    cluster_center, first_rows = lax.optimization_barrier((cluster_center, first_rows))
     pose_stats = pose_statistics(
         rotation_table,
         ligand_atoms,

time: 104 us -> 105 us (level)
  waiting for transfers between devices: 0.03 us -> 17.2 us
  other arithmetic: 16.9 us -> 11.3 us
  Pallas kernels: 60.7 us -> 55.7 us
  local copies, waits for them, and re-layouts: 9.28 us -> 6.01 us
  starting transfers between devices: 12.5 us -> 10.7 us
    ppermute x4 -> x2, waiting for transfers between devices: 0.01 us -> 14.8 us  [score_grids(): arrived.append([lax.ppermute(rows, 'slab', perm=pairs) for rows in own])]
    pallas_call x4 -> x2, Pallas kernels: 29.1 us -> 24.1 us  [cross_spectra(): pl.pallas_call(kernel, grid=(size // row_step,), in_specs=[pl.BlockSpec((...]
    select_n x3, other arithmetic: 3.12 us -> 0.06 us  [gather_pieces(): jnp.where(low_half, jnp.concatenate([held, other], axis=dim), jnp.concate...]
    ppermute x3, waiting for transfers between devices: 0.01 us -> 2.46 us  [gather_pieces(): other = lax.ppermute(held, axis_name, perm=pairs)]
    unnamed x11 -> x19, local copies, waits for them, and re-layouts: 1.76 us -> 0.13 us
    ppermute x3, starting transfers between devices: 4.48 us -> 3.26 us  [gather_direct(): held.append(lax.ppermute(piece, axis_name, perm=pairs))]
    ppermute x4 -> x2, starting transfers between devices: 2.25 us -> 1.64 us  [score_grids(): arrived.append([lax.ppermute(rows, 'slab', perm=pairs) for rows in own])]
  transfers between devices with their start and end apart: 10 -> 8, of which waited for: 0 -> 3; matrix products, arithmetic and copies ran while one was open for 25% -> 13% of each run, Pallas kernels for 32% -> 53%
where the time goes in v10:
time: 105 us; the launch traced here: 104 us
  Pallas kernels  55.7 us (53%)
  waiting for transfers between devices  17.2 us (16%)
  other arithmetic  11.3 us (11%)
  starting transfers between devices  10.7 us (10%)
  local copies, waits for them, and re-layouts  6.01 us (6%)
  matrix products  2.4 us (2%)
    pallas_call x2, Pallas kernels, cross_spectra(): pl.pallas_call(kernel, grid=(size // row_step,), in_specs=[pl.BlockSpec((...  24.1 us
    pallas_call x2, Pallas kernels, forward_planes(): pl.pallas_call(forward_plane_kernel, grid=(planes // plane_step,), in_spe...  20 us
    ppermute x2, waiting for transfers between devices, score_grids(): arrived.append([lax.ppermute(rows, 'slab', perm=pairs) for rows in own])  14.8 us
    pallas_call x1, Pallas kernels, inverse_planes(): pl.pallas_call(inverse_plane_kernel, grid=(sets, planes // plane_step), i...  11.7 us
    ppermute x3, starting transfers between devices, gather_pieces(): other = lax.ppermute(held, axis_name, perm=pairs)  5.78 us
    ppermute x3, starting transfers between devices, gather_direct(): held.append(lax.ppermute(piece, axis_name, perm=pairs))  3.26 us
    concatenate x4, other arithmetic, block2(): return jnp.concatenate([top, bottom], axis=0)  2.97 us
    ppermute x3, waiting for transfers between devices, gather_pieces(): other = lax.ppermute(held, axis_name, perm=pairs)  2.46 us
  transfers between devices with their start and end apart: 8, of which 3 were waited for; matrix products, arithmetic and copies ran while one was open for 13% of the time, Pallas kernels for 53%

profile of v10, /device:TPU:0, one launch (start us, length us, event | category | flops | bytes accessed | tf_op | source)
XLA Modules:
  0.0 104.4 jit_solution(14017906178368588529)
XLA Ops:
  0.6 1.3 %reshape.146 = f32[2,1,2,8,1024]{4,3,2,0,1:T(8,128)S(1)} reshape(f32[2,1,2,8,32,32]{5,4,3,2,1,0:T(8,128)} %param.11) | data formatting | bytes 262144 | tf_op jit(solution)/shard_map/reshape | solution.py:258
  1.9 2.5 %collective-permute-start.3 = (f32[2,1,2,8,1024]{4,3,2,0,1:T(8,128)S(1)}, f32[2,1,2,8,1024]{4,3,2,0,1:T(8,128)S(1)}, u32[]{:S(2)}, u32[]{:S(2)}) collective-permute-start(f32[2,1,2,8,1024]{4,3,2,0,1:T(8,128)S(1)} %reshape.146), channel_id=1, source_target_pairs={{0,24},{8,0},{16,8},{24,16},{1,25},{9,1},{17,9},{25,17},{2,26},{10... | collective-permute-start | bytes 393224 | tf_op jit(solution)/shard_map/ppermute | solution.py:236
  5.7 0.8 fusion.3
  6.6 9.3 %shard_map.113 = (f32[2,32,64,128]{3,2,1,0:T(8,128)}, f32[2,32,64,128]{3,2,1,0:T(8,128)}) custom-call(f32[2,32,128,128]{3,2,1,0:T(8,128)} %in_ref.1, f32[256,256]{1,0:T(8,128)} %get-tuple-element.23.rz_ref.refs_2_, f32[256,256]{1,0:T(8,128)} %get-tuple-element.22.ly_ref), custom_call_target="tpu_custom_call" | custom-call | tf_op jit(solution)/shard_map/pallas_call | solution.py:105
  15.9 1.6 %collective-permute-start = (f32[2,32,64,128]{3,2,1,0:T(8,128)}, f32[2,32,64,128]{3,2,1,0:T(8,128)}, u32[]{:S(2)}, u32[]{:S(2)}) collective-permute-start(f32[2,32,64,128]{3,2,1,0:T(8,128)} %get-tuple-element.5.refs_0_), channel_id=1, source_target_pairs={{0,24},{8,0},{16,8},{24,16},{1,25},{9,1},{17,9},{25,17},{2,26},{10... | collective-permute-start | bytes 6291464 | tf_op jit(solution)/shard_map/ppermute | solution.py:269
  18.2 0.7 fusion.69
  19.1 0.7 maximum_multiply_fusion.refs_5_
  20.9 0.7 maximum_maximum_fusion.3.refs_4_
  21.7 0.7 gather_fusion.1
  22.6 0.8 maximum_maximum_fusion.2.refs_3_
  25.2 0.8 maximum_maximum_fusion.ly_ref
  26.6 14.8 %collective-permute-done.refs_1_ = f32[2,32,64,128]{3,2,1,0:T(8,128)} collective-permute-done((f32[2,32,64,128]{3,2,1,0:T(8,128)}, f32[2,32,64,128]{3,2,1,0:T(8,128)}, u32[]{:S(2)}, u32[]{:S(2)}) %collective-permute-start) | collective-permute-done | bytes 2097184 | tf_op jit(solution)/shard_map/ppermute | solution.py:269
  41.4 1.5 %collective-permute-start.5 = (f32[8,3,128]{2,1,0:T(4,128)S(1)}, f32[8,3,128]{2,1,0:T(4,128)S(1)}, u32[]{:S(2)}, u32[]{:S(2)}) collective-permute-start(f32[8,3,128]{2,1,0:T(4,128)S(1)} %copy.61), channel_id=1, source_target_pairs={{0,1},{1,0},{2,3},{3,2},{4,5},{5,4},{6,7},{7,6},{8,9},{9,8},{10,11... | collective-permute-start | bytes 36872 | tf_op jit(solution)/shard_map/ppermute | solution.py:219
  42.9 2.2 %collective-permute-done.5 = f32[8,3,128]{2,1,0:T(4,128)S(1)} collective-permute-done((f32[8,3,128]{2,1,0:T(4,128)S(1)}, f32[8,3,128]{2,1,0:T(4,128)S(1)}, u32[]{:S(2)}, u32[]{:S(2)}) %collective-permute-start.5) | collective-permute-done | bytes 12320 | tf_op jit(solution)/shard_map/ppermute | solution.py:219
  45.1 1.6 %collective-permute-start.6 = (f32[16,3,128]{2,1,0:T(4,128)S(1)}, f32[16,3,128]{2,1,0:T(4,128)S(1)}, u32[]{:S(2)}, u32[]{:S(2)}) collective-permute-start(f32[16,3,128]{2,1,0:T(4,128)S(1)} %maximum_select_fusion.2), channel_id=1, source_target_pairs={{0,2},{1,3},{2,0},{3,1},{4,6},{5,7},{6,4},{7,5},{8,10},{9,11},{10,... | collective-permute-start | bytes 73736 | tf_op jit(solution)/shard_map/ppermute | solution.py:219
  46.8 1.4 %slice_multiply_fusion.1 = (f32[2,1,1,32,1024]{4,3,0,2,1:T(8,128)S(1)}, f32[2,1,1,32,1024]{4,3,0,2,1:T(8,128)S(1)}) fusion(f32[2,1,2,32,1024]{4,3,0,2,1:T(8,128)S(1)} %copy_bitcast_fusion, f32[]{:T(128)} %bitcast.8, f32[]{:T(128)} %bitcast.9), kind=kLoop, calls=%fused_computation.17 | loop fusion | flops 131072 | bytes 1048584 | tf_op jit(solution)/shard_map/mul | solution.py:272
  49.1 2.7 %collective-permute-start.7 = (f32[32,3,128]{2,1,0:T(4,128)S(1)}, f32[32,3,128]{2,1,0:T(4,128)S(1)}, u32[]{:S(2)}, u32[]{:S(2)}) collective-permute-start(f32[32,3,128]{2,1,0:T(4,128)S(1)} %maximum_select_fusion.1), channel_id=1, source_target_pairs={{0,4},{1,5},{2,6},{3,7},{4,0},{5,1},{6,2},{7,3},{8,12},{9,13},{10,... | collective-permute-start | bytes 147464 | tf_op jit(solution)/shard_map/ppermute | solution.py:219
  51.8 1.5 %pad_maximum_fusion.in_ref = f32[2,64,32,32]{3,2,1,0:T(8,128)} fusion(f32[1,64,32,32]{3,2,1,0:T(8,128)S(1)} %mul.227, f32[1,64,32,32]{3,2,1,0:T(8,128)S(1)} %mul.224), kind=kLoop, calls=%fused_computation.3 | loop fusion | flops 131072 | bytes 1048576 | tf_op jit(solution)/shard_map/stack | solution.py:271
  53.3 10.7 %shard_map.114.refs_2_ = f32[2,64,128,128]{3,2,1,0:T(8,128)} custom-call(f32[2,64,32,32]{3,2,1,0:T(8,128)} %pad_maximum_fusion.in_ref, f32[64,256]{1,0:T(8,128)} %maximum_maximum_fusion.1.rz_ref, f32[256,64]{1,0:T(8,128)} %maximum_maximum_fusion.ly_ref), custom_call_target="tpu_custom_call" | custom-call | tf_op jit(solution)/shard_map/pallas_call | solution.py:105
  64.0 12.0 %shard_map.115.refs_0_ = f32[2,2,32,64,128]{4,3,2,1,0:T(8,128)} custom-call(f32[2,32,64,128]{3,2,1,0:T(8,128)} %get-tuple-element.5.refs_0_, f32[2,32,64,128]{3,2,1,0:T(8,128)} %collective-permute-done.refs_1_, f32[2,64,128,128]{3,2,1,0:T(8,128)} %shard_map.114.refs_2_, f32[128,128]{1,0:T(8,128)} %maximum_maximum_fusion.2.refs_3_, ...), custom_call_target="tpu_custom_call" | custom-call | tf_op jit(solution)/shard_map/pallas_call | solution.py:170
  76.0 12.1 %shard_map.116.refs_1_ = f32[2,2,32,64,128]{4,3,2,1,0:T(8,128)} custom-call(f32[2,32,64,128]{3,2,1,0:T(8,128)} %get-tuple-element.6.refs_0_, f32[2,32,64,128]{3,2,1,0:T(8,128)} %collective-permute-done.4.refs_1_, f32[2,64,128,128]{3,2,1,0:T(8,128)} %shard_map.114.refs_2_, f32[128,128]{1,0:T(8,128)} %maximum_maximum_fusion.2.refs_3_, ...), custom_call_target="tpu_custom_call" | custom-call | tf_op jit(solution)/shard_map/pallas_call | solution.py:170
  88.0 11.7 %shard_map.117 = f32[2,32,128,128]{3,2,1,0:T(8,128)} custom-call(f32[2,2,32,64,128]{4,3,2,1,0:T(8,128)} %shard_map.115.refs_0_, f32[2,2,32,64,128]{4,3,2,1,0:T(8,128)} %shard_map.116.refs_1_, f32[256,256]{1,0:T(8,128)} %get-tuple-element.23.rz_ref.refs_2_, f32[256,128]{1,0:T(8,128)} %pad_maximum_fusion.5.refs_3_), custom_call_target="tpu_custom_call" | custom-call | tf_op jit(solution)/shard_map/pallas_call | solution.py:185
  99.8 1.0 gather_fusion.2
  101.7 1.9 %fusion = f32[256,3,3]{2,1,0:T(4,128)S(1)} fusion(f32[256,3,128]{2,1,0:T(4,128)S(1)} %copy.65, f32[256,3,128]{2,1,0:T(4,128)S(1)} %gather_fusion.2, f32[256,3]{1,0:T(8,128)S(1)} %broadcast_multiply_fusion), kind=kOutput, calls=%fused_computation.7 | convolution fusion | flops 3637248 | bytes 798720 | tf_op jit(solution)/shard_map/pja,pka->pjk/dot_general | solution.py:333
  (75 shorter events, 8.6 us)
Async XLA Ops:
  0.6 23.7 %copy-start = (f32[3,128]{1,0:T(4,128)S(1)}, f32[3,128]{1,0:T(4,128)}, u32[]{:S(2)}) copy-start(f32[3,128]{1,0:T(4,128)} %param.14) | copy-start | bytes 4612
  1.9 24.0 %collective-permute-start.3 = (f32[2,1,2,8,1024]{4,3,2,0,1:T(8,128)S(1)}, f32[2,1,2,8,1024]{4,3,2,0,1:T(8,128)S(1)}, u32[]{:S(2)}, u32[]{:S(2)}) collective-permute-start(f32[2,1,2,8,1024]{4,3,2,0,1:T(8,128)S(1)} %reshape.146), channel_id=1, source_target_pairs={{0,24},{8,0},{16,8},{24,16},{1,25},{9,1},{17,9},{25,17},{2,26},{10... | collective-permute-start | bytes 393224 | tf_op jit(solution)/shard_map/ppermute | solution.py:236
  4.4 21.6 %collective-permute-start.2 = (f32[2,1,2,8,1024]{4,3,2,0,1:T(8,128)S(1)}, f32[2,1,2,8,1024]{4,3,2,0,1:T(8,128)S(1)}, u32[]{:S(2)}, u32[]{:S(2)}) collective-permute-start(f32[2,1,2,8,1024]{4,3,2,0,1:T(8,128)S(1)} %reshape.146), channel_id=1, source_target_pairs={{0,16},{8,24},{16,0},{24,8},{1,17},{9,25},{17,1},{25,9},{2,18},{10... | collective-permute-start | bytes 393224 | tf_op jit(solution)/shard_map/ppermute | solution.py:236
  5.0 20.9 %collective-permute-start.1 = (f32[2,1,2,8,1024]{4,3,2,0,1:T(8,128)S(1)}, f32[2,1,2,8,1024]{4,3,2,0,1:T(8,128)S(1)}, u32[]{:S(2)}, u32[]{:S(2)}) collective-permute-start(f32[2,1,2,8,1024]{4,3,2,0,1:T(8,128)S(1)} %reshape.146), channel_id=1, source_target_pairs={{0,8},{8,16},{16,24},{24,0},{1,9},{9,17},{17,25},{25,1},{2,10},{10... | collective-permute-start | bytes 393224 | tf_op jit(solution)/shard_map/ppermute | solution.py:236
  6.6 11.6 %copy-start.7 = (s32[256,1]{0,1:T(1,128)S(1)}, s32[256,1]{0,1:T(1,128)}, u32[]{:S(2)}) copy-start(s32[256,1]{0,1:T(1,128)} %param.18) | copy-start | bytes 3076
  6.6 11.6 %copy-start.4 = (f32[2]{0:T(128)S(1)}, f32[2]{0:T(128)}, u32[]{:S(2)}) copy-start(f32[2]{0:T(128)} %param.12) | copy-start | bytes 28
  6.6 12.3 %copy-start.5 = (s32[256]{0:T(256)S(1)}, s32[256]{0:T(256)}, u32[]{:S(2)}) copy-start(s32[256]{0:T(256)} %param.19) | copy-start | bytes 3076
  6.6 12.3 %copy-start.8 = (s32[256]{0:T(256)S(1)}, s32[256]{0:T(256)}, u32[]{:S(2)}) copy-start(s32[256]{0:T(256)} %param.17) | copy-start | bytes 3076
  6.6 12.3 %copy-start.6 = (s32[256]{0:T(256)S(1)}, s32[256]{0:T(256)}, u32[]{:S(2)}) copy-start(s32[256]{0:T(256)} %param.16) | copy-start | bytes 3076
  6.6 15.0 %copy-start.3 = (f32[9,16]{1,0:T(8,128)S(1)}, f32[9,16]{1,0:T(8,128)}, u32[]{:S(2)}) copy-start(f32[9,16]{1,0:T(8,128)} %param.13) | copy-start | bytes 1732
  15.9 9.0 %copy-start.1 = (f32[2,1,2,8,32,32]{5,4,3,2,1,0:T(8,128)S(1)}, f32[2,1,2,8,32,32]{5,4,3,2,1,0:T(8,128)}, u32[]{:S(2)}) copy-start(f32[2,1,2,8,32,32]{5,4,3,2,1,0:T(8,128)} %param.11) | copy-start | bytes 393220
  15.9 25.5 %collective-permute-start = (f32[2,32,64,128]{3,2,1,0:T(8,128)}, f32[2,32,64,128]{3,2,1,0:T(8,128)}, u32[]{:S(2)}, u32[]{:S(2)}) collective-permute-start(f32[2,32,64,128]{3,2,1,0:T(8,128)} %get-tuple-element.5.refs_0_), channel_id=1, source_target_pairs={{0,24},{8,0},{16,8},{24,16},{1,25},{9,1},{17,9},{25,17},{2,26},{10... | collective-permute-start | bytes 6291464 | tf_op jit(solution)/shard_map/ppermute | solution.py:269
  17.5 58.5 %collective-permute-start.4 = (f32[2,32,64,128]{3,2,1,0:T(8,128)}, f32[2,32,64,128]{3,2,1,0:T(8,128)}, u32[]{:S(2)}, u32[]{:S(2)}) collective-permute-start(f32[2,32,64,128]{3,2,1,0:T(8,128)} %get-tuple-element.6.refs_0_), channel_id=1, source_target_pairs={{0,24},{8,0},{16,8},{24,16},{1,25},{9,1},{17,9},{25,17},{2,26},{10... | collective-permute-start | bytes 6291464 | tf_op jit(solution)/shard_map/ppermute | solution.py:269
  22.6 18.7 %copy-start.2 = (f32[8,3,128]{2,0,1:T(8,128)S(1)}, f32[8,3,128]{2,0,1:T(8,128)}, u32[]{:S(2)}) copy-start(f32[8,3,128]{2,0,1:T(8,128)} %param.15) | copy-start | bytes 36868
  41.4 3.7 %collective-permute-start.5 = (f32[8,3,128]{2,1,0:T(4,128)S(1)}, f32[8,3,128]{2,1,0:T(4,128)S(1)}, u32[]{:S(2)}, u32[]{:S(2)}) collective-permute-start(f32[8,3,128]{2,1,0:T(4,128)S(1)} %copy.61), channel_id=1, source_target_pairs={{0,1},{1,0},{2,3},{3,2},{4,5},{5,4},{6,7},{7,6},{8,9},{9,8},{10,11... | collective-permute-start | bytes 36872 | tf_op jit(solution)/shard_map/ppermute | solution.py:219
  45.1 4.0 %collective-permute-start.6 = (f32[16,3,128]{2,1,0:T(4,128)S(1)}, f32[16,3,128]{2,1,0:T(4,128)S(1)}, u32[]{:S(2)}, u32[]{:S(2)}) collective-permute-start(f32[16,3,128]{2,1,0:T(4,128)S(1)} %maximum_select_fusion.2), channel_id=1, source_target_pairs={{0,2},{1,3},{2,0},{3,1},{4,6},{5,7},{6,4},{7,5},{8,10},{9,11},{10,... | collective-permute-start | bytes 73736 | tf_op jit(solution)/shard_map/ppermute | solution.py:219
  49.1 50.6 %collective-permute-start.7 = (f32[32,3,128]{2,1,0:T(4,128)S(1)}, f32[32,3,128]{2,1,0:T(4,128)S(1)}, u32[]{:S(2)}, u32[]{:S(2)}) collective-permute-start(f32[32,3,128]{2,1,0:T(4,128)S(1)} %maximum_select_fusion.1), channel_id=1, source_target_pairs={{0,4},{1,5},{2,6},{3,7},{4,0},{5,1},{6,2},{7,3},{8,12},{9,13},{10,... | collective-permute-start | bytes 147464 | tf_op jit(solution)/shard_map/ppermute | solution.py:219

commit v11 on v10

--- a/solution.py
+++ b/solution.py
@@ -298,7 +298,7 @@
     rzi = jnp.concatenate([cos_n, -sin_n], axis=0)
     inverse_tables = (lyi, rzi)
     grids = inverse_planes(back_x, inverse_tables, plane_step)
-    return grids.reshape(sets, 1, part, size, size), arrived[0][0]
+    return grids.reshape(sets, 1, part, size, size), lig_yz
 
 
 def pose_statistics(

time: 105 us -> 94.1 us (0.90)
  waiting for transfers between devices: 17.2 us -> 6.37 us
    ppermute x2, waiting for transfers between devices: 14.8 us -> 0.01 us  [score_grids(): arrived.append([lax.ppermute(rows, 'slab', perm=pairs) for rows in own])]
    ppermute x3, waiting for transfers between devices: 2.46 us -> 6.35 us  [gather_pieces(): other = lax.ppermute(held, axis_name, perm=pairs)]
  transfers between devices with their start and end apart: 8 -> 8, of which waited for: 3 -> 3; matrix products, arithmetic and copies ran while one was open for 13% -> 20% of each run, Pallas kernels for 53% -> 34%
where the time goes in v11:
time: 94.1 us; the launch traced here: 93.5 us
  Pallas kernels  55.7 us (59%)
  other arithmetic  11.3 us (12%)
  starting transfers between devices  10.8 us (11%)
  waiting for transfers between devices  6.37 us (7%)
  local copies, waits for them, and re-layouts  6.01 us (6%)
  matrix products  2.39 us (3%)
    pallas_call x2, Pallas kernels, cross_spectra(): pl.pallas_call(kernel, grid=(size // row_step,), in_specs=[pl.BlockSpec((...  24.1 us
    pallas_call x2, Pallas kernels, forward_planes(): pl.pallas_call(forward_plane_kernel, grid=(planes // plane_step,), in_spe...  20 us
    pallas_call x1, Pallas kernels, inverse_planes(): pl.pallas_call(inverse_plane_kernel, grid=(sets, planes // plane_step), i...  11.7 us
    ppermute x3, waiting for transfers between devices, gather_pieces(): other = lax.ppermute(held, axis_name, perm=pairs)  6.35 us
    ppermute x3, starting transfers between devices, gather_pieces(): other = lax.ppermute(held, axis_name, perm=pairs)  5.85 us
    ppermute x3, starting transfers between devices, gather_direct(): held.append(lax.ppermute(piece, axis_name, perm=pairs))  3.26 us
    concatenate x4, other arithmetic, block2(): return jnp.concatenate([top, bottom], axis=0)  2.97 us
  transfers between devices with their start and end apart: 8, of which 3 were waited for; matrix products, arithmetic and copies ran while one was open for 20% of the time, Pallas kernels for 34%

profile of v11, /device:TPU:0, one launch (start us, length us, event | category | flops | bytes accessed | tf_op | source)
XLA Modules:
  0.0 93.5 jit_solution(8345956071407164572)
XLA Ops:
  0.6 1.3 %reshape.146 = f32[2,1,2,8,1024]{4,3,2,0,1:T(8,128)S(1)} reshape(f32[2,1,2,8,32,32]{5,4,3,2,1,0:T(8,128)} %param.11) | data formatting | bytes 262144 | tf_op jit(solution)/shard_map/reshape | solution.py:258
  1.9 2.5 %collective-permute-start.3 = (f32[2,1,2,8,1024]{4,3,2,0,1:T(8,128)S(1)}, f32[2,1,2,8,1024]{4,3,2,0,1:T(8,128)S(1)}, u32[]{:S(2)}, u32[]{:S(2)}) collective-permute-start(f32[2,1,2,8,1024]{4,3,2,0,1:T(8,128)S(1)} %reshape.146), channel_id=1, source_target_pairs={{0,24},{8,0},{16,8},{24,16},{1,25},{9,1},{17,9},{25,17},{2,26},{10... | collective-permute-start | bytes 393224 | tf_op jit(solution)/shard_map/ppermute | solution.py:236
  5.7 0.8 fusion.3
  6.6 9.3 %shard_map.113 = (f32[2,32,64,128]{3,2,1,0:T(8,128)}, f32[2,32,64,128]{3,2,1,0:T(8,128)}) custom-call(f32[2,32,128,128]{3,2,1,0:T(8,128)} %in_ref.1, f32[256,256]{1,0:T(8,128)} %get-tuple-element.23.rz_ref.refs_2_, f32[256,256]{1,0:T(8,128)} %get-tuple-element.22.ly_ref), custom_call_target="tpu_custom_call" | custom-call | tf_op jit(solution)/shard_map/pallas_call | solution.py:105
  15.9 1.6 %collective-permute-start = (f32[2,32,64,128]{3,2,1,0:T(8,128)}, f32[2,32,64,128]{3,2,1,0:T(8,128)}, u32[]{:S(2)}, u32[]{:S(2)}) collective-permute-start(f32[2,32,64,128]{3,2,1,0:T(8,128)} %get-tuple-element.5.refs_0_), channel_id=1, source_target_pairs={{0,24},{8,0},{16,8},{24,16},{1,25},{9,1},{17,9},{25,17},{2,26},{10... | collective-permute-start | bytes 6291464 | tf_op jit(solution)/shard_map/ppermute | solution.py:269
  20.4 0.7 gather_fusion.1
  22.0 0.7 maximum_maximum_fusion.3.refs_4_
  23.2 0.8 maximum_maximum_fusion.2.refs_3_
  24.2 0.8 maximum_maximum_fusion.ly_ref
  25.7 1.4 %slice_multiply_fusion.1 = (f32[2,1,1,32,1024]{4,3,0,2,1:T(8,128)S(1)}, f32[2,1,1,32,1024]{4,3,0,2,1:T(8,128)S(1)}) fusion(f32[2,1,2,32,1024]{4,3,0,2,1:T(8,128)S(1)} %copy_bitcast_fusion, f32[]{:T(128)} %bitcast.8, f32[]{:T(128)} %bitcast.9), kind=kLoop, calls=%fused_computation.17 | loop fusion | flops 131072 | bytes 1048584 | tf_op jit(solution)/shard_map/mul | solution.py:272
  27.8 1.5 %pad_maximum_fusion.in_ref = f32[2,64,32,32]{3,2,1,0:T(8,128)} fusion(f32[1,64,32,32]{3,2,1,0:T(8,128)S(1)} %mul.227, f32[1,64,32,32]{3,2,1,0:T(8,128)S(1)} %mul.224), kind=kLoop, calls=%fused_computation.3 | loop fusion | flops 131072 | bytes 1048576 | tf_op jit(solution)/shard_map/stack | solution.py:271
  29.3 10.7 %shard_map.114.refs_2_ = f32[2,64,128,128]{3,2,1,0:T(8,128)} custom-call(f32[2,64,32,32]{3,2,1,0:T(8,128)} %pad_maximum_fusion.in_ref, f32[64,256]{1,0:T(8,128)} %maximum_maximum_fusion.1.rz_ref, f32[256,64]{1,0:T(8,128)} %maximum_maximum_fusion.ly_ref), custom_call_target="tpu_custom_call" | custom-call | tf_op jit(solution)/shard_map/pallas_call | solution.py:105
  40.0 1.6 %collective-permute-start.5 = (f32[8,3,128]{2,1,0:T(4,128)S(1)}, f32[8,3,128]{2,1,0:T(4,128)S(1)}, u32[]{:S(2)}, u32[]{:S(2)}) collective-permute-start(f32[8,3,128]{2,1,0:T(4,128)S(1)} %copy.61), channel_id=1, source_target_pairs={{0,1},{1,0},{2,3},{3,2},{4,5},{5,4},{6,7},{7,6},{8,9},{9,8},{10,11... | collective-permute-start | bytes 36872 | tf_op jit(solution)/shard_map/ppermute | solution.py:219
  41.7 2.1 %collective-permute-done.5 = f32[8,3,128]{2,1,0:T(4,128)S(1)} collective-permute-done((f32[8,3,128]{2,1,0:T(4,128)S(1)}, f32[8,3,128]{2,1,0:T(4,128)S(1)}, u32[]{:S(2)}, u32[]{:S(2)}) %collective-permute-start.5) | collective-permute-done | bytes 12320 | tf_op jit(solution)/shard_map/ppermute | solution.py:219
  43.9 1.6 %collective-permute-start.6 = (f32[16,3,128]{2,1,0:T(4,128)S(1)}, f32[16,3,128]{2,1,0:T(4,128)S(1)}, u32[]{:S(2)}, u32[]{:S(2)}) collective-permute-start(f32[16,3,128]{2,1,0:T(4,128)S(1)} %maximum_select_fusion.2), channel_id=1, source_target_pairs={{0,2},{1,3},{2,0},{3,1},{4,6},{5,7},{6,4},{7,5},{8,10},{9,11},{10,... | collective-permute-start | bytes 73736 | tf_op jit(solution)/shard_map/ppermute | solution.py:219
  45.5 0.7 maximum_multiply_fusion.refs_5_
  46.2 1.6 %collective-permute-done.6 = f32[16,3,128]{2,1,0:T(4,128)S(1)} collective-permute-done((f32[16,3,128]{2,1,0:T(4,128)S(1)}, f32[16,3,128]{2,1,0:T(4,128)S(1)}, u32[]{:S(2)}, u32[]{:S(2)}) %collective-permute-start.6) | collective-permute-done | bytes 24608 | tf_op jit(solution)/shard_map/ppermute | solution.py:219
  47.9 2.7 %collective-permute-start.7 = (f32[32,3,128]{2,1,0:T(4,128)S(1)}, f32[32,3,128]{2,1,0:T(4,128)S(1)}, u32[]{:S(2)}, u32[]{:S(2)}) collective-permute-start(f32[32,3,128]{2,1,0:T(4,128)S(1)} %maximum_select_fusion.1), channel_id=1, source_target_pairs={{0,4},{1,5},{2,6},{3,7},{4,0},{5,1},{6,2},{7,3},{8,12},{9,13},{10,... | collective-permute-start | bytes 147464 | tf_op jit(solution)/shard_map/ppermute | solution.py:219
  50.5 2.6 %collective-permute-done.7 = f32[32,3,128]{2,1,0:T(4,128)S(1)} collective-permute-done((f32[32,3,128]{2,1,0:T(4,128)S(1)}, f32[32,3,128]{2,1,0:T(4,128)S(1)}, u32[]{:S(2)}, u32[]{:S(2)}) %collective-permute-start.7) | collective-permute-done | bytes 49184 | tf_op jit(solution)/shard_map/ppermute | solution.py:219
  53.1 1.0 %gather_fusion.2 = f32[256,3,128]{2,1,0:T(4,128)S(1)} fusion(f32[64,3,128]{2,1,0:T(4,128)S(1)} %maximum_select_fusion, s32[1024]{0:T(1024)S(1)} %pad_clamp_fusion), kind=kCustom, calls=%fused_computation.2 | custom fusion | bytes 787456 | tf_op jit(solution)/shard_map/jit(_take)/gather | solution.py:327
  55.1 1.9 %fusion = f32[256,3,3]{2,1,0:T(4,128)S(1)} fusion(f32[256,3,128]{2,1,0:T(4,128)S(1)} %copy.65, f32[256,3,128]{2,1,0:T(4,128)S(1)} %gather_fusion.2, f32[256,3]{1,0:T(8,128)S(1)} %broadcast_multiply_fusion), kind=kOutput, calls=%fused_computation.7 | convolution fusion | flops 3637248 | bytes 798720 | tf_op jit(solution)/shard_map/pja,pka->pjk/dot_general | solution.py:333
  57.7 12.0 %shard_map.115.refs_0_ = f32[2,2,32,64,128]{4,3,2,1,0:T(8,128)} custom-call(f32[2,32,64,128]{3,2,1,0:T(8,128)} %get-tuple-element.5.refs_0_, f32[2,32,64,128]{3,2,1,0:T(8,128)} %collective-permute-done.refs_1_, f32[2,64,128,128]{3,2,1,0:T(8,128)} %shard_map.114.refs_2_, f32[128,128]{1,0:T(8,128)} %maximum_maximum_fusion.2.refs_3_, ...), custom_call_target="tpu_custom_call" | custom-call | tf_op jit(solution)/shard_map/pallas_call | solution.py:170
  69.7 12.1 %shard_map.116.refs_1_ = f32[2,2,32,64,128]{4,3,2,1,0:T(8,128)} custom-call(f32[2,32,64,128]{3,2,1,0:T(8,128)} %get-tuple-element.6.refs_0_, f32[2,32,64,128]{3,2,1,0:T(8,128)} %collective-permute-done.4.refs_1_, f32[2,64,128,128]{3,2,1,0:T(8,128)} %shard_map.114.refs_2_, f32[128,128]{1,0:T(8,128)} %maximum_maximum_fusion.2.refs_3_, ...), custom_call_target="tpu_custom_call" | custom-call | tf_op jit(solution)/shard_map/pallas_call | solution.py:170
  81.8 11.7 %shard_map.117 = f32[2,32,128,128]{3,2,1,0:T(8,128)} custom-call(f32[2,2,32,64,128]{4,3,2,1,0:T(8,128)} %shard_map.115.refs_0_, f32[2,2,32,64,128]{4,3,2,1,0:T(8,128)} %shard_map.116.refs_1_, f32[256,256]{1,0:T(8,128)} %get-tuple-element.23.rz_ref.refs_2_, f32[256,128]{1,0:T(8,128)} %pad_maximum_fusion.5.refs_3_), custom_call_target="tpu_custom_call" | custom-call | tf_op jit(solution)/shard_map/pallas_call | solution.py:185
  (75 shorter events, 9.0 us)
Async XLA Ops:
  0.6 22.1 %copy-start = (f32[3,128]{1,0:T(4,128)S(1)}, f32[3,128]{1,0:T(4,128)}, u32[]{:S(2)}) copy-start(f32[3,128]{1,0:T(4,128)} %param.14) | copy-start | bytes 4612
  1.9 23.1 %collective-permute-start.3 = (f32[2,1,2,8,1024]{4,3,2,0,1:T(8,128)S(1)}, f32[2,1,2,8,1024]{4,3,2,0,1:T(8,128)S(1)}, u32[]{:S(2)}, u32[]{:S(2)}) collective-permute-start(f32[2,1,2,8,1024]{4,3,2,0,1:T(8,128)S(1)} %reshape.146), channel_id=1, source_target_pairs={{0,24},{8,0},{16,8},{24,16},{1,25},{9,1},{17,9},{25,17},{2,26},{10... | collective-permute-start | bytes 393224 | tf_op jit(solution)/shard_map/ppermute | solution.py:236
  4.4 20.6 %collective-permute-start.2 = (f32[2,1,2,8,1024]{4,3,2,0,1:T(8,128)S(1)}, f32[2,1,2,8,1024]{4,3,2,0,1:T(8,128)S(1)}, u32[]{:S(2)}, u32[]{:S(2)}) collective-permute-start(f32[2,1,2,8,1024]{4,3,2,0,1:T(8,128)S(1)} %reshape.146), channel_id=1, source_target_pairs={{0,16},{8,24},{16,0},{24,8},{1,17},{9,25},{17,1},{25,9},{2,18},{10... | collective-permute-start | bytes 393224 | tf_op jit(solution)/shard_map/ppermute | solution.py:236
  5.0 20.0 %collective-permute-start.1 = (f32[2,1,2,8,1024]{4,3,2,0,1:T(8,128)S(1)}, f32[2,1,2,8,1024]{4,3,2,0,1:T(8,128)S(1)}, u32[]{:S(2)}, u32[]{:S(2)}) collective-permute-start(f32[2,1,2,8,1024]{4,3,2,0,1:T(8,128)S(1)} %reshape.146), channel_id=1, source_target_pairs={{0,8},{8,16},{16,24},{24,0},{1,9},{9,17},{17,25},{25,1},{2,10},{10... | collective-permute-start | bytes 393224 | tf_op jit(solution)/shard_map/ppermute | solution.py:236
  6.6 13.0 %copy-start.4 = (f32[2]{0:T(128)S(1)}, f32[2]{0:T(128)}, u32[]{:S(2)}) copy-start(f32[2]{0:T(128)} %param.12) | copy-start | bytes 28
  6.6 13.7 %copy-start.3 = (f32[9,16]{1,0:T(8,128)S(1)}, f32[9,16]{1,0:T(8,128)}, u32[]{:S(2)}) copy-start(f32[9,16]{1,0:T(8,128)} %param.13) | copy-start | bytes 1732
  6.6 13.8 %copy-start.5 = (s32[256]{0:T(256)S(1)}, s32[256]{0:T(256)}, u32[]{:S(2)}) copy-start(s32[256]{0:T(256)} %param.16) | copy-start | bytes 3076
  6.6 14.6 %copy-start.8 = (s32[256]{0:T(256)S(1)}, s32[256]{0:T(256)}, u32[]{:S(2)}) copy-start(s32[256]{0:T(256)} %param.17) | copy-start | bytes 3076
  6.6 14.6 %copy-start.7 = (s32[256,1]{0,1:T(1,128)S(1)}, s32[256,1]{0,1:T(1,128)}, u32[]{:S(2)}) copy-start(s32[256,1]{0,1:T(1,128)} %param.18) | copy-start | bytes 3076
  15.9 8.1 %copy-start.1 = (f32[2,1,2,8,32,32]{5,4,3,2,1,0:T(8,128)S(1)}, f32[2,1,2,8,32,32]{5,4,3,2,1,0:T(8,128)}, u32[]{:S(2)}) copy-start(f32[2,1,2,8,32,32]{5,4,3,2,1,0:T(8,128)} %param.11) | copy-start | bytes 393220
  15.9 41.9 %collective-permute-start = (f32[2,32,64,128]{3,2,1,0:T(8,128)}, f32[2,32,64,128]{3,2,1,0:T(8,128)}, u32[]{:S(2)}, u32[]{:S(2)}) collective-permute-start(f32[2,32,64,128]{3,2,1,0:T(8,128)} %get-tuple-element.5.refs_0_), channel_id=1, source_target_pairs={{0,24},{8,0},{16,8},{24,16},{1,25},{9,1},{17,9},{25,17},{2,26},{10... | collective-permute-start | bytes 6291464 | tf_op jit(solution)/shard_map/ppermute | solution.py:269
  17.5 52.3 %collective-permute-start.4 = (f32[2,32,64,128]{3,2,1,0:T(8,128)}, f32[2,32,64,128]{3,2,1,0:T(8,128)}, u32[]{:S(2)}, u32[]{:S(2)}) collective-permute-start(f32[2,32,64,128]{3,2,1,0:T(8,128)} %get-tuple-element.6.refs_0_), channel_id=1, source_target_pairs={{0,24},{8,0},{16,8},{24,16},{1,25},{9,1},{17,9},{25,17},{2,26},{10... | collective-permute-start | bytes 6291464 | tf_op jit(solution)/shard_map/ppermute | solution.py:269
  29.3 10.7 %copy-start.2 = (f32[8,3,128]{2,0,1:T(8,128)S(1)}, f32[8,3,128]{2,0,1:T(8,128)}, u32[]{:S(2)}) copy-start(f32[8,3,128]{2,0,1:T(8,128)} %param.15) | copy-start | bytes 36868
  29.3 16.9 %copy-start.6 = (s32[256]{0:T(256)S(1)}, s32[256]{0:T(256)}, u32[]{:S(2)}) copy-start(s32[256]{0:T(256)} %param.19) | copy-start | bytes 3076
  40.0 3.8 %collective-permute-start.5 = (f32[8,3,128]{2,1,0:T(4,128)S(1)}, f32[8,3,128]{2,1,0:T(4,128)S(1)}, u32[]{:S(2)}, u32[]{:S(2)}) collective-permute-start(f32[8,3,128]{2,1,0:T(4,128)S(1)} %copy.61), channel_id=1, source_target_pairs={{0,1},{1,0},{2,3},{3,2},{4,5},{5,4},{6,7},{7,6},{8,9},{9,8},{10,11... | collective-permute-start | bytes 36872 | tf_op jit(solution)/shard_map/ppermute | solution.py:219
  43.9 4.0 %collective-permute-start.6 = (f32[16,3,128]{2,1,0:T(4,128)S(1)}, f32[16,3,128]{2,1,0:T(4,128)S(1)}, u32[]{:S(2)}, u32[]{:S(2)}) collective-permute-start(f32[16,3,128]{2,1,0:T(4,128)S(1)} %maximum_select_fusion.2), channel_id=1, source_target_pairs={{0,2},{1,3},{2,0},{3,1},{4,6},{5,7},{6,4},{7,5},{8,10},{9,11},{10,... | collective-permute-start | bytes 73736 | tf_op jit(solution)/shard_map/ppermute | solution.py:219
  47.9 5.2 %collective-permute-start.7 = (f32[32,3,128]{2,1,0:T(4,128)S(1)}, f32[32,3,128]{2,1,0:T(4,128)S(1)}, u32[]{:S(2)}, u32[]{:S(2)}) collective-permute-start(f32[32,3,128]{2,1,0:T(4,128)S(1)} %maximum_select_fusion.1), channel_id=1, source_target_pairs={{0,4},{1,5},{2,6},{3,7},{4,0},{5,1},{6,2},{7,3},{8,12},{9,13},{10,... | collective-permute-start | bytes 147464 | tf_op jit(solution)/shard_map/ppermute | solution.py:219

commit v12 on v11

--- a/solution.py
+++ b/solution.py
@@ -2,6 +2,7 @@
 
 import jax
 import jax.numpy as jnp
+import numpy as np
 from jax import lax
 from jax.experimental import pallas as pl
 from jax.experimental.pallas import tpu as pltpu
@@ -15,16 +16,15 @@
 
 
 def phase_tables(rows, cols, length):
-    row_index = lax.broadcasted_iota(jnp.int32, (rows, cols), 0)
-    col_index = lax.broadcasted_iota(jnp.int32, (rows, cols), 1)
-    phase = (row_index * col_index % length).astype(F32) * (TWO_PI / length)
-    return (jnp.cos(phase), jnp.sin(phase))
+    turns = np.outer(np.arange(rows), np.arange(cols)) % length
+    phase = turns.astype(np.float64) * (TWO_PI / length)
+    return (np.cos(phase), np.sin(phase))
 
 
 def block2(top_left, top_right, bottom_left, bottom_right):
-    top = jnp.concatenate([top_left, top_right], axis=1)
-    bottom = jnp.concatenate([bottom_left, bottom_right], axis=1)
-    return jnp.concatenate([top, bottom], axis=0)
+    top = np.concatenate([top_left, top_right], axis=1)
+    bottom = np.concatenate([bottom_left, bottom_right], axis=1)
+    return np.concatenate([top, bottom], axis=0).astype(np.float32)
 
 
 def hi_lo(table):
@@ -163,7 +163,7 @@
     offset = lig_from // row_step
     lanes = rec_blocks[0].shape[3]
     blocks = len(rec_blocks)
-    tables = [jnp.concatenate(g_tables, axis=1), gl, hx]
+    tables = [np.concatenate(g_tables, axis=1), gl, hx]
     kernel = functools.partial(
         cross_kernel, blocks=blocks, sets=sets, box=box, window=window, part=part
     )
@@ -285,7 +285,7 @@
     gl = block2(cos_xb, sin_xb, -sin_xb, cos_xb)
     cos_t, sin_t = phase_tables(part, window, window)
     scale = 1.0 / float(window * size * size)
-    hx = block2(cos_t, -sin_t, sin_t, cos_t) * scale
+    hx = (block2(cos_t, -sin_t, sin_t, cos_t) * scale).astype(np.float32)
     step = size // splits
     back_x = []
     for q in range(splits):
@@ -295,7 +295,7 @@
         )
 
     lyi = block2(cos_n, -sin_n, sin_n, cos_n)
-    rzi = jnp.concatenate([cos_n, -sin_n], axis=0)
+    rzi = np.concatenate([cos_n, -sin_n], axis=0).astype(np.float32)
     inverse_tables = (lyi, rzi)
     grids = inverse_planes(back_x, inverse_tables, plane_step)
     return grids.reshape(sets, 1, part, size, size), lig_yz

time: 94.1 us -> 88 us (0.935)
  other arithmetic: 11.3 us -> 4.13 us
    concatenate x6 -> x0, other arithmetic: 4.37 us -> none  [the longest x4 2.97 us: block2(): return jnp.concatenate([top, bottom], axis=0)]
    sin x6 -> x0, other arithmetic: 1.01 us -> none  [phase_tables(): return (jnp.cos(phase), jnp.sin(phase))]
  transfers between devices with their start and end apart: 8 -> 8, of which waited for: 3 -> 3; matrix products, arithmetic and copies ran while one was open for 20% -> 13% of each run, Pallas kernels for 34% -> 37%
where the time goes in v12:
time: 88 us; the launch traced here: 86.5 us
  Pallas kernels  55.7 us (63%)
  starting transfers between devices  10.7 us (12%)
  waiting for transfers between devices  6.61 us (8%)
  local copies, waits for them, and re-layouts  6.01 us (7%)
  other arithmetic  4.13 us (5%)
  matrix products  2.39 us (3%)
  between operations  0.9 us (1%)
    pallas_call x2, Pallas kernels, cross_spectra(): pl.pallas_call(kernel, grid=(size // row_step,), in_specs=[pl.BlockSpec((...  24.1 us
    pallas_call x2, Pallas kernels, forward_planes(): pl.pallas_call(forward_plane_kernel, grid=(planes // plane_step,), in_spe...  19.9 us
    pallas_call x1, Pallas kernels, inverse_planes(): pl.pallas_call(inverse_plane_kernel, grid=(sets, planes // plane_step), i...  11.7 us
    ppermute x3, waiting for transfers between devices, gather_pieces(): other = lax.ppermute(held, axis_name, perm=pairs)  6.6 us
    ppermute x3, starting transfers between devices, gather_pieces(): other = lax.ppermute(held, axis_name, perm=pairs)  5.85 us
    ppermute x3, starting transfers between devices, gather_direct(): held.append(lax.ppermute(piece, axis_name, perm=pairs))  3.26 us
    dot_general x1, matrix products, pose_statistics(): jnp.einsum('pja,pka->pjk', moved_centred, center_centred, precision=PRECISE)  1.87 us
  transfers between devices with their start and end apart: 8, of which 3 were waited for; matrix products, arithmetic and copies ran while one was open for 13% of the time, Pallas kernels for 37%

profile of v12, /device:TPU:0, one launch (start us, length us, event | category | flops | bytes accessed | tf_op | source)
XLA Modules:
  0.0 86.5 jit_solution(4755194582167470569)
XLA Ops:
  0.6 1.3 %reshape.146 = f32[2,1,2,8,1024]{4,3,2,0,1:T(8,128)S(1)} reshape(f32[2,1,2,8,32,32]{5,4,3,2,1,0:T(8,128)} %param.21) | data formatting | bytes 262144 | tf_op jit(solution)/shard_map/reshape | solution.py:258
  2.0 2.5 %collective-permute-start.3 = (f32[2,1,2,8,1024]{4,3,2,0,1:T(8,128)S(1)}, f32[2,1,2,8,1024]{4,3,2,0,1:T(8,128)S(1)}, u32[]{:S(2)}, u32[]{:S(2)}) collective-permute-start(f32[2,1,2,8,1024]{4,3,2,0,1:T(8,128)S(1)} %reshape.146), channel_id=1, source_target_pairs={{0,24},{8,0},{16,8},{24,16},{1,25},{9,1},{17,9},{25,17},{2,26},{10... | collective-permute-start | bytes 393224 | tf_op jit(solution)/shard_map/ppermute | solution.py:236
  4.4 0.6 collective-permute-start.2
  5.3 9.2 %shard_map.203 = (f32[2,32,64,128]{3,2,1,0:T(8,128)}, f32[2,32,64,128]{3,2,1,0:T(8,128)}) custom-call(f32[2,32,128,128]{3,2,1,0:T(8,128)} %in_ref.1, f32[256,256]{1,0:T(8,128)} %constant.153.clone.rz_ref.refs_2_, f32[256,256]{1,0:T(8,128)} %constant.154.clone.ly_ref), custom_call_target="tpu_custom_call" | custom-call | tf_op jit(solution)/shard_map/pallas_call | solution.py:105
  14.5 1.6 %collective-permute-start = (f32[2,32,64,128]{3,2,1,0:T(8,128)}, f32[2,32,64,128]{3,2,1,0:T(8,128)}, u32[]{:S(2)}, u32[]{:S(2)}) collective-permute-start(f32[2,32,64,128]{3,2,1,0:T(8,128)} %get-tuple-element.5.refs_0_), channel_id=1, source_target_pairs={{0,24},{8,0},{16,8},{24,16},{1,25},{9,1},{17,9},{25,17},{2,26},{10... | collective-permute-start | bytes 6291464 | tf_op jit(solution)/shard_map/ppermute | solution.py:269
  16.5 0.7 gather_fusion.1
  17.4 0.6 fusion.12
  18.1 0.6 gather_fusion
  18.7 1.3 %slice_multiply_fusion.1 = (f32[2,1,1,32,1024]{4,3,0,2,1:T(8,128)S(1)}, f32[2,1,1,32,1024]{4,3,0,2,1:T(8,128)S(1)}) fusion(f32[2,1,2,32,1024]{4,3,0,2,1:T(8,128)S(1)} %copy_bitcast_fusion, f32[]{:T(128)} %bitcast.8, f32[]{:T(128)} %bitcast.9), kind=kLoop, calls=%fused_computation.11 | loop fusion | flops 131072 | bytes 1048584 | tf_op jit(solution)/shard_map/mul | solution.py:272
  20.7 1.5 %pad_maximum_fusion.in_ref = f32[2,64,32,32]{3,2,1,0:T(8,128)} fusion(f32[1,64,32,32]{3,2,1,0:T(8,128)S(1)} %mul.51, f32[1,64,32,32]{3,2,1,0:T(8,128)S(1)} %mul.48), kind=kLoop, calls=%fused_computation.3 | loop fusion | flops 131072 | bytes 1048576 | tf_op jit(solution)/shard_map/stack | solution.py:271
  22.3 10.7 %shard_map.204.refs_2_ = f32[2,64,128,128]{3,2,1,0:T(8,128)} custom-call(f32[2,64,32,32]{3,2,1,0:T(8,128)} %pad_maximum_fusion.in_ref, f32[64,256]{1,0:T(8,128)} %constant.155.clone.rz_ref, f32[256,64]{1,0:T(8,128)} %constant.156.clone.ly_ref), custom_call_target="tpu_custom_call" | custom-call | tf_op jit(solution)/shard_map/pallas_call | solution.py:105
  33.0 1.6 %collective-permute-start.5 = (f32[8,3,128]{2,1,0:T(4,128)S(1)}, f32[8,3,128]{2,1,0:T(4,128)S(1)}, u32[]{:S(2)}, u32[]{:S(2)}) collective-permute-start(f32[8,3,128]{2,1,0:T(4,128)S(1)} %copy.71), channel_id=1, source_target_pairs={{0,1},{1,0},{2,3},{3,2},{4,5},{5,4},{6,7},{7,6},{8,9},{9,8},{10,11... | collective-permute-start | bytes 36872 | tf_op jit(solution)/shard_map/ppermute | solution.py:219
  34.5 0.5 convolution_add_fusion
  35.1 1.7 %collective-permute-done.5 = f32[8,3,128]{2,1,0:T(4,128)S(1)} collective-permute-done((f32[8,3,128]{2,1,0:T(4,128)S(1)}, f32[8,3,128]{2,1,0:T(4,128)S(1)}, u32[]{:S(2)}, u32[]{:S(2)}) %collective-permute-start.5) | collective-permute-done | bytes 12320 | tf_op jit(solution)/shard_map/ppermute | solution.py:219
  36.8 1.6 %collective-permute-start.6 = (f32[16,3,128]{2,1,0:T(4,128)S(1)}, f32[16,3,128]{2,1,0:T(4,128)S(1)}, u32[]{:S(2)}, u32[]{:S(2)}) collective-permute-start(f32[16,3,128]{2,1,0:T(4,128)S(1)} %maximum_select_fusion.2), channel_id=1, source_target_pairs={{0,2},{1,3},{2,0},{3,1},{4,6},{5,7},{6,4},{7,5},{8,10},{9,11},{10,... | collective-permute-start | bytes 73736 | tf_op jit(solution)/shard_map/ppermute | solution.py:219
  38.5 2.3 %collective-permute-done.6 = f32[16,3,128]{2,1,0:T(4,128)S(1)} collective-permute-done((f32[16,3,128]{2,1,0:T(4,128)S(1)}, f32[16,3,128]{2,1,0:T(4,128)S(1)}, u32[]{:S(2)}, u32[]{:S(2)}) %collective-permute-start.6) | collective-permute-done | bytes 24608 | tf_op jit(solution)/shard_map/ppermute | solution.py:219
  40.8 2.7 %collective-permute-start.7 = (f32[32,3,128]{2,1,0:T(4,128)S(1)}, f32[32,3,128]{2,1,0:T(4,128)S(1)}, u32[]{:S(2)}, u32[]{:S(2)}) collective-permute-start(f32[32,3,128]{2,1,0:T(4,128)S(1)} %maximum_select_fusion.1), channel_id=1, source_target_pairs={{0,4},{1,5},{2,6},{3,7},{4,0},{5,1},{6,2},{7,3},{8,12},{9,13},{10,... | collective-permute-start | bytes 147464 | tf_op jit(solution)/shard_map/ppermute | solution.py:219
  43.5 2.6 %collective-permute-done.7 = f32[32,3,128]{2,1,0:T(4,128)S(1)} collective-permute-done((f32[32,3,128]{2,1,0:T(4,128)S(1)}, f32[32,3,128]{2,1,0:T(4,128)S(1)}, u32[]{:S(2)}, u32[]{:S(2)}) %collective-permute-start.7) | collective-permute-done | bytes 49184 | tf_op jit(solution)/shard_map/ppermute | solution.py:219
  46.1 1.0 %gather_fusion.2 = f32[256,3,128]{2,1,0:T(4,128)S(1)} fusion(f32[64,3,128]{2,1,0:T(4,128)S(1)} %maximum_select_fusion, s32[1024]{0:T(1024)S(1)} %pad_clamp_fusion), kind=kCustom, calls=%fused_computation.2 | custom fusion | bytes 787456 | tf_op jit(solution)/shard_map/jit(_take)/gather | solution.py:327
  48.0 1.9 %fusion = f32[256,3,3]{2,1,0:T(4,128)S(1)} fusion(f32[256,3,128]{2,1,0:T(4,128)S(1)} %copy.75, f32[256,3,128]{2,1,0:T(4,128)S(1)} %gather_fusion.2, f32[256,3]{1,0:T(8,128)S(1)} %broadcast_multiply_fusion), kind=kOutput, calls=%fused_computation.7 | convolution fusion | flops 3637248 | bytes 798720 | tf_op jit(solution)/shard_map/pja,pka->pjk/dot_general | solution.py:333
  50.1 0.6 maximum_bitcast_fusion.1
  50.7 12.0 %shard_map.205.refs_0_ = f32[2,2,32,64,128]{4,3,2,1,0:T(8,128)} custom-call(f32[2,32,64,128]{3,2,1,0:T(8,128)} %get-tuple-element.5.refs_0_, f32[2,32,64,128]{3,2,1,0:T(8,128)} %collective-permute-done.refs_1_, f32[2,64,128,128]{3,2,1,0:T(8,128)} %shard_map.204.refs_2_, f32[128,128]{1,0:T(8,128)} %constant.157.clone.refs_3_, ...), custom_call_target="tpu_custom_call" | custom-call | tf_op jit(solution)/shard_map/pallas_call | solution.py:170
  62.7 12.1 %shard_map.206.refs_1_ = f32[2,2,32,64,128]{4,3,2,1,0:T(8,128)} custom-call(f32[2,32,64,128]{3,2,1,0:T(8,128)} %get-tuple-element.6.refs_0_, f32[2,32,64,128]{3,2,1,0:T(8,128)} %collective-permute-done.4.refs_1_, f32[2,64,128,128]{3,2,1,0:T(8,128)} %shard_map.204.refs_2_, f32[128,128]{1,0:T(8,128)} %constant.157.clone.refs_3_, ...), custom_call_target="tpu_custom_call" | custom-call | tf_op jit(solution)/shard_map/pallas_call | solution.py:170
  74.8 11.7 %shard_map.207 = f32[2,32,128,128]{3,2,1,0:T(8,128)} custom-call(f32[2,2,32,64,128]{4,3,2,1,0:T(8,128)} %shard_map.205.refs_0_, f32[2,2,32,64,128]{4,3,2,1,0:T(8,128)} %shard_map.206.refs_1_, f32[256,256]{1,0:T(8,128)} %constant.153.clone.rz_ref.refs_2_, f32[256,128]{1,0:T(8,128)} %constant.160.clone.refs_3_), custom_call_target="tpu_custom_call" | custom-call | tf_op jit(solution)/shard_map/pallas_call | solution.py:185
  (55 shorter events, 2.7 us)
Async XLA Ops:
  0.6 33.9 %copy-start = (f32[3,128]{1,0:T(4,128)S(1)}, f32[3,128]{1,0:T(4,128)}, u32[]{:S(2)}) copy-start(f32[3,128]{1,0:T(4,128)} %param.24) | copy-start | bytes 4612
  1.9 14.2 %copy-start.5 = (s32[256]{0:T(256)S(1)}, s32[256]{0:T(256)}, u32[]{:S(2)}) copy-start(s32[256]{0:T(256)} %param.26) | copy-start | bytes 3076
  1.9 14.2 %copy-start.8 = (s32[256]{0:T(256)S(1)}, s32[256]{0:T(256)}, u32[]{:S(2)}) copy-start(s32[256]{0:T(256)} %param.27) | copy-start | bytes 3076
  2.0 14.2 %copy-start.1 = (f32[2,1,2,8,32,32]{5,4,3,2,1,0:T(8,128)S(1)}, f32[2,1,2,8,32,32]{5,4,3,2,1,0:T(8,128)}, u32[]{:S(2)}) copy-start(f32[2,1,2,8,32,32]{5,4,3,2,1,0:T(8,128)} %param.21) | copy-start | bytes 393220
  2.0 14.5 %copy-start.3 = (f32[9,16]{1,0:T(8,128)S(1)}, f32[9,16]{1,0:T(8,128)}, u32[]{:S(2)}) copy-start(f32[9,16]{1,0:T(8,128)} %param.23) | copy-start | bytes 1732
  2.0 15.4 %copy-start.4 = (f32[2]{0:T(128)S(1)}, f32[2]{0:T(128)}, u32[]{:S(2)}) copy-start(f32[2]{0:T(128)} %param.22) | copy-start | bytes 28
  2.0 16.0 %collective-permute-start.3 = (f32[2,1,2,8,1024]{4,3,2,0,1:T(8,128)S(1)}, f32[2,1,2,8,1024]{4,3,2,0,1:T(8,128)S(1)}, u32[]{:S(2)}, u32[]{:S(2)}) collective-permute-start(f32[2,1,2,8,1024]{4,3,2,0,1:T(8,128)S(1)} %reshape.146), channel_id=1, source_target_pairs={{0,24},{8,0},{16,8},{24,16},{1,25},{9,1},{17,9},{25,17},{2,26},{10... | collective-permute-start | bytes 393224 | tf_op jit(solution)/shard_map/ppermute | solution.py:236
  4.4 13.6 %collective-permute-start.2 = (f32[2,1,2,8,1024]{4,3,2,0,1:T(8,128)S(1)}, f32[2,1,2,8,1024]{4,3,2,0,1:T(8,128)S(1)}, u32[]{:S(2)}, u32[]{:S(2)}) collective-permute-start(f32[2,1,2,8,1024]{4,3,2,0,1:T(8,128)S(1)} %reshape.146), channel_id=1, source_target_pairs={{0,16},{8,24},{16,0},{24,8},{1,17},{9,25},{17,1},{25,9},{2,18},{10... | collective-permute-start | bytes 393224 | tf_op jit(solution)/shard_map/ppermute | solution.py:236
  5.1 12.9 %collective-permute-start.1 = (f32[2,1,2,8,1024]{4,3,2,0,1:T(8,128)S(1)}, f32[2,1,2,8,1024]{4,3,2,0,1:T(8,128)S(1)}, u32[]{:S(2)}, u32[]{:S(2)}) collective-permute-start(f32[2,1,2,8,1024]{4,3,2,0,1:T(8,128)S(1)} %reshape.146), channel_id=1, source_target_pairs={{0,8},{8,16},{16,24},{24,0},{1,9},{9,17},{17,25},{25,1},{2,10},{10... | collective-permute-start | bytes 393224 | tf_op jit(solution)/shard_map/ppermute | solution.py:236
  14.5 36.2 %collective-permute-start = (f32[2,32,64,128]{3,2,1,0:T(8,128)}, f32[2,32,64,128]{3,2,1,0:T(8,128)}, u32[]{:S(2)}, u32[]{:S(2)}) collective-permute-start(f32[2,32,64,128]{3,2,1,0:T(8,128)} %get-tuple-element.5.refs_0_), channel_id=1, source_target_pairs={{0,24},{8,0},{16,8},{24,16},{1,25},{9,1},{17,9},{25,17},{2,26},{10... | collective-permute-start | bytes 6291464 | tf_op jit(solution)/shard_map/ppermute | solution.py:269
  16.1 46.6 %collective-permute-start.4 = (f32[2,32,64,128]{3,2,1,0:T(8,128)}, f32[2,32,64,128]{3,2,1,0:T(8,128)}, u32[]{:S(2)}, u32[]{:S(2)}) collective-permute-start(f32[2,32,64,128]{3,2,1,0:T(8,128)} %get-tuple-element.6.refs_0_), channel_id=1, source_target_pairs={{0,24},{8,0},{16,8},{24,16},{1,25},{9,1},{17,9},{25,17},{2,26},{10... | collective-permute-start | bytes 6291464 | tf_op jit(solution)/shard_map/ppermute | solution.py:269
  22.3 10.7 %copy-start.2 = (f32[8,3,128]{2,0,1:T(8,128)S(1)}, f32[8,3,128]{2,0,1:T(8,128)}, u32[]{:S(2)}) copy-start(f32[8,3,128]{2,0,1:T(8,128)} %param.25) | copy-start | bytes 36868
  22.3 16.2 %copy-start.7 = (s32[256,1]{0,1:T(1,128)S(1)}, s32[256,1]{0,1:T(1,128)}, u32[]{:S(2)}) copy-start(s32[256,1]{0,1:T(1,128)} %param.28) | copy-start | bytes 3076
  22.3 16.2 %copy-start.6 = (s32[256]{0:T(256)S(1)}, s32[256]{0:T(256)}, u32[]{:S(2)}) copy-start(s32[256]{0:T(256)} %param.29) | copy-start | bytes 3076
  33.0 3.8 %collective-permute-start.5 = (f32[8,3,128]{2,1,0:T(4,128)S(1)}, f32[8,3,128]{2,1,0:T(4,128)S(1)}, u32[]{:S(2)}, u32[]{:S(2)}) collective-permute-start(f32[8,3,128]{2,1,0:T(4,128)S(1)} %copy.71), channel_id=1, source_target_pairs={{0,1},{1,0},{2,3},{3,2},{4,5},{5,4},{6,7},{7,6},{8,9},{9,8},{10,11... | collective-permute-start | bytes 36872 | tf_op jit(solution)/shard_map/ppermute | solution.py:219
  36.8 4.0 %collective-permute-start.6 = (f32[16,3,128]{2,1,0:T(4,128)S(1)}, f32[16,3,128]{2,1,0:T(4,128)S(1)}, u32[]{:S(2)}, u32[]{:S(2)}) collective-permute-start(f32[16,3,128]{2,1,0:T(4,128)S(1)} %maximum_select_fusion.2), channel_id=1, source_target_pairs={{0,2},{1,3},{2,0},{3,1},{4,6},{5,7},{6,4},{7,5},{8,10},{9,11},{10,... | collective-permute-start | bytes 73736 | tf_op jit(solution)/shard_map/ppermute | solution.py:219
  40.8 5.2 %collective-permute-start.7 = (f32[32,3,128]{2,1,0:T(4,128)S(1)}, f32[32,3,128]{2,1,0:T(4,128)S(1)}, u32[]{:S(2)}, u32[]{:S(2)}) collective-permute-start(f32[32,3,128]{2,1,0:T(4,128)S(1)} %maximum_select_fusion.1), channel_id=1, source_target_pairs={{0,4},{1,5},{2,6},{3,7},{4,0},{5,1},{6,2},{7,3},{8,12},{9,13},{10,... | collective-permute-start | bytes 147464 | tf_op jit(solution)/shard_map/ppermute | solution.py:219

commit v13 on v12

--- a/solution.py
+++ b/solution.py
@@ -297,7 +297,7 @@
     lyi = block2(cos_n, -sin_n, sin_n, cos_n)
     rzi = np.concatenate([cos_n, -sin_n], axis=0).astype(np.float32)
     inverse_tables = (lyi, rzi)
-    grids = inverse_planes(back_x, inverse_tables, plane_step)
+    grids = inverse_planes(back_x, inverse_tables, min(2 * plane_step, part))
     return grids.reshape(sets, 1, part, size, size), lig_yz
 
 

time: 88 us -> 86.2 us (0.980)
  Pallas kernels: 55.7 us -> 54.2 us
    pallas_call x1, Pallas kernels: 11.7 us -> 10 us  [inverse_planes(): pl.pallas_call(inverse_plane_kernel, grid=(sets, planes // plane_step), i...]
  transfers between devices with their start and end apart: 8 -> 8, of which waited for: 3 -> 3; matrix products, arithmetic and copies ran while one was open for 13% -> 13% of each run, Pallas kernels for 37% -> 38%
where the time goes in v13:
time: 86.2 us; the launch traced here: 85 us
  Pallas kernels  54.2 us (63%)
  starting transfers between devices  10.7 us (12%)
  waiting for transfers between devices  6.61 us (8%)
  local copies, waits for them, and re-layouts  6.01 us (7%)
  other arithmetic  4.13 us (5%)
  matrix products  2.39 us (3%)
  between operations  0.91 us (1%)
    pallas_call x2, Pallas kernels, cross_spectra(): pl.pallas_call(kernel, grid=(size // row_step,), in_specs=[pl.BlockSpec((...  24.1 us
    pallas_call x2, Pallas kernels, forward_planes(): pl.pallas_call(forward_plane_kernel, grid=(planes // plane_step,), in_spe...  20.1 us
    pallas_call x1, Pallas kernels, inverse_planes(): pl.pallas_call(inverse_plane_kernel, grid=(sets, planes // plane_step), i...  10 us
    ppermute x3, waiting for transfers between devices, gather_pieces(): other = lax.ppermute(held, axis_name, perm=pairs)  6.6 us
    ppermute x3, starting transfers between devices, gather_pieces(): other = lax.ppermute(held, axis_name, perm=pairs)  5.85 us
    ppermute x3, starting transfers between devices, gather_direct(): held.append(lax.ppermute(piece, axis_name, perm=pairs))  3.26 us
    dot_general x1, matrix products, pose_statistics(): jnp.einsum('pja,pka->pjk', moved_centred, center_centred, precision=PRECISE)  1.87 us
  transfers between devices with their start and end apart: 8, of which 3 were waited for; matrix products, arithmetic and copies ran while one was open for 13% of the time, Pallas kernels for 38%

profile of v13, /device:TPU:0, one launch (start us, length us, event | category | flops | bytes accessed | tf_op | source)
XLA Modules:
  0.0 85.0 jit_solution(6942214199941668590)
XLA Ops:
  0.6 1.3 %reshape.146 = f32[2,1,2,8,1024]{4,3,2,0,1:T(8,128)S(1)} reshape(f32[2,1,2,8,32,32]{5,4,3,2,1,0:T(8,128)} %param.21) | data formatting | bytes 262144 | tf_op jit(solution)/shard_map/reshape | solution.py:258
  2.0 2.5 %collective-permute-start.3 = (f32[2,1,2,8,1024]{4,3,2,0,1:T(8,128)S(1)}, f32[2,1,2,8,1024]{4,3,2,0,1:T(8,128)S(1)}, u32[]{:S(2)}, u32[]{:S(2)}) collective-permute-start(f32[2,1,2,8,1024]{4,3,2,0,1:T(8,128)S(1)} %reshape.146), channel_id=1, source_target_pairs={{0,24},{8,0},{16,8},{24,16},{1,25},{9,1},{17,9},{25,17},{2,26},{10... | collective-permute-start | bytes 393224 | tf_op jit(solution)/shard_map/ppermute | solution.py:236
  4.4 0.6 collective-permute-start.2
  5.3 9.2 %shard_map.203 = (f32[2,32,64,128]{3,2,1,0:T(8,128)}, f32[2,32,64,128]{3,2,1,0:T(8,128)}) custom-call(f32[2,32,128,128]{3,2,1,0:T(8,128)} %in_ref.1, f32[256,256]{1,0:T(8,128)} %constant.153.clone.rz_ref.refs_2_, f32[256,256]{1,0:T(8,128)} %constant.154.clone.ly_ref), custom_call_target="tpu_custom_call" | custom-call | tf_op jit(solution)/shard_map/pallas_call | solution.py:105
  14.5 1.6 %collective-permute-start = (f32[2,32,64,128]{3,2,1,0:T(8,128)}, f32[2,32,64,128]{3,2,1,0:T(8,128)}, u32[]{:S(2)}, u32[]{:S(2)}) collective-permute-start(f32[2,32,64,128]{3,2,1,0:T(8,128)} %get-tuple-element.5.refs_0_), channel_id=1, source_target_pairs={{0,24},{8,0},{16,8},{24,16},{1,25},{9,1},{17,9},{25,17},{2,26},{10... | collective-permute-start | bytes 6291464 | tf_op jit(solution)/shard_map/ppermute | solution.py:269
  16.5 0.7 gather_fusion.1
  17.4 0.6 fusion.12
  18.1 0.6 gather_fusion
  18.7 1.3 %slice_multiply_fusion.1 = (f32[2,1,1,32,1024]{4,3,0,2,1:T(8,128)S(1)}, f32[2,1,1,32,1024]{4,3,0,2,1:T(8,128)S(1)}) fusion(f32[2,1,2,32,1024]{4,3,0,2,1:T(8,128)S(1)} %copy_bitcast_fusion, f32[]{:T(128)} %bitcast.8, f32[]{:T(128)} %bitcast.9), kind=kLoop, calls=%fused_computation.11 | loop fusion | flops 131072 | bytes 1048584 | tf_op jit(solution)/shard_map/mul | solution.py:272
  20.7 1.5 %pad_maximum_fusion.in_ref = f32[2,64,32,32]{3,2,1,0:T(8,128)} fusion(f32[1,64,32,32]{3,2,1,0:T(8,128)S(1)} %mul.51, f32[1,64,32,32]{3,2,1,0:T(8,128)S(1)} %mul.48), kind=kLoop, calls=%fused_computation.3 | loop fusion | flops 131072 | bytes 1048576 | tf_op jit(solution)/shard_map/stack | solution.py:271
  22.3 10.8 %shard_map.204.refs_2_ = f32[2,64,128,128]{3,2,1,0:T(8,128)} custom-call(f32[2,64,32,32]{3,2,1,0:T(8,128)} %pad_maximum_fusion.in_ref, f32[64,256]{1,0:T(8,128)} %constant.155.clone.rz_ref, f32[256,64]{1,0:T(8,128)} %constant.156.clone.ly_ref), custom_call_target="tpu_custom_call" | custom-call | tf_op jit(solution)/shard_map/pallas_call | solution.py:105
  33.1 1.6 %collective-permute-start.5 = (f32[8,3,128]{2,1,0:T(4,128)S(1)}, f32[8,3,128]{2,1,0:T(4,128)S(1)}, u32[]{:S(2)}, u32[]{:S(2)}) collective-permute-start(f32[8,3,128]{2,1,0:T(4,128)S(1)} %copy.71), channel_id=1, source_target_pairs={{0,1},{1,0},{2,3},{3,2},{4,5},{5,4},{6,7},{7,6},{8,9},{9,8},{10,11... | collective-permute-start | bytes 36872 | tf_op jit(solution)/shard_map/ppermute | solution.py:219
  34.7 0.5 convolution_add_fusion
  35.2 1.7 %collective-permute-done.5 = f32[8,3,128]{2,1,0:T(4,128)S(1)} collective-permute-done((f32[8,3,128]{2,1,0:T(4,128)S(1)}, f32[8,3,128]{2,1,0:T(4,128)S(1)}, u32[]{:S(2)}, u32[]{:S(2)}) %collective-permute-start.5) | collective-permute-done | bytes 12320 | tf_op jit(solution)/shard_map/ppermute | solution.py:219
  37.0 1.6 %collective-permute-start.6 = (f32[16,3,128]{2,1,0:T(4,128)S(1)}, f32[16,3,128]{2,1,0:T(4,128)S(1)}, u32[]{:S(2)}, u32[]{:S(2)}) collective-permute-start(f32[16,3,128]{2,1,0:T(4,128)S(1)} %maximum_select_fusion.2), channel_id=1, source_target_pairs={{0,2},{1,3},{2,0},{3,1},{4,6},{5,7},{6,4},{7,5},{8,10},{9,11},{10,... | collective-permute-start | bytes 73736 | tf_op jit(solution)/shard_map/ppermute | solution.py:219
  38.6 2.3 %collective-permute-done.6 = f32[16,3,128]{2,1,0:T(4,128)S(1)} collective-permute-done((f32[16,3,128]{2,1,0:T(4,128)S(1)}, f32[16,3,128]{2,1,0:T(4,128)S(1)}, u32[]{:S(2)}, u32[]{:S(2)}) %collective-permute-start.6) | collective-permute-done | bytes 24608 | tf_op jit(solution)/shard_map/ppermute | solution.py:219
  41.0 2.7 %collective-permute-start.7 = (f32[32,3,128]{2,1,0:T(4,128)S(1)}, f32[32,3,128]{2,1,0:T(4,128)S(1)}, u32[]{:S(2)}, u32[]{:S(2)}) collective-permute-start(f32[32,3,128]{2,1,0:T(4,128)S(1)} %maximum_select_fusion.1), channel_id=1, source_target_pairs={{0,4},{1,5},{2,6},{3,7},{4,0},{5,1},{6,2},{7,3},{8,12},{9,13},{10,... | collective-permute-start | bytes 147464 | tf_op jit(solution)/shard_map/ppermute | solution.py:219
  43.6 2.6 %collective-permute-done.7 = f32[32,3,128]{2,1,0:T(4,128)S(1)} collective-permute-done((f32[32,3,128]{2,1,0:T(4,128)S(1)}, f32[32,3,128]{2,1,0:T(4,128)S(1)}, u32[]{:S(2)}, u32[]{:S(2)}) %collective-permute-start.7) | collective-permute-done | bytes 49184 | tf_op jit(solution)/shard_map/ppermute | solution.py:219
  46.2 1.0 %gather_fusion.2 = f32[256,3,128]{2,1,0:T(4,128)S(1)} fusion(f32[64,3,128]{2,1,0:T(4,128)S(1)} %maximum_select_fusion, s32[1024]{0:T(1024)S(1)} %pad_clamp_fusion), kind=kCustom, calls=%fused_computation.2 | custom fusion | bytes 787456 | tf_op jit(solution)/shard_map/jit(_take)/gather | solution.py:327
  48.2 1.9 %fusion = f32[256,3,3]{2,1,0:T(4,128)S(1)} fusion(f32[256,3,128]{2,1,0:T(4,128)S(1)} %copy.75, f32[256,3,128]{2,1,0:T(4,128)S(1)} %gather_fusion.2, f32[256,3]{1,0:T(8,128)S(1)} %broadcast_multiply_fusion), kind=kOutput, calls=%fused_computation.7 | convolution fusion | flops 3637248 | bytes 798720 | tf_op jit(solution)/shard_map/pja,pka->pjk/dot_general | solution.py:333
  50.2 0.6 maximum_bitcast_fusion.1
  50.8 12.0 %shard_map.205.refs_0_ = f32[2,2,32,64,128]{4,3,2,1,0:T(8,128)} custom-call(f32[2,32,64,128]{3,2,1,0:T(8,128)} %get-tuple-element.5.refs_0_, f32[2,32,64,128]{3,2,1,0:T(8,128)} %collective-permute-done.refs_1_, f32[2,64,128,128]{3,2,1,0:T(8,128)} %shard_map.204.refs_2_, f32[128,128]{1,0:T(8,128)} %constant.157.clone.refs_3_, ...), custom_call_target="tpu_custom_call" | custom-call | tf_op jit(solution)/shard_map/pallas_call | solution.py:170
  62.9 12.1 %shard_map.206.refs_1_ = f32[2,2,32,64,128]{4,3,2,1,0:T(8,128)} custom-call(f32[2,32,64,128]{3,2,1,0:T(8,128)} %get-tuple-element.6.refs_0_, f32[2,32,64,128]{3,2,1,0:T(8,128)} %collective-permute-done.4.refs_1_, f32[2,64,128,128]{3,2,1,0:T(8,128)} %shard_map.204.refs_2_, f32[128,128]{1,0:T(8,128)} %constant.157.clone.refs_3_, ...), custom_call_target="tpu_custom_call" | custom-call | tf_op jit(solution)/shard_map/pallas_call | solution.py:170
  74.9 10.0 %shard_map.207 = f32[2,32,128,128]{3,2,1,0:T(8,128)} custom-call(f32[2,2,32,64,128]{4,3,2,1,0:T(8,128)} %shard_map.205.refs_0_, f32[2,2,32,64,128]{4,3,2,1,0:T(8,128)} %shard_map.206.refs_1_, f32[256,256]{1,0:T(8,128)} %constant.153.clone.rz_ref.refs_2_, f32[256,128]{1,0:T(8,128)} %constant.160.clone.refs_3_), custom_call_target="tpu_custom_call" | custom-call | tf_op jit(solution)/shard_map/pallas_call | solution.py:185
  (55 shorter events, 2.7 us)
Async XLA Ops:
  0.6 34.1 %copy-start = (f32[3,128]{1,0:T(4,128)S(1)}, f32[3,128]{1,0:T(4,128)}, u32[]{:S(2)}) copy-start(f32[3,128]{1,0:T(4,128)} %param.24) | copy-start | bytes 4612
  1.9 14.2 %copy-start.5 = (s32[256]{0:T(256)S(1)}, s32[256]{0:T(256)}, u32[]{:S(2)}) copy-start(s32[256]{0:T(256)} %param.26) | copy-start | bytes 3076
  1.9 14.2 %copy-start.8 = (s32[256]{0:T(256)S(1)}, s32[256]{0:T(256)}, u32[]{:S(2)}) copy-start(s32[256]{0:T(256)} %param.27) | copy-start | bytes 3076
  2.0 14.2 %copy-start.1 = (f32[2,1,2,8,32,32]{5,4,3,2,1,0:T(8,128)S(1)}, f32[2,1,2,8,32,32]{5,4,3,2,1,0:T(8,128)}, u32[]{:S(2)}) copy-start(f32[2,1,2,8,32,32]{5,4,3,2,1,0:T(8,128)} %param.21) | copy-start | bytes 393220
  2.0 14.5 %copy-start.3 = (f32[9,16]{1,0:T(8,128)S(1)}, f32[9,16]{1,0:T(8,128)}, u32[]{:S(2)}) copy-start(f32[9,16]{1,0:T(8,128)} %param.23) | copy-start | bytes 1732
  2.0 15.4 %copy-start.4 = (f32[2]{0:T(128)S(1)}, f32[2]{0:T(128)}, u32[]{:S(2)}) copy-start(f32[2]{0:T(128)} %param.22) | copy-start | bytes 28
  2.0 16.0 %collective-permute-start.3 = (f32[2,1,2,8,1024]{4,3,2,0,1:T(8,128)S(1)}, f32[2,1,2,8,1024]{4,3,2,0,1:T(8,128)S(1)}, u32[]{:S(2)}, u32[]{:S(2)}) collective-permute-start(f32[2,1,2,8,1024]{4,3,2,0,1:T(8,128)S(1)} %reshape.146), channel_id=1, source_target_pairs={{0,24},{8,0},{16,8},{24,16},{1,25},{9,1},{17,9},{25,17},{2,26},{10... | collective-permute-start | bytes 393224 | tf_op jit(solution)/shard_map/ppermute | solution.py:236
  4.4 13.6 %collective-permute-start.2 = (f32[2,1,2,8,1024]{4,3,2,0,1:T(8,128)S(1)}, f32[2,1,2,8,1024]{4,3,2,0,1:T(8,128)S(1)}, u32[]{:S(2)}, u32[]{:S(2)}) collective-permute-start(f32[2,1,2,8,1024]{4,3,2,0,1:T(8,128)S(1)} %reshape.146), channel_id=1, source_target_pairs={{0,16},{8,24},{16,0},{24,8},{1,17},{9,25},{17,1},{25,9},{2,18},{10... | collective-permute-start | bytes 393224 | tf_op jit(solution)/shard_map/ppermute | solution.py:236
  5.1 12.9 %collective-permute-start.1 = (f32[2,1,2,8,1024]{4,3,2,0,1:T(8,128)S(1)}, f32[2,1,2,8,1024]{4,3,2,0,1:T(8,128)S(1)}, u32[]{:S(2)}, u32[]{:S(2)}) collective-permute-start(f32[2,1,2,8,1024]{4,3,2,0,1:T(8,128)S(1)} %reshape.146), channel_id=1, source_target_pairs={{0,8},{8,16},{16,24},{24,0},{1,9},{9,17},{17,25},{25,1},{2,10},{10... | collective-permute-start | bytes 393224 | tf_op jit(solution)/shard_map/ppermute | solution.py:236
  14.5 36.4 %collective-permute-start = (f32[2,32,64,128]{3,2,1,0:T(8,128)}, f32[2,32,64,128]{3,2,1,0:T(8,128)}, u32[]{:S(2)}, u32[]{:S(2)}) collective-permute-start(f32[2,32,64,128]{3,2,1,0:T(8,128)} %get-tuple-element.5.refs_0_), channel_id=1, source_target_pairs={{0,24},{8,0},{16,8},{24,16},{1,25},{9,1},{17,9},{25,17},{2,26},{10... | collective-permute-start | bytes 6291464 | tf_op jit(solution)/shard_map/ppermute | solution.py:269
  16.1 46.8 %collective-permute-start.4 = (f32[2,32,64,128]{3,2,1,0:T(8,128)}, f32[2,32,64,128]{3,2,1,0:T(8,128)}, u32[]{:S(2)}, u32[]{:S(2)}) collective-permute-start(f32[2,32,64,128]{3,2,1,0:T(8,128)} %get-tuple-element.6.refs_0_), channel_id=1, source_target_pairs={{0,24},{8,0},{16,8},{24,16},{1,25},{9,1},{17,9},{25,17},{2,26},{10... | collective-permute-start | bytes 6291464 | tf_op jit(solution)/shard_map/ppermute | solution.py:269
  22.3 10.9 %copy-start.2 = (f32[8,3,128]{2,0,1:T(8,128)S(1)}, f32[8,3,128]{2,0,1:T(8,128)}, u32[]{:S(2)}) copy-start(f32[8,3,128]{2,0,1:T(8,128)} %param.25) | copy-start | bytes 36868
  22.3 16.3 %copy-start.7 = (s32[256,1]{0,1:T(1,128)S(1)}, s32[256,1]{0,1:T(1,128)}, u32[]{:S(2)}) copy-start(s32[256,1]{0,1:T(1,128)} %param.28) | copy-start | bytes 3076
  22.3 16.3 %copy-start.6 = (s32[256]{0:T(256)S(1)}, s32[256]{0:T(256)}, u32[]{:S(2)}) copy-start(s32[256]{0:T(256)} %param.29) | copy-start | bytes 3076
  33.1 3.8 %collective-permute-start.5 = (f32[8,3,128]{2,1,0:T(4,128)S(1)}, f32[8,3,128]{2,1,0:T(4,128)S(1)}, u32[]{:S(2)}, u32[]{:S(2)}) collective-permute-start(f32[8,3,128]{2,1,0:T(4,128)S(1)} %copy.71), channel_id=1, source_target_pairs={{0,1},{1,0},{2,3},{3,2},{4,5},{5,4},{6,7},{7,6},{8,9},{9,8},{10,11... | collective-permute-start | bytes 36872 | tf_op jit(solution)/shard_map/ppermute | solution.py:219
  37.0 4.0 %collective-permute-start.6 = (f32[16,3,128]{2,1,0:T(4,128)S(1)}, f32[16,3,128]{2,1,0:T(4,128)S(1)}, u32[]{:S(2)}, u32[]{:S(2)}) collective-permute-start(f32[16,3,128]{2,1,0:T(4,128)S(1)} %maximum_select_fusion.2), channel_id=1, source_target_pairs={{0,2},{1,3},{2,0},{3,1},{4,6},{5,7},{6,4},{7,5},{8,10},{9,11},{10,... | collective-permute-start | bytes 73736 | tf_op jit(solution)/shard_map/ppermute | solution.py:219
  41.0 5.2 %collective-permute-start.7 = (f32[32,3,128]{2,1,0:T(4,128)S(1)}, f32[32,3,128]{2,1,0:T(4,128)S(1)}, u32[]{:S(2)}, u32[]{:S(2)}) collective-permute-start(f32[32,3,128]{2,1,0:T(4,128)S(1)} %maximum_select_fusion.1), channel_id=1, source_target_pairs={{0,4},{1,5},{2,6},{3,7},{4,0},{5,1},{6,2},{7,3},{8,12},{9,13},{10,... | collective-permute-start | bytes 147464 | tf_op jit(solution)/shard_map/ppermute | solution.py:219

commit v14 on v13

--- a/solution.py
+++ b/solution.py
@@ -274,7 +274,7 @@
     cos_b, sin_b = phase_tables(box, size, size)
     rz_box = block2(cos_b, -sin_b, sin_b, cos_b)
     ly_box = block2(cos_b.T, sin_b.T, -sin_b.T, cos_b.T)
-    lig_yz = forward_planes(lig, (rz_box, ly_box), plane_step, size)
+    lig_yz = forward_planes(lig, (rz_box, ly_box), 2 * plane_step, size)
 
     cos_w, sin_w = phase_tables(window, window, window)
     g_tables = []

time: 86.2 us -> 86 us (level)
  Pallas kernels: 54.2 us -> 53 us
    pallas_call x2, Pallas kernels: 20.1 us -> 18.9 us  [forward_planes(): pl.pallas_call(forward_plane_kernel, grid=(planes // plane_step,), in_spe...]
  transfers between devices with their start and end apart: 8 -> 8, of which waited for: 3 -> 4; matrix products, arithmetic and copies ran while one was open for 13% -> 13% of each run, Pallas kernels for 38% -> 37%
where the time goes in v14:
time: 86 us; the launch traced here: 84.5 us
  Pallas kernels  53 us (62%)
  starting transfers between devices  10.7 us (12%)
  waiting for transfers between devices  7.35 us (9%)
  local copies, waits for them, and re-layouts  6.01 us (7%)
  other arithmetic  4.13 us (5%)
  matrix products  2.39 us (3%)
  between operations  0.91 us (1%)
    pallas_call x2, Pallas kernels, cross_spectra(): pl.pallas_call(kernel, grid=(size // row_step,), in_specs=[pl.BlockSpec((...  24.1 us
    pallas_call x2, Pallas kernels, forward_planes(): pl.pallas_call(forward_plane_kernel, grid=(planes // plane_step,), in_spe...  18.9 us
    pallas_call x1, Pallas kernels, inverse_planes(): pl.pallas_call(inverse_plane_kernel, grid=(sets, planes // plane_step), i...  10 us
    ppermute x3, waiting for transfers between devices, gather_pieces(): other = lax.ppermute(held, axis_name, perm=pairs)  6.59 us
    ppermute x3, starting transfers between devices, gather_pieces(): other = lax.ppermute(held, axis_name, perm=pairs)  5.85 us
    ppermute x3, starting transfers between devices, gather_direct(): held.append(lax.ppermute(piece, axis_name, perm=pairs))  3.26 us
    dot_general x1, matrix products, pose_statistics(): jnp.einsum('pja,pka->pjk', moved_centred, center_centred, precision=PRECISE)  1.87 us
  transfers between devices with their start and end apart: 8, of which 4 were waited for; matrix products, arithmetic and copies ran while one was open for 13% of the time, Pallas kernels for 37%

profile of v14, /device:TPU:0, one launch (start us, length us, event | category | flops | bytes accessed | tf_op | source)
XLA Modules:
  0.0 84.5 jit_solution(13782607699197640601)
XLA Ops:
  0.6 1.3 %reshape.146 = f32[2,1,2,8,1024]{4,3,2,0,1:T(8,128)S(1)} reshape(f32[2,1,2,8,32,32]{5,4,3,2,1,0:T(8,128)} %param.21) | data formatting | bytes 262144 | tf_op jit(solution)/shard_map/reshape | solution.py:258
  2.0 2.5 %collective-permute-start.3 = (f32[2,1,2,8,1024]{4,3,2,0,1:T(8,128)S(1)}, f32[2,1,2,8,1024]{4,3,2,0,1:T(8,128)S(1)}, u32[]{:S(2)}, u32[]{:S(2)}) collective-permute-start(f32[2,1,2,8,1024]{4,3,2,0,1:T(8,128)S(1)} %reshape.146), channel_id=1, source_target_pairs={{0,24},{8,0},{16,8},{24,16},{1,25},{9,1},{17,9},{25,17},{2,26},{10... | collective-permute-start | bytes 393224 | tf_op jit(solution)/shard_map/ppermute | solution.py:236
  4.4 0.6 collective-permute-start.2
  5.3 9.2 %shard_map.203 = (f32[2,32,64,128]{3,2,1,0:T(8,128)}, f32[2,32,64,128]{3,2,1,0:T(8,128)}) custom-call(f32[2,32,128,128]{3,2,1,0:T(8,128)} %in_ref.1, f32[256,256]{1,0:T(8,128)} %constant.153.clone.rz_ref.refs_2_, f32[256,256]{1,0:T(8,128)} %constant.154.clone.ly_ref), custom_call_target="tpu_custom_call" | custom-call | tf_op jit(solution)/shard_map/pallas_call | solution.py:105
  14.5 1.6 %collective-permute-start = (f32[2,32,64,128]{3,2,1,0:T(8,128)}, f32[2,32,64,128]{3,2,1,0:T(8,128)}, u32[]{:S(2)}, u32[]{:S(2)}) collective-permute-start(f32[2,32,64,128]{3,2,1,0:T(8,128)} %get-tuple-element.5.refs_0_), channel_id=1, source_target_pairs={{0,24},{8,0},{16,8},{24,16},{1,25},{9,1},{17,9},{25,17},{2,26},{10... | collective-permute-start | bytes 6291464 | tf_op jit(solution)/shard_map/ppermute | solution.py:269
  16.5 0.7 gather_fusion.1
  17.4 0.6 fusion.12
  18.1 0.6 gather_fusion
  18.7 1.3 %slice_multiply_fusion.1 = (f32[2,1,1,32,1024]{4,3,0,2,1:T(8,128)S(1)}, f32[2,1,1,32,1024]{4,3,0,2,1:T(8,128)S(1)}) fusion(f32[2,1,2,32,1024]{4,3,0,2,1:T(8,128)S(1)} %copy_bitcast_fusion, f32[]{:T(128)} %bitcast.8, f32[]{:T(128)} %bitcast.9), kind=kLoop, calls=%fused_computation.11 | loop fusion | flops 131072 | bytes 1048584 | tf_op jit(solution)/shard_map/mul | solution.py:272
  20.7 1.5 %pad_maximum_fusion.in_ref = f32[2,64,32,32]{3,2,1,0:T(8,128)} fusion(f32[1,64,32,32]{3,2,1,0:T(8,128)S(1)} %mul.51, f32[1,64,32,32]{3,2,1,0:T(8,128)S(1)} %mul.48), kind=kLoop, calls=%fused_computation.3 | loop fusion | flops 131072 | bytes 1048576 | tf_op jit(solution)/shard_map/stack | solution.py:271
  22.3 9.7 %shard_map.204.refs_2_ = f32[2,64,128,128]{3,2,1,0:T(8,128)} custom-call(f32[2,64,32,32]{3,2,1,0:T(8,128)} %pad_maximum_fusion.in_ref, f32[64,256]{1,0:T(8,128)} %constant.155.clone.rz_ref, f32[256,64]{1,0:T(8,128)} %constant.156.clone.ly_ref), custom_call_target="tpu_custom_call" | custom-call | tf_op jit(solution)/shard_map/pallas_call | solution.py:105
  31.9 1.6 %collective-permute-start.5 = (f32[8,3,128]{2,1,0:T(4,128)S(1)}, f32[8,3,128]{2,1,0:T(4,128)S(1)}, u32[]{:S(2)}, u32[]{:S(2)}) collective-permute-start(f32[8,3,128]{2,1,0:T(4,128)S(1)} %copy.71), channel_id=1, source_target_pairs={{0,1},{1,0},{2,3},{3,2},{4,5},{5,4},{6,7},{7,6},{8,9},{9,8},{10,11... | collective-permute-start | bytes 36872 | tf_op jit(solution)/shard_map/ppermute | solution.py:219
  34.0 1.7 %collective-permute-done.5 = f32[8,3,128]{2,1,0:T(4,128)S(1)} collective-permute-done((f32[8,3,128]{2,1,0:T(4,128)S(1)}, f32[8,3,128]{2,1,0:T(4,128)S(1)}, u32[]{:S(2)}, u32[]{:S(2)}) %collective-permute-start.5) | collective-permute-done | bytes 12320 | tf_op jit(solution)/shard_map/ppermute | solution.py:219
  35.8 1.6 %collective-permute-start.6 = (f32[16,3,128]{2,1,0:T(4,128)S(1)}, f32[16,3,128]{2,1,0:T(4,128)S(1)}, u32[]{:S(2)}, u32[]{:S(2)}) collective-permute-start(f32[16,3,128]{2,1,0:T(4,128)S(1)} %maximum_select_fusion.2), channel_id=1, source_target_pairs={{0,2},{1,3},{2,0},{3,1},{4,6},{5,7},{6,4},{7,5},{8,10},{9,11},{10,... | collective-permute-start | bytes 73736 | tf_op jit(solution)/shard_map/ppermute | solution.py:219
  37.4 2.3 %collective-permute-done.6 = f32[16,3,128]{2,1,0:T(4,128)S(1)} collective-permute-done((f32[16,3,128]{2,1,0:T(4,128)S(1)}, f32[16,3,128]{2,1,0:T(4,128)S(1)}, u32[]{:S(2)}, u32[]{:S(2)}) %collective-permute-start.6) | collective-permute-done | bytes 24608 | tf_op jit(solution)/shard_map/ppermute | solution.py:219
  39.8 2.7 %collective-permute-start.7 = (f32[32,3,128]{2,1,0:T(4,128)S(1)}, f32[32,3,128]{2,1,0:T(4,128)S(1)}, u32[]{:S(2)}, u32[]{:S(2)}) collective-permute-start(f32[32,3,128]{2,1,0:T(4,128)S(1)} %maximum_select_fusion.1), channel_id=1, source_target_pairs={{0,4},{1,5},{2,6},{3,7},{4,0},{5,1},{6,2},{7,3},{8,12},{9,13},{10,... | collective-permute-start | bytes 147464 | tf_op jit(solution)/shard_map/ppermute | solution.py:219
  42.4 2.6 %collective-permute-done.7 = f32[32,3,128]{2,1,0:T(4,128)S(1)} collective-permute-done((f32[32,3,128]{2,1,0:T(4,128)S(1)}, f32[32,3,128]{2,1,0:T(4,128)S(1)}, u32[]{:S(2)}, u32[]{:S(2)}) %collective-permute-start.7) | collective-permute-done | bytes 49184 | tf_op jit(solution)/shard_map/ppermute | solution.py:219
  45.0 1.0 %gather_fusion.2 = f32[256,3,128]{2,1,0:T(4,128)S(1)} fusion(f32[64,3,128]{2,1,0:T(4,128)S(1)} %maximum_select_fusion, s32[1024]{0:T(1024)S(1)} %pad_clamp_fusion), kind=kCustom, calls=%fused_computation.2 | custom fusion | bytes 787456 | tf_op jit(solution)/shard_map/jit(_take)/gather | solution.py:327
  47.0 1.9 %fusion = f32[256,3,3]{2,1,0:T(4,128)S(1)} fusion(f32[256,3,128]{2,1,0:T(4,128)S(1)} %copy.75, f32[256,3,128]{2,1,0:T(4,128)S(1)} %gather_fusion.2, f32[256,3]{1,0:T(8,128)S(1)} %broadcast_multiply_fusion), kind=kOutput, calls=%fused_computation.7 | convolution fusion | flops 3637248 | bytes 798720 | tf_op jit(solution)/shard_map/pja,pka->pjk/dot_general | solution.py:333
  49.0 0.6 maximum_bitcast_fusion.1
  49.6 12.0 %shard_map.205.refs_0_ = f32[2,2,32,64,128]{4,3,2,1,0:T(8,128)} custom-call(f32[2,32,64,128]{3,2,1,0:T(8,128)} %get-tuple-element.5.refs_0_, f32[2,32,64,128]{3,2,1,0:T(8,128)} %collective-permute-done.refs_1_, f32[2,64,128,128]{3,2,1,0:T(8,128)} %shard_map.204.refs_2_, f32[128,128]{1,0:T(8,128)} %constant.157.clone.refs_3_, ...), custom_call_target="tpu_custom_call" | custom-call | tf_op jit(solution)/shard_map/pallas_call | solution.py:170
  61.7 0.7 collective-permute-done.4.refs_1_
  62.4 12.0 %shard_map.206.refs_1_ = f32[2,2,32,64,128]{4,3,2,1,0:T(8,128)} custom-call(f32[2,32,64,128]{3,2,1,0:T(8,128)} %get-tuple-element.6.refs_0_, f32[2,32,64,128]{3,2,1,0:T(8,128)} %collective-permute-done.4.refs_1_, f32[2,64,128,128]{3,2,1,0:T(8,128)} %shard_map.204.refs_2_, f32[128,128]{1,0:T(8,128)} %constant.157.clone.refs_3_, ...), custom_call_target="tpu_custom_call" | custom-call | tf_op jit(solution)/shard_map/pallas_call | solution.py:170
  74.4 10.0 %shard_map.207 = f32[2,32,128,128]{3,2,1,0:T(8,128)} custom-call(f32[2,2,32,64,128]{4,3,2,1,0:T(8,128)} %shard_map.205.refs_0_, f32[2,2,32,64,128]{4,3,2,1,0:T(8,128)} %shard_map.206.refs_1_, f32[256,256]{1,0:T(8,128)} %constant.153.clone.rz_ref.refs_2_, f32[256,128]{1,0:T(8,128)} %constant.160.clone.refs_3_), custom_call_target="tpu_custom_call" | custom-call | tf_op jit(solution)/shard_map/pallas_call | solution.py:185
  (55 shorter events, 3.2 us)
Async XLA Ops:
  0.6 32.9 %copy-start = (f32[3,128]{1,0:T(4,128)S(1)}, f32[3,128]{1,0:T(4,128)}, u32[]{:S(2)}) copy-start(f32[3,128]{1,0:T(4,128)} %param.24) | copy-start | bytes 4612
  1.9 14.2 %copy-start.5 = (s32[256]{0:T(256)S(1)}, s32[256]{0:T(256)}, u32[]{:S(2)}) copy-start(s32[256]{0:T(256)} %param.26) | copy-start | bytes 3076
  1.9 14.2 %copy-start.8 = (s32[256]{0:T(256)S(1)}, s32[256]{0:T(256)}, u32[]{:S(2)}) copy-start(s32[256]{0:T(256)} %param.27) | copy-start | bytes 3076
  2.0 14.2 %copy-start.1 = (f32[2,1,2,8,32,32]{5,4,3,2,1,0:T(8,128)S(1)}, f32[2,1,2,8,32,32]{5,4,3,2,1,0:T(8,128)}, u32[]{:S(2)}) copy-start(f32[2,1,2,8,32,32]{5,4,3,2,1,0:T(8,128)} %param.21) | copy-start | bytes 393220
  2.0 14.5 %copy-start.3 = (f32[9,16]{1,0:T(8,128)S(1)}, f32[9,16]{1,0:T(8,128)}, u32[]{:S(2)}) copy-start(f32[9,16]{1,0:T(8,128)} %param.23) | copy-start | bytes 1732
  2.0 15.4 %copy-start.4 = (f32[2]{0:T(128)S(1)}, f32[2]{0:T(128)}, u32[]{:S(2)}) copy-start(f32[2]{0:T(128)} %param.22) | copy-start | bytes 28
  2.0 16.0 %collective-permute-start.3 = (f32[2,1,2,8,1024]{4,3,2,0,1:T(8,128)S(1)}, f32[2,1,2,8,1024]{4,3,2,0,1:T(8,128)S(1)}, u32[]{:S(2)}, u32[]{:S(2)}) collective-permute-start(f32[2,1,2,8,1024]{4,3,2,0,1:T(8,128)S(1)} %reshape.146), channel_id=1, source_target_pairs={{0,24},{8,0},{16,8},{24,16},{1,25},{9,1},{17,9},{25,17},{2,26},{10... | collective-permute-start | bytes 393224 | tf_op jit(solution)/shard_map/ppermute | solution.py:236
  4.4 13.6 %collective-permute-start.2 = (f32[2,1,2,8,1024]{4,3,2,0,1:T(8,128)S(1)}, f32[2,1,2,8,1024]{4,3,2,0,1:T(8,128)S(1)}, u32[]{:S(2)}, u32[]{:S(2)}) collective-permute-start(f32[2,1,2,8,1024]{4,3,2,0,1:T(8,128)S(1)} %reshape.146), channel_id=1, source_target_pairs={{0,16},{8,24},{16,0},{24,8},{1,17},{9,25},{17,1},{25,9},{2,18},{10... | collective-permute-start | bytes 393224 | tf_op jit(solution)/shard_map/ppermute | solution.py:236
  5.1 12.9 %collective-permute-start.1 = (f32[2,1,2,8,1024]{4,3,2,0,1:T(8,128)S(1)}, f32[2,1,2,8,1024]{4,3,2,0,1:T(8,128)S(1)}, u32[]{:S(2)}, u32[]{:S(2)}) collective-permute-start(f32[2,1,2,8,1024]{4,3,2,0,1:T(8,128)S(1)} %reshape.146), channel_id=1, source_target_pairs={{0,8},{8,16},{16,24},{24,0},{1,9},{9,17},{17,25},{25,1},{2,10},{10... | collective-permute-start | bytes 393224 | tf_op jit(solution)/shard_map/ppermute | solution.py:236
  14.5 35.2 %collective-permute-start = (f32[2,32,64,128]{3,2,1,0:T(8,128)}, f32[2,32,64,128]{3,2,1,0:T(8,128)}, u32[]{:S(2)}, u32[]{:S(2)}) collective-permute-start(f32[2,32,64,128]{3,2,1,0:T(8,128)} %get-tuple-element.5.refs_0_), channel_id=1, source_target_pairs={{0,24},{8,0},{16,8},{24,16},{1,25},{9,1},{17,9},{25,17},{2,26},{10... | collective-permute-start | bytes 6291464 | tf_op jit(solution)/shard_map/ppermute | solution.py:269
  16.1 46.3 %collective-permute-start.4 = (f32[2,32,64,128]{3,2,1,0:T(8,128)}, f32[2,32,64,128]{3,2,1,0:T(8,128)}, u32[]{:S(2)}, u32[]{:S(2)}) collective-permute-start(f32[2,32,64,128]{3,2,1,0:T(8,128)} %get-tuple-element.6.refs_0_), channel_id=1, source_target_pairs={{0,24},{8,0},{16,8},{24,16},{1,25},{9,1},{17,9},{25,17},{2,26},{10... | collective-permute-start | bytes 6291464 | tf_op jit(solution)/shard_map/ppermute | solution.py:269
  22.3 9.7 %copy-start.2 = (f32[8,3,128]{2,0,1:T(8,128)S(1)}, f32[8,3,128]{2,0,1:T(8,128)}, u32[]{:S(2)}) copy-start(f32[8,3,128]{2,0,1:T(8,128)} %param.25) | copy-start | bytes 36868
  22.3 15.1 %copy-start.7 = (s32[256,1]{0,1:T(1,128)S(1)}, s32[256,1]{0,1:T(1,128)}, u32[]{:S(2)}) copy-start(s32[256,1]{0,1:T(1,128)} %param.28) | copy-start | bytes 3076
  22.3 15.1 %copy-start.6 = (s32[256]{0:T(256)S(1)}, s32[256]{0:T(256)}, u32[]{:S(2)}) copy-start(s32[256]{0:T(256)} %param.29) | copy-start | bytes 3076
  31.9 3.8 %collective-permute-start.5 = (f32[8,3,128]{2,1,0:T(4,128)S(1)}, f32[8,3,128]{2,1,0:T(4,128)S(1)}, u32[]{:S(2)}, u32[]{:S(2)}) collective-permute-start(f32[8,3,128]{2,1,0:T(4,128)S(1)} %copy.71), channel_id=1, source_target_pairs={{0,1},{1,0},{2,3},{3,2},{4,5},{5,4},{6,7},{7,6},{8,9},{9,8},{10,11... | collective-permute-start | bytes 36872 | tf_op jit(solution)/shard_map/ppermute | solution.py:219
  35.8 4.0 %collective-permute-start.6 = (f32[16,3,128]{2,1,0:T(4,128)S(1)}, f32[16,3,128]{2,1,0:T(4,128)S(1)}, u32[]{:S(2)}, u32[]{:S(2)}) collective-permute-start(f32[16,3,128]{2,1,0:T(4,128)S(1)} %maximum_select_fusion.2), channel_id=1, source_target_pairs={{0,2},{1,3},{2,0},{3,1},{4,6},{5,7},{6,4},{7,5},{8,10},{9,11},{10,... | collective-permute-start | bytes 73736 | tf_op jit(solution)/shard_map/ppermute | solution.py:219
  39.8 5.2 %collective-permute-start.7 = (f32[32,3,128]{2,1,0:T(4,128)S(1)}, f32[32,3,128]{2,1,0:T(4,128)S(1)}, u32[]{:S(2)}, u32[]{:S(2)}) collective-permute-start(f32[32,3,128]{2,1,0:T(4,128)S(1)} %maximum_select_fusion.1), channel_id=1, source_target_pairs={{0,4},{1,5},{2,6},{3,7},{4,0},{5,1},{6,2},{7,3},{8,12},{9,13},{10,... | collective-permute-start | bytes 147464 | tf_op jit(solution)/shard_map/ppermute | solution.py:219

commit v15 on v14

--- a/solution.py
+++ b/solution.py
@@ -311,7 +311,10 @@
     pose_member,
     size,
 ):
-    all_centers = gather_pieces(cluster_center, "rot", 0)
+    count = lax.axis_size("rot")
+    copies = jnp.broadcast_to(cluster_center[None], (count,) + cluster_center.shape)
+    copies = copies.reshape((count * cluster_center.shape[0],) + cluster_center.shape[1:])
+    all_centers = lax.all_to_all(copies, "rot", split_axis=0, concat_axis=0, tiled=True)
     local_count = cluster_center.shape[0]
     cluster = pose_owner[:, 0] * local_count + pose_member
     rotation = jnp.take(rotation_table, pose_rotation, axis=1, mode="clip").T.reshape(-1, 3, 3)

time: 86 us -> 86.1 us (level)
    all_to_all x0 -> x1, waiting for transfers between devices: none -> 7.59 us  [pose_statistics(): lax.all_to_all(copies, 'rot', split_axis=0, concat_axis=0, tiled=True)]
    ppermute x3 -> x0, waiting for transfers between devices: 6.59 us -> none  [gather_pieces(): other = lax.ppermute(held, axis_name, perm=pairs)]
    ppermute x3 -> x0, starting transfers between devices: 5.85 us -> none  [gather_pieces(): other = lax.ppermute(held, axis_name, perm=pairs)]
    all_to_all x0 -> x1, starting transfers between devices: none -> 5.81 us  [pose_statistics(): lax.all_to_all(copies, 'rot', split_axis=0, concat_axis=0, tiled=True)]
  transfers between devices with their start and end apart: 8 -> 6, of which waited for: 4 -> 1; matrix products, arithmetic and copies ran while one was open for 13% -> 14% of each run, Pallas kernels for 37% -> 36%
where the time goes in v15:
time: 86.1 us; the launch traced here: 85.2 us
  Pallas kernels  52.8 us (61%)
  starting transfers between devices  10.7 us (12%)
  waiting for transfers between devices  7.61 us (9%)
  local copies, waits for them, and re-layouts  6.71 us (8%)
  other arithmetic  4.03 us (5%)
  matrix products  2.45 us (3%)
  between operations  0.93 us (1%)
    pallas_call x2, Pallas kernels, cross_spectra(): pl.pallas_call(kernel, grid=(size // row_step,), in_specs=[pl.BlockSpec((...  24 us
    pallas_call x2, Pallas kernels, forward_planes(): pl.pallas_call(forward_plane_kernel, grid=(planes // plane_step,), in_spe...  18.7 us
    pallas_call x1, Pallas kernels, inverse_planes(): pl.pallas_call(inverse_plane_kernel, grid=(sets, planes // plane_step), i...  10 us
    all_to_all x1, waiting for transfers between devices, pose_statistics(): lax.all_to_all(copies, 'rot', split_axis=0, concat_axis=0, tiled=True)  7.59 us
    all_to_all x1, starting transfers between devices, pose_statistics(): lax.all_to_all(copies, 'rot', split_axis=0, concat_axis=0, tiled=True)  5.81 us
    ppermute x3, starting transfers between devices, gather_direct(): held.append(lax.ppermute(piece, axis_name, perm=pairs))  3.26 us
    dot_general x1, matrix products, pose_statistics(): jnp.einsum('pja,pka->pjk', moved_centred, center_centred, precision=PRECISE)  1.87 us
  transfers between devices with their start and end apart: 6, of which 1 were waited for; matrix products, arithmetic and copies ran while one was open for 14% of the time, Pallas kernels for 36%

profile of v15, /device:TPU:0, one launch (start us, length us, event | category | flops | bytes accessed | tf_op | source)
XLA Modules:
  0.0 85.2 jit_solution(4033279870484714094)
XLA Ops:
  0.6 1.3 %reshape.150 = f32[2,1,2,8,1024]{4,3,2,0,1:T(8,128)S(1)} reshape(f32[2,1,2,8,32,32]{5,4,3,2,1,0:T(8,128)} %param.21) | data formatting | bytes 262144 | tf_op jit(solution)/shard_map/reshape | solution.py:258
  2.0 2.5 %collective-permute-start.3 = (f32[2,1,2,8,1024]{4,3,2,0,1:T(8,128)S(1)}, f32[2,1,2,8,1024]{4,3,2,0,1:T(8,128)S(1)}, u32[]{:S(2)}, u32[]{:S(2)}) collective-permute-start(f32[2,1,2,8,1024]{4,3,2,0,1:T(8,128)S(1)} %reshape.150), channel_id=1, source_target_pairs={{0,24},{8,0},{16,8},{24,16},{1,25},{9,1},{17,9},{25,17},{2,26},{10... | collective-permute-start | bytes 393224 | tf_op jit(solution)/shard_map/ppermute | solution.py:236
  4.5 0.6 collective-permute-start.2
  5.3 9.2 %shard_map.203 = (f32[2,32,64,128]{3,2,1,0:T(8,128)}, f32[2,32,64,128]{3,2,1,0:T(8,128)}) custom-call(f32[2,32,128,128]{3,2,1,0:T(8,128)} %in_ref.1, f32[256,256]{1,0:T(8,128)} %constant.103.clone.rz_ref.refs_2_, f32[256,256]{1,0:T(8,128)} %constant.104.clone.ly_ref), custom_call_target="tpu_custom_call" | custom-call | tf_op jit(solution)/shard_map/pallas_call | solution.py:105
  14.5 1.6 %collective-permute-start = (f32[2,32,64,128]{3,2,1,0:T(8,128)}, f32[2,32,64,128]{3,2,1,0:T(8,128)}, u32[]{:S(2)}, u32[]{:S(2)}) collective-permute-start(f32[2,32,64,128]{3,2,1,0:T(8,128)} %get-tuple-element.5.refs_0_), channel_id=1, source_target_pairs={{0,24},{8,0},{16,8},{24,16},{1,25},{9,1},{17,9},{25,17},{2,26},{10... | collective-permute-start | bytes 6291464 | tf_op jit(solution)/shard_map/ppermute | solution.py:269
  16.6 0.7 gather_fusion.1
  17.4 0.7 fusion.12
  18.2 0.6 gather_fusion
  18.8 1.4 %slice_multiply_fusion.1 = (f32[2,1,1,32,1024]{4,3,0,2,1:T(8,128)S(1)}, f32[2,1,1,32,1024]{4,3,0,2,1:T(8,128)S(1)}) fusion(f32[2,1,2,32,1024]{4,3,0,2,1:T(8,128)S(1)} %copy_bitcast_fusion, f32[]{:T(128)} %bitcast.8, f32[]{:T(128)} %bitcast.9), kind=kLoop, calls=%fused_computation.11 | loop fusion | flops 131072 | bytes 1048584 | tf_op jit(solution)/shard_map/mul | solution.py:272
  20.2 0.3 mul.51
  20.5 0.3 mul.48
  20.9 1.5 %pad_maximum_fusion.in_ref = f32[2,64,32,32]{3,2,1,0:T(8,128)} fusion(f32[1,64,32,32]{3,2,1,0:T(8,128)S(1)} %mul.51, f32[1,64,32,32]{3,2,1,0:T(8,128)S(1)} %mul.48), kind=kLoop, calls=%fused_computation.3 | loop fusion | flops 131072 | bytes 1048576 | tf_op jit(solution)/shard_map/stack | solution.py:271
  22.4 9.5 %shard_map.204.refs_2_ = f32[2,64,128,128]{3,2,1,0:T(8,128)} custom-call(f32[2,64,32,32]{3,2,1,0:T(8,128)} %pad_maximum_fusion.in_ref, f32[64,256]{1,0:T(8,128)} %constant.105.clone.rz_ref, f32[256,64]{1,0:T(8,128)} %constant.106.clone.ly_ref), custom_call_target="tpu_custom_call" | custom-call | tf_op jit(solution)/shard_map/pallas_call | solution.py:105
  31.9 0.7 broadcast_in_dim.13
  32.6 5.8 %all-to-all-start = ((f32[64,3,128]{2,1,0:T(4,128)}), f32[64,3,128]{2,1,0:T(4,128)S(1)}, u32[]{:S(2)}, u32[]{:S(2)}) async-start(f32[64,3,128]{2,1,0:T(4,128)} %bitcast.16), calls=%async_computation | async-start | bytes 262144 | tf_op jit(solution)/shard_map/all_to_all | solution.py:317
  38.4 7.6 %all-to-all-done = f32[64,3,128]{2,1,0:T(4,128)S(1)} async-done(((f32[64,3,128]{2,1,0:T(4,128)}), f32[64,3,128]{2,1,0:T(4,128)S(1)}, u32[]{:S(2)}, u32[]{:S(2)}) %all-to-all-start) | async-done | bytes 98336 | tf_op jit(solution)/shard_map/all_to_all | solution.py:317
  46.0 1.0 %gather_fusion.2 = f32[256,3,128]{2,1,0:T(4,128)S(1)} fusion(f32[64,3,128]{2,1,0:T(4,128)S(1)} %all-to-all-done, s32[1024]{0:T(1024)S(1)} %pad_clamp_fusion), kind=kCustom, calls=%fused_computation.2 | custom fusion | bytes 787456 | tf_op jit(solution)/shard_map/jit(_take)/gather | solution.py:330
  47.2 0.6 fusion.11
  48.0 0.3 reduce_sum.32
  48.4 1.9 %fusion = f32[256,3,3]{2,1,0:T(4,128)S(1)} fusion(f32[256,3,128]{2,1,0:T(4,128)S(1)} %copy.68, f32[256,3,128]{2,1,0:T(4,128)S(1)} %gather_fusion.2, f32[256,3]{1,0:T(8,128)S(1)} %broadcast_multiply_fusion), kind=kOutput, calls=%fused_computation.7 | convolution fusion | flops 3637248 | bytes 798720 | tf_op jit(solution)/shard_map/pja,pka->pjk/dot_general | solution.py:336
  50.5 0.6 maximum_bitcast_fusion.1
  51.1 12.0 %shard_map.205.refs_0_ = f32[2,2,32,64,128]{4,3,2,1,0:T(8,128)} custom-call(f32[2,32,64,128]{3,2,1,0:T(8,128)} %get-tuple-element.5.refs_0_, f32[2,32,64,128]{3,2,1,0:T(8,128)} %collective-permute-done.refs_1_, f32[2,64,128,128]{3,2,1,0:T(8,128)} %shard_map.204.refs_2_, f32[128,128]{1,0:T(8,128)} %constant.107.clone.refs_3_, ...), custom_call_target="tpu_custom_call" | custom-call | tf_op jit(solution)/shard_map/pallas_call | solution.py:170
  63.1 12.0 %shard_map.206.refs_1_ = f32[2,2,32,64,128]{4,3,2,1,0:T(8,128)} custom-call(f32[2,32,64,128]{3,2,1,0:T(8,128)} %get-tuple-element.6.refs_0_, f32[2,32,64,128]{3,2,1,0:T(8,128)} %collective-permute-done.4.refs_1_, f32[2,64,128,128]{3,2,1,0:T(8,128)} %shard_map.204.refs_2_, f32[128,128]{1,0:T(8,128)} %constant.107.clone.refs_3_, ...), custom_call_target="tpu_custom_call" | custom-call | tf_op jit(solution)/shard_map/pallas_call | solution.py:170
  75.1 10.0 %shard_map.207 = f32[2,32,128,128]{3,2,1,0:T(8,128)} custom-call(f32[2,2,32,64,128]{4,3,2,1,0:T(8,128)} %shard_map.205.refs_0_, f32[2,2,32,64,128]{4,3,2,1,0:T(8,128)} %shard_map.206.refs_1_, f32[256,256]{1,0:T(8,128)} %constant.103.clone.rz_ref.refs_2_, f32[256,128]{1,0:T(8,128)} %constant.110.clone.refs_3_), custom_call_target="tpu_custom_call" | custom-call | tf_op jit(solution)/shard_map/pallas_call | solution.py:185
  (48 shorter events, 1.5 us)
Async XLA Ops:
  0.6 46.5 %copy-start = (f32[3,128]{1,0:T(4,128)S(1)}, f32[3,128]{1,0:T(4,128)}, u32[]{:S(2)}) copy-start(f32[3,128]{1,0:T(4,128)} %param.24) | copy-start | bytes 4612
  1.9 14.2 %copy-start.7 = (s32[256,1]{0,1:T(1,128)S(1)}, s32[256,1]{0,1:T(1,128)}, u32[]{:S(2)}) copy-start(s32[256,1]{0,1:T(1,128)} %param.28) | copy-start | bytes 3076
  1.9 14.2 %copy-start.8 = (s32[256]{0:T(256)S(1)}, s32[256]{0:T(256)}, u32[]{:S(2)}) copy-start(s32[256]{0:T(256)} %param.27) | copy-start | bytes 3076
  2.0 14.3 %copy-start.5 = (s32[256]{0:T(256)S(1)}, s32[256]{0:T(256)}, u32[]{:S(2)}) copy-start(s32[256]{0:T(256)} %param.26) | copy-start | bytes 3076
  2.0 14.3 %copy-start.1 = (f32[2,1,2,8,32,32]{5,4,3,2,1,0:T(8,128)S(1)}, f32[2,1,2,8,32,32]{5,4,3,2,1,0:T(8,128)}, u32[]{:S(2)}) copy-start(f32[2,1,2,8,32,32]{5,4,3,2,1,0:T(8,128)} %param.21) | copy-start | bytes 393220
  2.0 14.5 %copy-start.3 = (f32[9,16]{1,0:T(8,128)S(1)}, f32[9,16]{1,0:T(8,128)}, u32[]{:S(2)}) copy-start(f32[9,16]{1,0:T(8,128)} %param.23) | copy-start | bytes 1732
  2.0 15.4 %copy-start.6 = (s32[256]{0:T(256)S(1)}, s32[256]{0:T(256)}, u32[]{:S(2)}) copy-start(s32[256]{0:T(256)} %param.29) | copy-start | bytes 3076
  2.0 15.4 %copy-start.4 = (f32[2]{0:T(128)S(1)}, f32[2]{0:T(128)}, u32[]{:S(2)}) copy-start(f32[2]{0:T(128)} %param.22) | copy-start | bytes 28
  2.0 16.1 %collective-permute-start.3 = (f32[2,1,2,8,1024]{4,3,2,0,1:T(8,128)S(1)}, f32[2,1,2,8,1024]{4,3,2,0,1:T(8,128)S(1)}, u32[]{:S(2)}, u32[]{:S(2)}) collective-permute-start(f32[2,1,2,8,1024]{4,3,2,0,1:T(8,128)S(1)} %reshape.150), channel_id=1, source_target_pairs={{0,24},{8,0},{16,8},{24,16},{1,25},{9,1},{17,9},{25,17},{2,26},{10... | collective-permute-start | bytes 393224 | tf_op jit(solution)/shard_map/ppermute | solution.py:236
  4.5 13.6 %collective-permute-start.2 = (f32[2,1,2,8,1024]{4,3,2,0,1:T(8,128)S(1)}, f32[2,1,2,8,1024]{4,3,2,0,1:T(8,128)S(1)}, u32[]{:S(2)}, u32[]{:S(2)}) collective-permute-start(f32[2,1,2,8,1024]{4,3,2,0,1:T(8,128)S(1)} %reshape.150), channel_id=1, source_target_pairs={{0,16},{8,24},{16,0},{24,8},{1,17},{9,25},{17,1},{25,9},{2,18},{10... | collective-permute-start | bytes 393224 | tf_op jit(solution)/shard_map/ppermute | solution.py:236
  5.1 13.0 %collective-permute-start.1 = (f32[2,1,2,8,1024]{4,3,2,0,1:T(8,128)S(1)}, f32[2,1,2,8,1024]{4,3,2,0,1:T(8,128)S(1)}, u32[]{:S(2)}, u32[]{:S(2)}) collective-permute-start(f32[2,1,2,8,1024]{4,3,2,0,1:T(8,128)S(1)} %reshape.150), channel_id=1, source_target_pairs={{0,8},{8,16},{16,24},{24,0},{1,9},{9,17},{17,25},{25,1},{2,10},{10... | collective-permute-start | bytes 393224 | tf_op jit(solution)/shard_map/ppermute | solution.py:236
  14.5 36.6 %collective-permute-start = (f32[2,32,64,128]{3,2,1,0:T(8,128)}, f32[2,32,64,128]{3,2,1,0:T(8,128)}, u32[]{:S(2)}, u32[]{:S(2)}) collective-permute-start(f32[2,32,64,128]{3,2,1,0:T(8,128)} %get-tuple-element.5.refs_0_), channel_id=1, source_target_pairs={{0,24},{8,0},{16,8},{24,16},{1,25},{9,1},{17,9},{25,17},{2,26},{10... | collective-permute-start | bytes 6291464 | tf_op jit(solution)/shard_map/ppermute | solution.py:269
  16.1 47.0 %collective-permute-start.4 = (f32[2,32,64,128]{3,2,1,0:T(8,128)}, f32[2,32,64,128]{3,2,1,0:T(8,128)}, u32[]{:S(2)}, u32[]{:S(2)}) collective-permute-start(f32[2,32,64,128]{3,2,1,0:T(8,128)} %get-tuple-element.6.refs_0_), channel_id=1, source_target_pairs={{0,24},{8,0},{16,8},{24,16},{1,25},{9,1},{17,9},{25,17},{2,26},{10... | collective-permute-start | bytes 6291464 | tf_op jit(solution)/shard_map/ppermute | solution.py:269
  22.4 9.5 %copy-start.2 = (f32[8,3,128]{2,0,1:T(8,128)S(1)}, f32[8,3,128]{2,0,1:T(8,128)}, u32[]{:S(2)}) copy-start(f32[8,3,128]{2,0,1:T(8,128)} %param.25) | copy-start | bytes 36868
  32.6 13.4 %all-to-all-start = ((f32[64,3,128]{2,1,0:T(4,128)}), f32[64,3,128]{2,1,0:T(4,128)S(1)}, u32[]{:S(2)}, u32[]{:S(2)}) async-start(f32[64,3,128]{2,1,0:T(4,128)} %bitcast.16), calls=%async_computation | async-start | bytes 262144 | tf_op jit(solution)/shard_map/all_to_all | solution.py:317

commit v16 on v14

--- a/solution.py
+++ b/solution.py
@@ -2,6 +2,7 @@
 
 import jax
 import jax.numpy as jnp
+import ml_dtypes
 import numpy as np
 from jax import lax
 from jax.experimental import pallas as pl
@@ -31,6 +32,12 @@
     high = table.astype(BF16)
     low = (table - high.astype(F32)).astype(BF16)
     return high, low
+
+
+def table_parts(table):
+    high = table.astype(ml_dtypes.bfloat16)
+    low = (table - high.astype(np.float32)).astype(ml_dtypes.bfloat16)
+    return [high, low]
 
 
 def split_dot(a, b_high, b_low, a_left):
@@ -42,11 +49,11 @@
     return dot(b_high, a_high) + (dot(b_high, a_low) + dot(b_low, a_high))
 
 
-def forward_plane_kernel(in_ref, rz_ref, ly_ref, *out_refs):
+def forward_plane_kernel(in_ref, rz_hi_ref, rz_lo_ref, ly_hi_ref, ly_lo_ref, *out_refs):
     planes, rows, cols = in_ref.shape[1], in_ref.shape[2], in_ref.shape[3]
     size = out_refs[0].shape[3]
-    rz_hi, rz_lo = hi_lo(rz_ref[...])
-    ly_hi, ly_lo = hi_lo(ly_ref[...])
+    rz_hi, rz_lo = rz_hi_ref[...], rz_lo_ref[...]
+    ly_hi, ly_lo = ly_hi_ref[...], ly_lo_ref[...]
     joined = jnp.concatenate(
         [in_ref[0].reshape(planes * rows, cols), in_ref[1].reshape(planes * rows, cols)], axis=1
     )
@@ -71,12 +78,12 @@
 
 
 def inverse_plane_kernel(*refs):
-    in_refs = refs[:-3]
-    ly_ref, rz_ref, out_ref = refs[-3:]
+    in_refs = refs[:-5]
+    ly_hi_ref, ly_lo_ref, rz_hi_ref, rz_lo_ref, out_ref = refs[-5:]
     planes = in_refs[0].shape[2]
     size = in_refs[0].shape[4]
-    ly_hi, ly_lo = hi_lo(ly_ref[...])
-    rz_hi, rz_lo = hi_lo(rz_ref[...])
+    ly_hi, ly_lo = ly_hi_ref[...], ly_lo_ref[...]
+    rz_hi, rz_lo = rz_hi_ref[...], rz_lo_ref[...]
 
     def plane(c, p):
         return jnp.concatenate([r[0, c, p] for r in in_refs], axis=0)
@@ -100,6 +107,7 @@
 
 def forward_planes(block, tables, plane_step, size, splits=1):
     planes, rows, cols = block.shape[1], block.shape[2], block.shape[3]
+    tables = [part for t in tables for part in table_parts(t)]
     table_specs = [pl.BlockSpec(t.shape, lambda i: (0, 0)) for t in tables]
     step = size // splits
     outs = pl.pallas_call(
@@ -115,9 +123,7 @@
 def cross_kernel(*refs, blocks, sets, box, window, part):
     rec_refs = refs[:blocks]
     lig_ref = refs[blocks]
-    g_hi, g_lo = hi_lo(refs[blocks + 1][...])
-    gl_hi, gl_lo = hi_lo(refs[blocks + 2][...])
-    h_hi, h_lo = hi_lo(refs[blocks + 3][...])
+    g_hi, g_lo, gl_hi, gl_lo, h_hi, h_lo = [r[...] for r in refs[blocks + 1 : blocks + 7]]
     out_ref = refs[-1]
     rows = out_ref.shape[3]
     lanes = out_ref.shape[4]
@@ -164,6 +170,7 @@
     lanes = rec_blocks[0].shape[3]
     blocks = len(rec_blocks)
     tables = [np.concatenate(g_tables, axis=1), gl, hx]
+    tables = [part for t in tables for part in table_parts(t)]
     kernel = functools.partial(
         cross_kernel, blocks=blocks, sets=sets, box=box, window=window, part=part
     )
@@ -189,10 +196,10 @@
             pl.BlockSpec((1, 2, plane_step, x.shape[3], size), lambda s, i: (s, 0, i, 0, 0))
             for x in spectra
         ]
-        + [ly_spec, rz_spec],
+        + [ly_spec, ly_spec, rz_spec, rz_spec],
         out_specs=pl.BlockSpec((1, plane_step, size, size), lambda s, i: (s, i, 0, 0)),
         out_shape=jax.ShapeDtypeStruct((sets, planes, size, size), F32),
-    )(*spectra, *tables)
+    )(*spectra, *[part for t in tables for part in table_parts(t)])
 
 
 def gather_by_sum(piece, axis_name, dim):

time: 86 us -> 85.9 us (level)
  no operation moved by 1% of the time
where the time goes in v16:
time: 85.9 us; the launch traced here: 84.4 us
  Pallas kernels  52.8 us (61%)
  starting transfers between devices  10.7 us (12%)
  waiting for transfers between devices  7.43 us (9%)
  local copies, waits for them, and re-layouts  6.01 us (7%)
  other arithmetic  4.13 us (5%)
  matrix products  2.39 us (3%)
  between operations  0.91 us (1%)
    pallas_call x2, Pallas kernels, cross_spectra(): pl.pallas_call(kernel, grid=(size // row_step,), in_specs=[pl.BlockSpec((...  23.9 us
    pallas_call x2, Pallas kernels, forward_planes(): pl.pallas_call(forward_plane_kernel, grid=(planes // plane_step,), in_spe...  18.9 us
    pallas_call x1, Pallas kernels, inverse_planes(): pl.pallas_call(inverse_plane_kernel, grid=(sets, planes // plane_step), i...  9.99 us
    ppermute x3, waiting for transfers between devices, gather_pieces(): other = lax.ppermute(held, axis_name, perm=pairs)  6.59 us
    ppermute x3, starting transfers between devices, gather_pieces(): other = lax.ppermute(held, axis_name, perm=pairs)  5.85 us
    ppermute x3, starting transfers between devices, gather_direct(): held.append(lax.ppermute(piece, axis_name, perm=pairs))  3.26 us
    dot_general x1, matrix products, pose_statistics(): jnp.einsum('pja,pka->pjk', moved_centred, center_centred, precision=PRECISE)  1.87 us
  transfers between devices with their start and end apart: 8, of which 4 were waited for; matrix products, arithmetic and copies ran while one was open for 13% of the time, Pallas kernels for 37%

profile of v16, /device:TPU:0, one launch (start us, length us, event | category | flops | bytes accessed | tf_op | source)
XLA Modules:
  0.0 84.4 jit_solution(7994760973073905781)
XLA Ops:
  0.6 1.3 %reshape.146 = f32[2,1,2,8,1024]{4,3,2,0,1:T(8,128)S(1)} reshape(f32[2,1,2,8,32,32]{5,4,3,2,1,0:T(8,128)} %param.35) | data formatting | bytes 262144 | tf_op jit(solution)/shard_map/reshape | solution.py:265
  2.0 2.5 %collective-permute-start.3 = (f32[2,1,2,8,1024]{4,3,2,0,1:T(8,128)S(1)}, f32[2,1,2,8,1024]{4,3,2,0,1:T(8,128)S(1)}, u32[]{:S(2)}, u32[]{:S(2)}) collective-permute-start(f32[2,1,2,8,1024]{4,3,2,0,1:T(8,128)S(1)} %reshape.146), channel_id=1, source_target_pairs={{0,24},{8,0},{16,8},{24,16},{1,25},{9,1},{17,9},{25,17},{2,26},{10... | collective-permute-start | bytes 393224 | tf_op jit(solution)/shard_map/ppermute | solution.py:243
  4.4 0.6 collective-permute-start.2
  5.3 9.2 %shard_map.329 = (f32[2,32,64,128]{3,2,1,0:T(8,128)}, f32[2,32,64,128]{3,2,1,0:T(8,128)}) custom-call(f32[2,32,128,128]{3,2,1,0:T(8,128)} %in_ref.1, bf16[256,256]{1,0:T(8,128)(2,1)} %constant.169.clone.rz_hi_ref.refs_2_, bf16[256,256]{1,0:T(8,128)(2,1)} %constant.170.clone.rz_lo_ref.refs_3_, bf16[256,256]{1,0:T(8,128)(2,1)} %constant.171.clone.ly_hi_ref, ...), custom_call_target="tpu_custom_call" | custom-call | tf_op jit(solution)/shard_map/pallas_call | solution.py:113
  14.5 1.6 %collective-permute-start = (f32[2,32,64,128]{3,2,1,0:T(8,128)}, f32[2,32,64,128]{3,2,1,0:T(8,128)}, u32[]{:S(2)}, u32[]{:S(2)}) collective-permute-start(f32[2,32,64,128]{3,2,1,0:T(8,128)} %get-tuple-element.5.refs_0_), channel_id=1, source_target_pairs={{0,24},{8,0},{16,8},{24,16},{1,25},{9,1},{17,9},{25,17},{2,26},{10... | collective-permute-start | bytes 6291464 | tf_op jit(solution)/shard_map/ppermute | solution.py:276
  16.5 0.7 gather_fusion.1
  17.4 0.6 fusion.12
  18.1 0.6 gather_fusion
  18.7 1.3 %slice_multiply_fusion.1 = (f32[2,1,1,32,1024]{4,3,0,2,1:T(8,128)S(1)}, f32[2,1,1,32,1024]{4,3,0,2,1:T(8,128)S(1)}) fusion(f32[2,1,2,32,1024]{4,3,0,2,1:T(8,128)S(1)} %copy_bitcast_fusion, f32[]{:T(128)} %bitcast.8, f32[]{:T(128)} %bitcast.9), kind=kLoop, calls=%fused_computation.11 | loop fusion | flops 131072 | bytes 1048584 | tf_op jit(solution)/shard_map/mul | solution.py:279
  20.7 1.5 %pad_maximum_fusion.in_ref = f32[2,64,32,32]{3,2,1,0:T(8,128)} fusion(f32[1,64,32,32]{3,2,1,0:T(8,128)S(1)} %mul.51, f32[1,64,32,32]{3,2,1,0:T(8,128)S(1)} %mul.48), kind=kLoop, calls=%fused_computation.3 | loop fusion | flops 131072 | bytes 1048576 | tf_op jit(solution)/shard_map/stack | solution.py:278
  22.3 9.6 %shard_map.330.refs_2_ = f32[2,64,128,128]{3,2,1,0:T(8,128)} custom-call(f32[2,64,32,32]{3,2,1,0:T(8,128)} %pad_maximum_fusion.in_ref, bf16[64,256]{1,0:T(8,128)(2,1)} %constant.173.clone.rz_hi_ref, bf16[64,256]{1,0:T(8,128)(2,1)} %constant.174.clone.rz_lo_ref, bf16[256,64]{1,0:T(8,128)(2,1)} %constant.175.clone.ly_hi_ref, ...), custom_call_target="tpu_custom_call" | custom-call | tf_op jit(solution)/shard_map/pallas_call | solution.py:113
  31.9 1.6 %collective-permute-start.5 = (f32[8,3,128]{2,1,0:T(4,128)S(1)}, f32[8,3,128]{2,1,0:T(4,128)S(1)}, u32[]{:S(2)}, u32[]{:S(2)}) collective-permute-start(f32[8,3,128]{2,1,0:T(4,128)S(1)} %copy.85), channel_id=1, source_target_pairs={{0,1},{1,0},{2,3},{3,2},{4,5},{5,4},{6,7},{7,6},{8,9},{9,8},{10,11... | collective-permute-start | bytes 36872 | tf_op jit(solution)/shard_map/ppermute | solution.py:226
  34.0 1.7 %collective-permute-done.5 = f32[8,3,128]{2,1,0:T(4,128)S(1)} collective-permute-done((f32[8,3,128]{2,1,0:T(4,128)S(1)}, f32[8,3,128]{2,1,0:T(4,128)S(1)}, u32[]{:S(2)}, u32[]{:S(2)}) %collective-permute-start.5) | collective-permute-done | bytes 12320 | tf_op jit(solution)/shard_map/ppermute | solution.py:226
  35.8 1.6 %collective-permute-start.6 = (f32[16,3,128]{2,1,0:T(4,128)S(1)}, f32[16,3,128]{2,1,0:T(4,128)S(1)}, u32[]{:S(2)}, u32[]{:S(2)}) collective-permute-start(f32[16,3,128]{2,1,0:T(4,128)S(1)} %maximum_select_fusion.2), channel_id=1, source_target_pairs={{0,2},{1,3},{2,0},{3,1},{4,6},{5,7},{6,4},{7,5},{8,10},{9,11},{10,... | collective-permute-start | bytes 73736 | tf_op jit(solution)/shard_map/ppermute | solution.py:226
  37.4 2.3 %collective-permute-done.6 = f32[16,3,128]{2,1,0:T(4,128)S(1)} collective-permute-done((f32[16,3,128]{2,1,0:T(4,128)S(1)}, f32[16,3,128]{2,1,0:T(4,128)S(1)}, u32[]{:S(2)}, u32[]{:S(2)}) %collective-permute-start.6) | collective-permute-done | bytes 24608 | tf_op jit(solution)/shard_map/ppermute | solution.py:226
  39.8 2.7 %collective-permute-start.7 = (f32[32,3,128]{2,1,0:T(4,128)S(1)}, f32[32,3,128]{2,1,0:T(4,128)S(1)}, u32[]{:S(2)}, u32[]{:S(2)}) collective-permute-start(f32[32,3,128]{2,1,0:T(4,128)S(1)} %maximum_select_fusion.1), channel_id=1, source_target_pairs={{0,4},{1,5},{2,6},{3,7},{4,0},{5,1},{6,2},{7,3},{8,12},{9,13},{10,... | collective-permute-start | bytes 147464 | tf_op jit(solution)/shard_map/ppermute | solution.py:226
  42.4 2.6 %collective-permute-done.7 = f32[32,3,128]{2,1,0:T(4,128)S(1)} collective-permute-done((f32[32,3,128]{2,1,0:T(4,128)S(1)}, f32[32,3,128]{2,1,0:T(4,128)S(1)}, u32[]{:S(2)}, u32[]{:S(2)}) %collective-permute-start.7) | collective-permute-done | bytes 49184 | tf_op jit(solution)/shard_map/ppermute | solution.py:226
  45.0 1.0 %gather_fusion.2 = f32[256,3,128]{2,1,0:T(4,128)S(1)} fusion(f32[64,3,128]{2,1,0:T(4,128)S(1)} %maximum_select_fusion, s32[1024]{0:T(1024)S(1)} %pad_clamp_fusion), kind=kCustom, calls=%fused_computation.2 | custom fusion | bytes 787456 | tf_op jit(solution)/shard_map/jit(_take)/gather | solution.py:334
  47.0 1.9 %fusion = f32[256,3,3]{2,1,0:T(4,128)S(1)} fusion(f32[256,3,128]{2,1,0:T(4,128)S(1)} %copy.89, f32[256,3,128]{2,1,0:T(4,128)S(1)} %gather_fusion.2, f32[256,3]{1,0:T(8,128)S(1)} %broadcast_multiply_fusion), kind=kOutput, calls=%fused_computation.7 | convolution fusion | flops 3637248 | bytes 798720 | tf_op jit(solution)/shard_map/pja,pka->pjk/dot_general | solution.py:340
  49.0 0.6 maximum_bitcast_fusion.1
  49.6 11.9 %shard_map.331.refs_0_ = f32[2,2,32,64,128]{4,3,2,1,0:T(8,128)} custom-call(f32[2,32,64,128]{3,2,1,0:T(8,128)} %get-tuple-element.5.refs_0_, f32[2,32,64,128]{3,2,1,0:T(8,128)} %collective-permute-done.refs_1_, f32[2,64,128,128]{3,2,1,0:T(8,128)} %shard_map.330.refs_2_, bf16[128,128]{1,0:T(8,128)(2,1)} %constant.177.clone.refs_3_, ...), custom_call_target="tpu_custom_call" | custom-call | tf_op jit(solution)/shard_map/pallas_call | solution.py:177
  61.6 0.8 collective-permute-done.4.refs_1_
  62.4 12.0 %shard_map.332.refs_1_ = f32[2,2,32,64,128]{4,3,2,1,0:T(8,128)} custom-call(f32[2,32,64,128]{3,2,1,0:T(8,128)} %get-tuple-element.6.refs_0_, f32[2,32,64,128]{3,2,1,0:T(8,128)} %collective-permute-done.4.refs_1_, f32[2,64,128,128]{3,2,1,0:T(8,128)} %shard_map.330.refs_2_, bf16[128,128]{1,0:T(8,128)(2,1)} %constant.177.clone.refs_3_, ...), custom_call_target="tpu_custom_call" | custom-call | tf_op jit(solution)/shard_map/pallas_call | solution.py:177
  74.4 10.0 %shard_map.333 = f32[2,32,128,128]{3,2,1,0:T(8,128)} custom-call(f32[2,2,32,64,128]{4,3,2,1,0:T(8,128)} %shard_map.331.refs_0_, f32[2,2,32,64,128]{4,3,2,1,0:T(8,128)} %shard_map.332.refs_1_, bf16[256,256]{1,0:T(8,128)(2,1)} %constant.169.clone.rz_hi_ref.refs_2_, bf16[256,256]{1,0:T(8,128)(2,1)} %constant.170.clone.rz_lo_ref.refs_3_, ...), custom_call_target="tpu_custom_call" | custom-call | tf_op jit(solution)/shard_map/pallas_call | solution.py:192
  (55 shorter events, 3.2 us)
Async XLA Ops:
  0.6 32.9 %copy-start = (f32[3,128]{1,0:T(4,128)S(1)}, f32[3,128]{1,0:T(4,128)}, u32[]{:S(2)}) copy-start(f32[3,128]{1,0:T(4,128)} %param.38) | copy-start | bytes 4612
  1.9 14.2 %copy-start.5 = (s32[256]{0:T(256)S(1)}, s32[256]{0:T(256)}, u32[]{:S(2)}) copy-start(s32[256]{0:T(256)} %param.40) | copy-start | bytes 3076
  1.9 14.2 %copy-start.8 = (s32[256]{0:T(256)S(1)}, s32[256]{0:T(256)}, u32[]{:S(2)}) copy-start(s32[256]{0:T(256)} %param.41) | copy-start | bytes 3076
  2.0 14.2 %copy-start.1 = (f32[2,1,2,8,32,32]{5,4,3,2,1,0:T(8,128)S(1)}, f32[2,1,2,8,32,32]{5,4,3,2,1,0:T(8,128)}, u32[]{:S(2)}) copy-start(f32[2,1,2,8,32,32]{5,4,3,2,1,0:T(8,128)} %param.35) | copy-start | bytes 393220
  2.0 14.5 %copy-start.3 = (f32[9,16]{1,0:T(8,128)S(1)}, f32[9,16]{1,0:T(8,128)}, u32[]{:S(2)}) copy-start(f32[9,16]{1,0:T(8,128)} %param.37) | copy-start | bytes 1732
  2.0 15.4 %copy-start.4 = (f32[2]{0:T(128)S(1)}, f32[2]{0:T(128)}, u32[]{:S(2)}) copy-start(f32[2]{0:T(128)} %param.36) | copy-start | bytes 28
  2.0 16.0 %collective-permute-start.3 = (f32[2,1,2,8,1024]{4,3,2,0,1:T(8,128)S(1)}, f32[2,1,2,8,1024]{4,3,2,0,1:T(8,128)S(1)}, u32[]{:S(2)}, u32[]{:S(2)}) collective-permute-start(f32[2,1,2,8,1024]{4,3,2,0,1:T(8,128)S(1)} %reshape.146), channel_id=1, source_target_pairs={{0,24},{8,0},{16,8},{24,16},{1,25},{9,1},{17,9},{25,17},{2,26},{10... | collective-permute-start | bytes 393224 | tf_op jit(solution)/shard_map/ppermute | solution.py:243
  4.4 13.6 %collective-permute-start.2 = (f32[2,1,2,8,1024]{4,3,2,0,1:T(8,128)S(1)}, f32[2,1,2,8,1024]{4,3,2,0,1:T(8,128)S(1)}, u32[]{:S(2)}, u32[]{:S(2)}) collective-permute-start(f32[2,1,2,8,1024]{4,3,2,0,1:T(8,128)S(1)} %reshape.146), channel_id=1, source_target_pairs={{0,16},{8,24},{16,0},{24,8},{1,17},{9,25},{17,1},{25,9},{2,18},{10... | collective-permute-start | bytes 393224 | tf_op jit(solution)/shard_map/ppermute | solution.py:243
  5.1 12.9 %collective-permute-start.1 = (f32[2,1,2,8,1024]{4,3,2,0,1:T(8,128)S(1)}, f32[2,1,2,8,1024]{4,3,2,0,1:T(8,128)S(1)}, u32[]{:S(2)}, u32[]{:S(2)}) collective-permute-start(f32[2,1,2,8,1024]{4,3,2,0,1:T(8,128)S(1)} %reshape.146), channel_id=1, source_target_pairs={{0,8},{8,16},{16,24},{24,0},{1,9},{9,17},{17,25},{25,1},{2,10},{10... | collective-permute-start | bytes 393224 | tf_op jit(solution)/shard_map/ppermute | solution.py:243
  14.5 35.2 %collective-permute-start = (f32[2,32,64,128]{3,2,1,0:T(8,128)}, f32[2,32,64,128]{3,2,1,0:T(8,128)}, u32[]{:S(2)}, u32[]{:S(2)}) collective-permute-start(f32[2,32,64,128]{3,2,1,0:T(8,128)} %get-tuple-element.5.refs_0_), channel_id=1, source_target_pairs={{0,24},{8,0},{16,8},{24,16},{1,25},{9,1},{17,9},{25,17},{2,26},{10... | collective-permute-start | bytes 6291464 | tf_op jit(solution)/shard_map/ppermute | solution.py:276
  16.1 46.3 %collective-permute-start.4 = (f32[2,32,64,128]{3,2,1,0:T(8,128)}, f32[2,32,64,128]{3,2,1,0:T(8,128)}, u32[]{:S(2)}, u32[]{:S(2)}) collective-permute-start(f32[2,32,64,128]{3,2,1,0:T(8,128)} %get-tuple-element.6.refs_0_), channel_id=1, source_target_pairs={{0,24},{8,0},{16,8},{24,16},{1,25},{9,1},{17,9},{25,17},{2,26},{10... | collective-permute-start | bytes 6291464 | tf_op jit(solution)/shard_map/ppermute | solution.py:276
  22.3 9.7 %copy-start.2 = (f32[8,3,128]{2,0,1:T(8,128)S(1)}, f32[8,3,128]{2,0,1:T(8,128)}, u32[]{:S(2)}) copy-start(f32[8,3,128]{2,0,1:T(8,128)} %param.39) | copy-start | bytes 36868
  22.3 15.1 %copy-start.7 = (s32[256,1]{0,1:T(1,128)S(1)}, s32[256,1]{0,1:T(1,128)}, u32[]{:S(2)}) copy-start(s32[256,1]{0,1:T(1,128)} %param.42) | copy-start | bytes 3076
  22.3 15.1 %copy-start.6 = (s32[256]{0:T(256)S(1)}, s32[256]{0:T(256)}, u32[]{:S(2)}) copy-start(s32[256]{0:T(256)} %param.43) | copy-start | bytes 3076
  31.9 3.8 %collective-permute-start.5 = (f32[8,3,128]{2,1,0:T(4,128)S(1)}, f32[8,3,128]{2,1,0:T(4,128)S(1)}, u32[]{:S(2)}, u32[]{:S(2)}) collective-permute-start(f32[8,3,128]{2,1,0:T(4,128)S(1)} %copy.85), channel_id=1, source_target_pairs={{0,1},{1,0},{2,3},{3,2},{4,5},{5,4},{6,7},{7,6},{8,9},{9,8},{10,11... | collective-permute-start | bytes 36872 | tf_op jit(solution)/shard_map/ppermute | solution.py:226
  35.8 4.0 %collective-permute-start.6 = (f32[16,3,128]{2,1,0:T(4,128)S(1)}, f32[16,3,128]{2,1,0:T(4,128)S(1)}, u32[]{:S(2)}, u32[]{:S(2)}) collective-permute-start(f32[16,3,128]{2,1,0:T(4,128)S(1)} %maximum_select_fusion.2), channel_id=1, source_target_pairs={{0,2},{1,3},{2,0},{3,1},{4,6},{5,7},{6,4},{7,5},{8,10},{9,11},{10,... | collective-permute-start | bytes 73736 | tf_op jit(solution)/shard_map/ppermute | solution.py:226
  39.8 5.2 %collective-permute-start.7 = (f32[32,3,128]{2,1,0:T(4,128)S(1)}, f32[32,3,128]{2,1,0:T(4,128)S(1)}, u32[]{:S(2)}, u32[]{:S(2)}) collective-permute-start(f32[32,3,128]{2,1,0:T(4,128)S(1)} %maximum_select_fusion.1), channel_id=1, source_target_pairs={{0,4},{1,5},{2,6},{3,7},{4,0},{5,1},{6,2},{7,3},{8,12},{9,13},{10,... | collective-permute-start | bytes 147464 | tf_op jit(solution)/shard_map/ppermute | solution.py:226

commit v17 on v16

--- a/solution.py
+++ b/solution.py
@@ -259,7 +259,7 @@
     extra = -(-(box - 1) // part)
     window = part * (1 + extra)
     plane_step = 8
-    row_step = 16
+    row_step = 32
 
     lead = ligand_box.shape[:4]
     dense = ligand_box.reshape(lead + (box * box,))

time: 85.9 us -> 87.2 us (1.015)
  Pallas kernels: 52.8 us -> 55.6 us
    pallas_call x2, Pallas kernels: 23.9 us -> 26.9 us  [cross_spectra(): pl.pallas_call(kernel, grid=(size // row_step,), in_specs=[pl.BlockSpec((...]
  transfers between devices with their start and end apart: 8 -> 8, of which waited for: 4 -> 3; matrix products, arithmetic and copies ran while one was open for 13% -> 13% of each run, Pallas kernels for 37% -> 37%
where the time goes in v17:
time: 87.2 us; the launch traced here: 86.4 us
  Pallas kernels  55.6 us (64%)
  starting transfers between devices  10.7 us (12%)
  waiting for transfers between devices  6.62 us (8%)
  local copies, waits for them, and re-layouts  6.01 us (7%)
  other arithmetic  4.13 us (5%)
  matrix products  2.39 us (3%)
  between operations  0.91 us (1%)
    pallas_call x2, Pallas kernels, cross_spectra(): pl.pallas_call(kernel, grid=(size // row_step,), in_specs=[pl.BlockSpec((...  26.9 us
    pallas_call x2, Pallas kernels, forward_planes(): pl.pallas_call(forward_plane_kernel, grid=(planes // plane_step,), in_spe...  18.7 us
    pallas_call x1, Pallas kernels, inverse_planes(): pl.pallas_call(inverse_plane_kernel, grid=(sets, planes // plane_step), i...  9.99 us
    ppermute x3, waiting for transfers between devices, gather_pieces(): other = lax.ppermute(held, axis_name, perm=pairs)  6.6 us
    ppermute x3, starting transfers between devices, gather_pieces(): other = lax.ppermute(held, axis_name, perm=pairs)  5.85 us
    ppermute x3, starting transfers between devices, gather_direct(): held.append(lax.ppermute(piece, axis_name, perm=pairs))  3.26 us
    dot_general x1, matrix products, pose_statistics(): jnp.einsum('pja,pka->pjk', moved_centred, center_centred, precision=PRECISE)  1.87 us
  transfers between devices with their start and end apart: 8, of which 3 were waited for; matrix products, arithmetic and copies ran while one was open for 13% of the time, Pallas kernels for 37%

profile of v17, /device:TPU:0, one launch (start us, length us, event | category | flops | bytes accessed | tf_op | source)
XLA Modules:
  0.0 86.4 jit_solution(6536049934008205796)
XLA Ops:
  0.6 1.3 %reshape.146 = f32[2,1,2,8,1024]{4,3,2,0,1:T(8,128)S(1)} reshape(f32[2,1,2,8,32,32]{5,4,3,2,1,0:T(8,128)} %param.35) | data formatting | bytes 262144 | tf_op jit(solution)/shard_map/reshape | solution.py:265
  2.0 2.5 %collective-permute-start.3 = (f32[2,1,2,8,1024]{4,3,2,0,1:T(8,128)S(1)}, f32[2,1,2,8,1024]{4,3,2,0,1:T(8,128)S(1)}, u32[]{:S(2)}, u32[]{:S(2)}) collective-permute-start(f32[2,1,2,8,1024]{4,3,2,0,1:T(8,128)S(1)} %reshape.146), channel_id=1, source_target_pairs={{0,24},{8,0},{16,8},{24,16},{1,25},{9,1},{17,9},{25,17},{2,26},{10... | collective-permute-start | bytes 393224 | tf_op jit(solution)/shard_map/ppermute | solution.py:243
  4.4 0.6 collective-permute-start.2
  5.3 9.2 %shard_map.329 = (f32[2,32,64,128]{3,2,1,0:T(8,128)}, f32[2,32,64,128]{3,2,1,0:T(8,128)}) custom-call(f32[2,32,128,128]{3,2,1,0:T(8,128)} %in_ref.1, bf16[256,256]{1,0:T(8,128)(2,1)} %constant.169.clone.rz_hi_ref.refs_2_, bf16[256,256]{1,0:T(8,128)(2,1)} %constant.170.clone.rz_lo_ref.refs_3_, bf16[256,256]{1,0:T(8,128)(2,1)} %constant.171.clone.ly_hi_ref, ...), custom_call_target="tpu_custom_call" | custom-call | tf_op jit(solution)/shard_map/pallas_call | solution.py:113
  14.5 1.6 %collective-permute-start = (f32[2,32,64,128]{3,2,1,0:T(8,128)}, f32[2,32,64,128]{3,2,1,0:T(8,128)}, u32[]{:S(2)}, u32[]{:S(2)}) collective-permute-start(f32[2,32,64,128]{3,2,1,0:T(8,128)} %get-tuple-element.5.refs_0_), channel_id=1, source_target_pairs={{0,24},{8,0},{16,8},{24,16},{1,25},{9,1},{17,9},{25,17},{2,26},{10... | collective-permute-start | bytes 6291464 | tf_op jit(solution)/shard_map/ppermute | solution.py:276
  16.5 0.7 gather_fusion.1
  17.4 0.6 fusion.12
  18.1 0.6 gather_fusion
  18.7 1.3 %slice_multiply_fusion.1 = (f32[2,1,1,32,1024]{4,3,0,2,1:T(8,128)S(1)}, f32[2,1,1,32,1024]{4,3,0,2,1:T(8,128)S(1)}) fusion(f32[2,1,2,32,1024]{4,3,0,2,1:T(8,128)S(1)} %copy_bitcast_fusion, f32[]{:T(128)} %bitcast.8, f32[]{:T(128)} %bitcast.9), kind=kLoop, calls=%fused_computation.11 | loop fusion | flops 131072 | bytes 1048584 | tf_op jit(solution)/shard_map/mul | solution.py:279
  20.7 1.5 %pad_maximum_fusion.in_ref = f32[2,64,32,32]{3,2,1,0:T(8,128)} fusion(f32[1,64,32,32]{3,2,1,0:T(8,128)S(1)} %mul.51, f32[1,64,32,32]{3,2,1,0:T(8,128)S(1)} %mul.48), kind=kLoop, calls=%fused_computation.3 | loop fusion | flops 131072 | bytes 1048576 | tf_op jit(solution)/shard_map/stack | solution.py:278
  22.3 9.5 %shard_map.330.refs_2_ = f32[2,64,128,128]{3,2,1,0:T(8,128)} custom-call(f32[2,64,32,32]{3,2,1,0:T(8,128)} %pad_maximum_fusion.in_ref, bf16[64,256]{1,0:T(8,128)(2,1)} %constant.173.clone.rz_hi_ref, bf16[64,256]{1,0:T(8,128)(2,1)} %constant.174.clone.rz_lo_ref, bf16[256,64]{1,0:T(8,128)(2,1)} %constant.175.clone.ly_hi_ref, ...), custom_call_target="tpu_custom_call" | custom-call | tf_op jit(solution)/shard_map/pallas_call | solution.py:113
  31.8 1.6 %collective-permute-start.5 = (f32[8,3,128]{2,1,0:T(4,128)S(1)}, f32[8,3,128]{2,1,0:T(4,128)S(1)}, u32[]{:S(2)}, u32[]{:S(2)}) collective-permute-start(f32[8,3,128]{2,1,0:T(4,128)S(1)} %copy.85), channel_id=1, source_target_pairs={{0,1},{1,0},{2,3},{3,2},{4,5},{5,4},{6,7},{7,6},{8,9},{9,8},{10,11... | collective-permute-start | bytes 36872 | tf_op jit(solution)/shard_map/ppermute | solution.py:226
  33.3 0.5 convolution_add_fusion
  33.9 1.7 %collective-permute-done.5 = f32[8,3,128]{2,1,0:T(4,128)S(1)} collective-permute-done((f32[8,3,128]{2,1,0:T(4,128)S(1)}, f32[8,3,128]{2,1,0:T(4,128)S(1)}, u32[]{:S(2)}, u32[]{:S(2)}) %collective-permute-start.5) | collective-permute-done | bytes 12320 | tf_op jit(solution)/shard_map/ppermute | solution.py:226
  35.6 1.6 %collective-permute-start.6 = (f32[16,3,128]{2,1,0:T(4,128)S(1)}, f32[16,3,128]{2,1,0:T(4,128)S(1)}, u32[]{:S(2)}, u32[]{:S(2)}) collective-permute-start(f32[16,3,128]{2,1,0:T(4,128)S(1)} %maximum_select_fusion.2), channel_id=1, source_target_pairs={{0,2},{1,3},{2,0},{3,1},{4,6},{5,7},{6,4},{7,5},{8,10},{9,11},{10,... | collective-permute-start | bytes 73736 | tf_op jit(solution)/shard_map/ppermute | solution.py:226
  37.3 2.3 %collective-permute-done.6 = f32[16,3,128]{2,1,0:T(4,128)S(1)} collective-permute-done((f32[16,3,128]{2,1,0:T(4,128)S(1)}, f32[16,3,128]{2,1,0:T(4,128)S(1)}, u32[]{:S(2)}, u32[]{:S(2)}) %collective-permute-start.6) | collective-permute-done | bytes 24608 | tf_op jit(solution)/shard_map/ppermute | solution.py:226
  39.6 2.7 %collective-permute-start.7 = (f32[32,3,128]{2,1,0:T(4,128)S(1)}, f32[32,3,128]{2,1,0:T(4,128)S(1)}, u32[]{:S(2)}, u32[]{:S(2)}) collective-permute-start(f32[32,3,128]{2,1,0:T(4,128)S(1)} %maximum_select_fusion.1), channel_id=1, source_target_pairs={{0,4},{1,5},{2,6},{3,7},{4,0},{5,1},{6,2},{7,3},{8,12},{9,13},{10,... | collective-permute-start | bytes 147464 | tf_op jit(solution)/shard_map/ppermute | solution.py:226
  42.3 2.6 %collective-permute-done.7 = f32[32,3,128]{2,1,0:T(4,128)S(1)} collective-permute-done((f32[32,3,128]{2,1,0:T(4,128)S(1)}, f32[32,3,128]{2,1,0:T(4,128)S(1)}, u32[]{:S(2)}, u32[]{:S(2)}) %collective-permute-start.7) | collective-permute-done | bytes 49184 | tf_op jit(solution)/shard_map/ppermute | solution.py:226
  44.9 1.0 %gather_fusion.2 = f32[256,3,128]{2,1,0:T(4,128)S(1)} fusion(f32[64,3,128]{2,1,0:T(4,128)S(1)} %maximum_select_fusion, s32[1024]{0:T(1024)S(1)} %pad_clamp_fusion), kind=kCustom, calls=%fused_computation.2 | custom fusion | bytes 787456 | tf_op jit(solution)/shard_map/jit(_take)/gather | solution.py:334
  46.8 1.9 %fusion = f32[256,3,3]{2,1,0:T(4,128)S(1)} fusion(f32[256,3,128]{2,1,0:T(4,128)S(1)} %copy.89, f32[256,3,128]{2,1,0:T(4,128)S(1)} %gather_fusion.2, f32[256,3]{1,0:T(8,128)S(1)} %broadcast_multiply_fusion), kind=kOutput, calls=%fused_computation.7 | convolution fusion | flops 3637248 | bytes 798720 | tf_op jit(solution)/shard_map/pja,pka->pjk/dot_general | solution.py:340
  48.9 0.6 maximum_bitcast_fusion.1
  49.5 13.4 %shard_map.331.refs_0_ = f32[2,2,32,64,128]{4,3,2,1,0:T(8,128)} custom-call(f32[2,32,64,128]{3,2,1,0:T(8,128)} %get-tuple-element.5.refs_0_, f32[2,32,64,128]{3,2,1,0:T(8,128)} %collective-permute-done.refs_1_, f32[2,64,128,128]{3,2,1,0:T(8,128)} %shard_map.330.refs_2_, bf16[128,128]{1,0:T(8,128)(2,1)} %constant.177.clone.refs_3_, ...), custom_call_target="tpu_custom_call" | custom-call | tf_op jit(solution)/shard_map/pallas_call | solution.py:177
  62.9 13.5 %shard_map.332.refs_1_ = f32[2,2,32,64,128]{4,3,2,1,0:T(8,128)} custom-call(f32[2,32,64,128]{3,2,1,0:T(8,128)} %get-tuple-element.6.refs_0_, f32[2,32,64,128]{3,2,1,0:T(8,128)} %collective-permute-done.4.refs_1_, f32[2,64,128,128]{3,2,1,0:T(8,128)} %shard_map.330.refs_2_, bf16[128,128]{1,0:T(8,128)(2,1)} %constant.177.clone.refs_3_, ...), custom_call_target="tpu_custom_call" | custom-call | tf_op jit(solution)/shard_map/pallas_call | solution.py:177
  76.4 10.0 %shard_map.333 = f32[2,32,128,128]{3,2,1,0:T(8,128)} custom-call(f32[2,2,32,64,128]{4,3,2,1,0:T(8,128)} %shard_map.331.refs_0_, f32[2,2,32,64,128]{4,3,2,1,0:T(8,128)} %shard_map.332.refs_1_, bf16[256,256]{1,0:T(8,128)(2,1)} %constant.169.clone.rz_hi_ref.refs_2_, bf16[256,256]{1,0:T(8,128)(2,1)} %constant.170.clone.rz_lo_ref.refs_3_, ...), custom_call_target="tpu_custom_call" | custom-call | tf_op jit(solution)/shard_map/pallas_call | solution.py:192
  (55 shorter events, 2.7 us)
Async XLA Ops:
  0.6 32.7 %copy-start = (f32[3,128]{1,0:T(4,128)S(1)}, f32[3,128]{1,0:T(4,128)}, u32[]{:S(2)}) copy-start(f32[3,128]{1,0:T(4,128)} %param.38) | copy-start | bytes 4612
  1.9 14.2 %copy-start.5 = (s32[256]{0:T(256)S(1)}, s32[256]{0:T(256)}, u32[]{:S(2)}) copy-start(s32[256]{0:T(256)} %param.40) | copy-start | bytes 3076
  1.9 14.2 %copy-start.8 = (s32[256]{0:T(256)S(1)}, s32[256]{0:T(256)}, u32[]{:S(2)}) copy-start(s32[256]{0:T(256)} %param.41) | copy-start | bytes 3076
  2.0 14.2 %copy-start.1 = (f32[2,1,2,8,32,32]{5,4,3,2,1,0:T(8,128)S(1)}, f32[2,1,2,8,32,32]{5,4,3,2,1,0:T(8,128)}, u32[]{:S(2)}) copy-start(f32[2,1,2,8,32,32]{5,4,3,2,1,0:T(8,128)} %param.35) | copy-start | bytes 393220
  2.0 14.5 %copy-start.3 = (f32[9,16]{1,0:T(8,128)S(1)}, f32[9,16]{1,0:T(8,128)}, u32[]{:S(2)}) copy-start(f32[9,16]{1,0:T(8,128)} %param.37) | copy-start | bytes 1732
  2.0 15.4 %copy-start.4 = (f32[2]{0:T(128)S(1)}, f32[2]{0:T(128)}, u32[]{:S(2)}) copy-start(f32[2]{0:T(128)} %param.36) | copy-start | bytes 28
  2.0 16.0 %collective-permute-start.3 = (f32[2,1,2,8,1024]{4,3,2,0,1:T(8,128)S(1)}, f32[2,1,2,8,1024]{4,3,2,0,1:T(8,128)S(1)}, u32[]{:S(2)}, u32[]{:S(2)}) collective-permute-start(f32[2,1,2,8,1024]{4,3,2,0,1:T(8,128)S(1)} %reshape.146), channel_id=1, source_target_pairs={{0,24},{8,0},{16,8},{24,16},{1,25},{9,1},{17,9},{25,17},{2,26},{10... | collective-permute-start | bytes 393224 | tf_op jit(solution)/shard_map/ppermute | solution.py:243
  4.4 13.6 %collective-permute-start.2 = (f32[2,1,2,8,1024]{4,3,2,0,1:T(8,128)S(1)}, f32[2,1,2,8,1024]{4,3,2,0,1:T(8,128)S(1)}, u32[]{:S(2)}, u32[]{:S(2)}) collective-permute-start(f32[2,1,2,8,1024]{4,3,2,0,1:T(8,128)S(1)} %reshape.146), channel_id=1, source_target_pairs={{0,16},{8,24},{16,0},{24,8},{1,17},{9,25},{17,1},{25,9},{2,18},{10... | collective-permute-start | bytes 393224 | tf_op jit(solution)/shard_map/ppermute | solution.py:243
  5.1 12.9 %collective-permute-start.1 = (f32[2,1,2,8,1024]{4,3,2,0,1:T(8,128)S(1)}, f32[2,1,2,8,1024]{4,3,2,0,1:T(8,128)S(1)}, u32[]{:S(2)}, u32[]{:S(2)}) collective-permute-start(f32[2,1,2,8,1024]{4,3,2,0,1:T(8,128)S(1)} %reshape.146), channel_id=1, source_target_pairs={{0,8},{8,16},{16,24},{24,0},{1,9},{9,17},{17,25},{25,1},{2,10},{10... | collective-permute-start | bytes 393224 | tf_op jit(solution)/shard_map/ppermute | solution.py:243
  14.5 35.0 %collective-permute-start = (f32[2,32,64,128]{3,2,1,0:T(8,128)}, f32[2,32,64,128]{3,2,1,0:T(8,128)}, u32[]{:S(2)}, u32[]{:S(2)}) collective-permute-start(f32[2,32,64,128]{3,2,1,0:T(8,128)} %get-tuple-element.5.refs_0_), channel_id=1, source_target_pairs={{0,24},{8,0},{16,8},{24,16},{1,25},{9,1},{17,9},{25,17},{2,26},{10... | collective-permute-start | bytes 6291464 | tf_op jit(solution)/shard_map/ppermute | solution.py:276
  16.1 46.8 %collective-permute-start.4 = (f32[2,32,64,128]{3,2,1,0:T(8,128)}, f32[2,32,64,128]{3,2,1,0:T(8,128)}, u32[]{:S(2)}, u32[]{:S(2)}) collective-permute-start(f32[2,32,64,128]{3,2,1,0:T(8,128)} %get-tuple-element.6.refs_0_), channel_id=1, source_target_pairs={{0,24},{8,0},{16,8},{24,16},{1,25},{9,1},{17,9},{25,17},{2,26},{10... | collective-permute-start | bytes 6291464 | tf_op jit(solution)/shard_map/ppermute | solution.py:276
  22.3 9.5 %copy-start.2 = (f32[8,3,128]{2,0,1:T(8,128)S(1)}, f32[8,3,128]{2,0,1:T(8,128)}, u32[]{:S(2)}) copy-start(f32[8,3,128]{2,0,1:T(8,128)} %param.39) | copy-start | bytes 36868
  22.3 15.0 %copy-start.7 = (s32[256,1]{0,1:T(1,128)S(1)}, s32[256,1]{0,1:T(1,128)}, u32[]{:S(2)}) copy-start(s32[256,1]{0,1:T(1,128)} %param.42) | copy-start | bytes 3076
  22.3 15.0 %copy-start.6 = (s32[256]{0:T(256)S(1)}, s32[256]{0:T(256)}, u32[]{:S(2)}) copy-start(s32[256]{0:T(256)} %param.43) | copy-start | bytes 3076
  31.8 3.8 %collective-permute-start.5 = (f32[8,3,128]{2,1,0:T(4,128)S(1)}, f32[8,3,128]{2,1,0:T(4,128)S(1)}, u32[]{:S(2)}, u32[]{:S(2)}) collective-permute-start(f32[8,3,128]{2,1,0:T(4,128)S(1)} %copy.85), channel_id=1, source_target_pairs={{0,1},{1,0},{2,3},{3,2},{4,5},{5,4},{6,7},{7,6},{8,9},{9,8},{10,11... | collective-permute-start | bytes 36872 | tf_op jit(solution)/shard_map/ppermute | solution.py:226
  35.6 4.0 %collective-permute-start.6 = (f32[16,3,128]{2,1,0:T(4,128)S(1)}, f32[16,3,128]{2,1,0:T(4,128)S(1)}, u32[]{:S(2)}, u32[]{:S(2)}) collective-permute-start(f32[16,3,128]{2,1,0:T(4,128)S(1)} %maximum_select_fusion.2), channel_id=1, source_target_pairs={{0,2},{1,3},{2,0},{3,1},{4,6},{5,7},{6,4},{7,5},{8,10},{9,11},{10,... | collective-permute-start | bytes 73736 | tf_op jit(solution)/shard_map/ppermute | solution.py:226
  39.6 5.2 %collective-permute-start.7 = (f32[32,3,128]{2,1,0:T(4,128)S(1)}, f32[32,3,128]{2,1,0:T(4,128)S(1)}, u32[]{:S(2)}, u32[]{:S(2)}) collective-permute-start(f32[32,3,128]{2,1,0:T(4,128)S(1)} %maximum_select_fusion.1), channel_id=1, source_target_pairs={{0,4},{1,5},{2,6},{3,7},{4,0},{5,1},{6,2},{7,3},{8,12},{9,13},{10,... | collective-permute-start | bytes 147464 | tf_op jit(solution)/shard_map/ppermute | solution.py:226
